TPU v7x, 512 devices: a whole 4x8x8 slice. The times are simulated.
512 devices in a mesh: row: 64 (over z, y), col: 8 (over x, core).
Axes of the slice: x: 4, y: 8, z: 8, core: 2. Of those that a mesh axis runs over, the one named last changes fastest.
Arguments:
- tiles: float32 [64, 8, 64, 128, 128], P('row', 'col'), may hold values from -0.0625 to 0.0625
- tile_rows: int32 [64, 8, 64], P('row', 'col'), may hold values from 0 to 15, as said below
- tile_cols: int32 [64, 8, 64], P('row', 'col'), may hold values from 0 to 63, as said below
- exponents: int32 [65536], P('col'), may hold values from 0 to 3
- u_basis: float32 [64, 131072], P(None, 'row'), may hold values from -6 to 6
- v_basis: float32 [64, 65536], P(None, ('col', 'row')), may hold values from -6 to 6
- prior: float32 [64, 64], replicated, may hold values from -0.75 to 0.75
Outputs:
- u_next: float32 [64, 131072], P(None, ('row', 'col'))
- v_next: float32 [64, 65536], P(None, ('col', 'row'))
- v_factor: float32 [64, 64], replicated
- u_factor: float32 [64, 64], replicated
Inputs may be any that keep to these rules, and one draw needn't show every extreme that they name: `tile_rows`: within each grid cell every tile row of 0 to 15 appears exactly 64 / 16 times. `tile_cols`: within each grid cell every tile column of 0 to 63 appears exactly 64 / 64 times.
All inputs are finite; a program needn't handle non-finite values.
Results may differ from a plain program's by a relative error of at most 0.00018.
Values sent between devices are 32-bit elements; how exact they have to be, the bound alone decides.
No kernel may reach another device: no remote copies, remote signals or barrier semaphores. Data moves between devices by JAX's collectives and lax.ppermute only.
A program may use at most 64 MiB of HBM per device.

v0:
```python
import math

import jax
import jax.numpy as jnp
from jax import lax
from jax.sharding import PartitionSpec as P

HIGH = lax.Precision.HIGHEST


def lower_solve(factor, rhs):
    return lax.linalg.triangular_solve(factor, rhs, left_side=True, lower=True)


def per_device(tiles, tile_rows, tile_cols, exponents, u_basis, v_basis, prior):
    local_tiles = tiles[0, 0]
    rows_here = tile_rows[0, 0]
    cols_here = tile_cols[0, 0]
    count, tl, _ = local_tiles.shape
    width, block_rows = u_basis.shape
    block_cols = exponents.shape[0]
    rows_tiles = block_rows // tl
    cols_tiles = block_cols // tl
    total_rows = block_rows * lax.axis_size("row")
    total_cols = block_cols * lax.axis_size("col")
    v_piece = v_basis.shape[1]
    u_piece = block_rows // lax.axis_size("col")
    col_scale = jnp.exp2(-exponents.astype(jnp.float32))
    lowtri = jnp.tril(prior)
    col_hits = (cols_here[:, None] == jnp.arange(cols_tiles, dtype=jnp.int32)[None, :]).astype(
        jnp.float32
    )
    row_hits = (rows_here[:, None] == jnp.arange(rows_tiles, dtype=jnp.int32)[None, :]).astype(
        jnp.float32
    )
    picked = jnp.take(u_basis.reshape(width, rows_tiles, tl), rows_here, axis=1)
    prod = jnp.einsum("sta,tab->stb", picked, local_tiles, precision=HIGH)
    partial_value = (
        jnp.einsum("stb,tc->scb", prod, col_hits, precision=HIGH).reshape(width, block_cols)
        * col_scale
    )
    offset = lax.axis_index("row") * v_piece
    own_term = jnp.dot(lowtri, v_basis, precision=HIGH)
    slot = lax.dynamic_slice_in_dim(partial_value, offset, v_piece, 1) - own_term
    partial_value = lax.dynamic_update_slice_in_dim(partial_value, slot, offset, 1)
    pt_piece = lax.psum_scatter(partial_value, "row", scatter_dimension=1, tiled=True)
    gram = lax.psum(jnp.dot(pt_piece, pt_piece.T, precision=HIGH), ("row", "col"))
    v_factor = jnp.linalg.cholesky(gram / total_cols)
    v_next = lower_solve(v_factor, pt_piece)
    source = lax.all_gather(v_next, "row", axis=1, tiled=True)
    factor = math.sqrt(total_rows / total_cols)
    scaled = (source * col_scale).reshape(width, cols_tiles, tl)
    chosen = jnp.take(scaled, cols_here, axis=1)
    products = jnp.einsum("stb,tab->sta", chosen, local_tiles, precision=HIGH)
    terms = factor * jnp.einsum("sta,tr->sra", products, row_hits, precision=HIGH).reshape(
        width, block_rows
    )
    summed = lax.psum_scatter(terms, "col", scatter_dimension=1, tiled=True)
    u_own = lax.dynamic_slice_in_dim(u_basis, lax.axis_index("col") * u_piece, u_piece, 1)
    qt_piece = summed - jnp.dot(v_factor.T, u_own, precision=HIGH)
    ugram = lax.psum(jnp.dot(qt_piece, qt_piece.T, precision=HIGH), ("row", "col"))
    u_factor = jnp.linalg.cholesky(ugram / total_rows)
    u_next = lower_solve(u_factor, qt_piece)
    return (u_next, v_next, v_factor, u_factor)


def solution(mesh):
    placed = (
        P("row", "col", None, None, None),
        P("row", "col", None),
        P("row", "col", None),
        P("col"),
        P(None, "row"),
        P(None, ("col", "row")),
        P(),
    )
    return jax.shard_map(
        per_device,
        mesh=mesh,
        in_specs=placed,
        out_specs=(P(None, ("row", "col")), P(None, ("col", "row")), P(), P()),
        check_vma=False,
    )
```

profile of v0, /device:TPU:1, one launch (start us, length us, event | category | flops | bytes accessed | tf_op | source)
XLA Modules:
  0.0 630.2 jit_solution(3144894267777404665)
XLA Ops:
  7.2 0.0 copy-start
  7.2 0.0 reduce-scatter.3.cloned.1.call-start
  7.2 0.7 fusion.48
  7.9 0.7 compare_and_fusion
  8.7 0.8 multiply_exponential_fusion
  9.5 0.7 gather_fusion
  10.2 0.0 copy-start.5
  10.2 5.7 fusion.12
  15.9 0.0 copy-done.5
  15.9 2.5 fusion.8
  18.4 0.0 copy-start.3
  18.4 0.0 copy-start.4
  18.4 1.2 bitcast_multiply_fusion
  19.6 0.2 fusion.25
  19.8 0.0 copy-start.1
  19.8 1.3 copy-done.1
  21.2 0.0 reduce-scatter.3.cloned.1.call-update
  21.2 0.0 all-gather.2.cloned.1.call-start
  21.2 246.1 %reduce-scatter.3.cloned.1.call-done = f32[64,128]{1,0:T(8,128)} async-done(((f32[64,8192]{1,0:T(8,128)}), f32[64,128]{1,0:T(8,128)}) %reduce-scatter.3.cloned.1.call-update) | async-done | bytes 32784 | tf_op jit(solution)/shard_map/reduce_scatter | solution.py:46
  267.3 1.0 fusion.53
  268.3 99.8 %psum.14 = f32[64,64]{0,1:T(8,128)S(1)} all-reduce(f32[64,64]{0,1:T(8,128)S(1)} %fusion.53), channel_id=1, replica_groups=mesh['row'=64,'col'=8] {'row','col'}, use_global_device_ids=true, to_apply=%region_1.2 | all-reduce | flops 4096 | bytes 32768 | tf_op jit(solution)/shard_map/psum | solution.py:47
  368.1 0.1 copy.23
  368.2 5.8 cholesky.44
  374.1 0.6 compare_reduce_fusion.1
  374.7 0.7 select_bitcast_fusion.1
  375.4 0.0 copy-start.2
  375.4 4.9 custom-call.8
  380.3 1.6 fusion.34
  381.9 0.0 all-gather.2.cloned.1.call-update
  382.0 0.2 reduce-scatter.5.cloned.1.call-start
  382.2 76.0 %all-gather.2.cloned.1.call-done = f32[64,8192]{1,0:T(8,128)} async-done(((f32[64,128]{1,0:T(8,128)}), f32[64,8192]{1,0:T(8,128)}) %all-gather.2.cloned.1.call-update) | async-done | bytes 2097168 | tf_op jit(solution)/shard_map/all_gather | solution.py:50
  458.2 1.9 copy_bitcast_fusion
  460.1 2.0 gather_fusion.1
  462.1 10.1 %fusion.17 = f32[64,64,128]{2,0,1:T(8,128)S(1)} fusion(f32[1,1,64,128,128]{4,3,2,1,0:T(8,128)} %param.8, f32[64,64,128]{2,1,0:T(8,128)} %gather_fusion.1, pred[64]{0:T(512)(128)(4,1)S(1)} %get-tuple-element.10), kind=kOutput, calls=%fused_computation.18 | convolution fusion | flops 805830656 | bytes 8388672 | tf_op jit(solution)/shard_map/stb,tab->sta/dot_general | solution.py:54
  472.2 2.0 fusion.22
  474.2 1.0 copy.44
  475.2 0.0 reduce-scatter.5.cloned.1.call-update
  475.2 34.1 %reduce-scatter.5.cloned.1.call-done = f32[64,256]{1,0:T(8,128)} async-done(((f32[64,2048]{1,0:T(8,128)}), f32[64,256]{1,0:T(8,128)}) %reduce-scatter.5.cloned.1.call-update) | async-done | bytes 65552 | tf_op jit(solution)/shard_map/reduce_scatter | solution.py:58
  509.3 0.0 copy-done.2
  509.3 1.1 convolution_subtract_fusion
  510.4 0.2 fusion.54
  510.6 99.4 %psum.15 = f32[64,64]{0,1:T(8,128)S(1)} all-reduce(f32[64,64]{0,1:T(8,128)S(1)} %fusion.54), channel_id=1, replica_groups=mesh['row'=64,'col'=8] {'row','col'}, use_global_device_ids=true, to_apply=%region_5.7 | all-reduce | flops 4096 | bytes 32768 | tf_op jit(solution)/shard_map/psum | solution.py:61
  610.0 0.1 copy.27
  610.1 5.8 cholesky.55
  616.0 0.6 compare_reduce_fusion
  616.6 1.3 select_bitcast_fusion
  617.9 4.9 custom-call.9
  622.8 0.9 fusion.31
  (15 shorter events, 0.2 us)
Async XLA Ops:
  7.2 1.5 copy-start
  7.2 260.1 %reduce-scatter.3.cloned.1.call-start = ((), (), s32[]{:S(2)}) async-start(), calls=%async_computation.2 | async-start | bytes 2129920 | tf_op jit(solution)/shard_map/reduce_scatter | solution.py:46
  10.2 5.7 copy-start.5
  18.4 1.2 copy-start.3
  18.4 1.2 copy-start.4
  19.8 1.4 copy-start.1
  21.2 437.0 %all-gather.2.cloned.1.call-start = ((), (), s32[]{:S(2)}) async-start(), calls=%async_computation.3 | async-start | bytes 2129920 | tf_op jit(solution)/shard_map/all_gather | solution.py:50
  375.4 133.9 %copy-start.2 = (f32[64,64]{1,0:T(8,128)}, f32[64,64]{1,0:T(8,128)S(1)}, u32[]{:S(2)}) copy-start(f32[64,64]{1,0:T(8,128)S(1)} %get-tuple-element.8) | copy-start | bytes 49156
  382.0 127.3 %reduce-scatter.5.cloned.1.call-start = ((), (), s32[]{:S(2)}) async-start(), calls=%async_computation.4 | async-start | bytes 589824 | tf_op jit(solution)/shard_map/reduce_scatter | solution.py:58
  462.1 10.1 %copy-start.6 = (s32[1,1,64]{2,1,0:T(1,128)S(1)}, s32[1,1,64]{2,1,0:T(1,128)}, u32[]{:S(2)}) copy-start(s32[1,1,64]{2,1,0:T(1,128)} %param.9) | copy-start | bytes 772
Sparse Core Ops, SparseCore 0:
  21.3 245.9 reduce-scatter.2
  382.1 76.0 all-gather.1
  475.3 33.9 reduce-scatter.4
where the time goes:
time: 631 us; the launch traced here: 630 us
  waiting for transfers between devices  356 us (56%)
  blocking collectives  199 us (32%)
  other arithmetic  30 us (5%)
  matrix products  25.2 us (4%)
  between operations  14 us (2%)
    reduce_scatter x1, waiting for transfers between devices, per_device(): lax.psum_scatter(partial_value, 'row', scatter_dimension=1, tiled=True)  246 us
    psum x1, blocking collectives, per_device(): lax.psum(jnp.dot(pt_piece, pt_piece.T, precision=HIGH), ('row', 'col'))  99.8 us
    psum x1, blocking collectives, per_device(): lax.psum(jnp.dot(qt_piece, qt_piece.T, precision=HIGH), ('row', 'col'))  99.4 us
    all_gather x1, waiting for transfers between devices, per_device(): source = lax.all_gather(v_next, 'row', axis=1, tiled=True)  76 us
    reduce_scatter x1, waiting for transfers between devices, per_device(): summed = lax.psum_scatter(terms, 'col', scatter_dimension=1, tiled=True)  34.1 us
  transfers between devices with their start and end apart: 3, of which 3 were waited for; matrix products, arithmetic and copies ran while one was open for 0% of the time, Pallas kernels for 0%

commit v1 on v0

v1 whole, which is shorter than its diff:
```python
import math

import jax
import jax.numpy as jnp
from jax import lax
from jax.sharding import PartitionSpec as P

HIGH = lax.Precision.HIGHEST


def lower_solve(factor, rhs):
    return lax.linalg.triangular_solve(factor, rhs, left_side=True, lower=True)


def butterfly_sum(x, axis):
    n = lax.axis_size(axis)
    k = 1
    while k < n:
        x = x + lax.ppermute(x, axis, [(i, i ^ k) for i in range(n)])
        k *= 2
    return x


def per_device(tiles, tile_rows, tile_cols, exponents, u_basis, v_basis, prior):
    local_tiles = tiles[0, 0]
    rows_here = tile_rows[0, 0]
    cols_here = tile_cols[0, 0]
    count, tl, _ = local_tiles.shape
    width, block_rows = u_basis.shape
    block_cols = exponents.shape[0]
    rows_tiles = block_rows // tl
    cols_tiles = block_cols // tl
    n_row = lax.axis_size("row")
    n_col = lax.axis_size("col")
    total_rows = block_rows * n_row
    total_cols = block_cols * n_col
    v_piece = v_basis.shape[1]
    u_piece = block_rows // n_col
    col_scale = jnp.exp2(-exponents.astype(jnp.float32))
    lowtri = jnp.tril(prior)
    col_hits = (cols_here[:, None] == jnp.arange(cols_tiles, dtype=jnp.int32)[None, :]).astype(
        jnp.float32
    )
    row_hits = (rows_here[:, None] == jnp.arange(rows_tiles, dtype=jnp.int32)[None, :]).astype(
        jnp.float32
    )
    picked = jnp.take(u_basis.reshape(width, rows_tiles, tl), rows_here, axis=1)
    prod = jnp.einsum("sta,tab->stb", picked, local_tiles, precision=HIGH)
    partial = jnp.einsum("stb,tc->csb", prod, col_hits, precision=HIGH).reshape(
        n_row, v_piece // tl, width, tl
    )
    partial = (partial * col_scale.reshape(n_row, v_piece // tl, 1, tl)).transpose(0, 2, 1, 3)
    partial = partial.reshape(n_row, width, v_piece)
    received = lax.all_to_all(partial, "row", 0, 0, tiled=True)
    pt_piece = received.sum(0) - jnp.dot(lowtri, v_basis, precision=HIGH)
    spread = jnp.broadcast_to(pt_piece[None], (n_row, width, v_piece))
    column = lax.all_to_all(spread, "row", 0, 0, tiled=True)
    gram = butterfly_sum(jnp.einsum("jsb,jtb->st", column, column, precision=HIGH), "col")
    v_factor = jnp.linalg.cholesky(gram / total_cols)
    pt_column = column.transpose(1, 0, 2).reshape(width, block_cols)
    v_column = lower_solve(v_factor, pt_column)
    offset = lax.axis_index("row") * v_piece
    v_next = lax.dynamic_slice_in_dim(v_column, offset, v_piece, 1)
    factor = math.sqrt(total_rows / total_cols)
    scaled = (v_column * col_scale).reshape(width, cols_tiles, tl)
    chosen = jnp.take(scaled, cols_here, axis=1)
    products = jnp.einsum("stb,tab->sta", chosen, local_tiles, precision=HIGH)
    terms = factor * jnp.einsum("sta,tr->rsa", products, row_hits, precision=HIGH)
    terms = terms.reshape(n_col, u_piece // tl, width, tl).transpose(0, 2, 1, 3)
    terms = terms.reshape(n_col, width, u_piece)
    summed = lax.all_to_all(terms, "col", 0, 0, tiled=True).sum(0)
    u_own = lax.dynamic_slice_in_dim(u_basis, lax.axis_index("col") * u_piece, u_piece, 1)
    qt_piece = summed - jnp.dot(v_factor.T, u_own, precision=HIGH)
    ugram = jnp.dot(qt_piece, qt_piece.T, precision=HIGH)
    ugram = butterfly_sum(butterfly_sum(ugram, "col"), "row")
    u_factor = jnp.linalg.cholesky(ugram / total_rows)
    u_next = lower_solve(u_factor, qt_piece)
    return (u_next, v_next, v_factor, u_factor)


def solution(mesh):
    placed = (
        P("row", "col", None, None, None),
        P("row", "col", None),
        P("row", "col", None),
        P("col"),
        P(None, "row"),
        P(None, ("col", "row")),
        P(),
    )
    return jax.shard_map(
        per_device,
        mesh=mesh,
        in_specs=placed,
        out_specs=(P(None, ("row", "col")), P(None, ("col", "row")), P(), P()),
        check_vma=False,
    )
```

time: 631 us -> 283 us (0.45)
  the two profiles are of different devices: /device:TPU:1 before, /device:TPU:2 now
where the time goes in v1:
time: 283 us; the launch traced here: 282 us
  blocking collectives  129 us (46%)
  waiting for transfers between devices  48.8 us (17%)
  starting transfers between devices  41.1 us (15%)
  other arithmetic  27.5 us (10%)
  matrix products  25.5 us (9%)
  local copies, waits for them, and re-layouts  9.12 us (3%)
    all_to_all x1, blocking collectives, per_device(): received = lax.all_to_all(partial, 'row', 0, 0, tiled=True)  68.8 us
    all_to_all x1, blocking collectives, per_device(): column = lax.all_to_all(spread, 'row', 0, 0, tiled=True)  60.5 us
    ppermute x12, waiting for transfers between devices, butterfly_sum(): x = x + lax.ppermute(x, axis, [(i, i ^ k) for i in range(n)])  39.9 us
    ppermute x12, starting transfers between devices, butterfly_sum(): x = x + lax.ppermute(x, axis, [(i, i ^ k) for i in range(n)])  36.4 us
    another operation x4, other arithmetic, lower_solve(): return lax.linalg.triangular_solve(factor, rhs, left_side=True, lower=True)  11.7 us
    dot_general x1, matrix products, per_device(): products = jnp.einsum('stb,tab->sta', chosen, local_tiles, precision=HIGH)  10.1 us
    all_to_all x1, waiting for transfers between devices, per_device(): summed = lax.all_to_all(terms, 'col', 0, 0, tiled=True).sum(0)  8.89 us
    another operation x3, other arithmetic, per_device(): u_factor = jnp.linalg.cholesky(ugram / total_rows)  6.52 us
  transfers between devices with their start and end apart: 13, of which 13 were waited for; matrix products, arithmetic and copies ran while one was open for 0% of the time, Pallas kernels for 0%

profile of v1, /device:TPU:2, one launch (start us, length us, event | category | flops | bytes accessed | tf_op | source)
XLA Modules:
  0.0 282.3 jit_solution(9380763129918522461)
XLA Ops:
  0.6 0.7 compare_and_fusion
  2.0 0.8 multiply_exponential_fusion
  2.9 0.7 gather_fusion
  3.6 5.7 %fusion.15 = f32[64,64,128]{2,0,1:T(8,128)S(1)} fusion(f32[1,1,64,128,128]{4,3,2,1,0:T(8,128)} %param.8, f32[64,64,128]{2,1,0:T(8,128)S(1)} %gather_fusion, pred[64]{0:T(512)(128)(4,1)S(1)} %compare_and_fusion), kind=kOutput, calls=%fused_computation.19 | convolution fusion | flops 805830656 | bytes 8388672 | tf_op jit(solution)/shard_map/sta,tab->stb/dot_general | solution.py:48
  9.3 2.5 fusion.25
  11.8 1.2 copy.38
  13.0 68.8 %all_to_all.15 = f32[64,64,128]{2,1,0:T(8,128)S(1)} all-to-all(f32[64,64,128]{2,1,0:T(8,128)S(1)} %copy.38), channel_id=1, replica_groups=mesh['row'=64,'col'=8] {'row'}, dimensions={0} | all-to-all | bytes 4194304 | tf_op jit(solution)/shard_map/all_to_all | solution.py:54
  83.0 60.5 %all_to_all.16 = f32[64,64,128]{2,1,0:T(8,128)S(1)} all-to-all(f32[64,64,128]{2,1,0:T(8,128)S(1)} %broadcast_in_dim.36), channel_id=1, replica_groups=mesh['row'=64,'col'=8] {'row'}, dimensions={0} | all-to-all | bytes 4194304 | tf_op jit(solution)/shard_map/all_to_all | solution.py:57
  143.5 1.8 convolution_bitcast_fusion
  145.3 1.9 collective-permute-start
  147.2 1.2 collective-permute-done
  148.4 2.4 collective-permute-start.1
  150.9 3.3 %collective-permute-done.1 = f32[64,64]{0,1:T(8,128)S(1)} collective-permute-done((f32[64,64]{0,1:T(8,128)S(1)}, f32[64,64]{0,1:T(8,128)S(1)}, u32[]{:S(2)}, u32[]{:S(2)}) %collective-permute-start.1) | collective-permute-done | bytes 16416 | tf_op jit(solution)/shard_map/ppermute | solution.py:19
  154.2 4.2 %collective-permute-start.2 = (f32[64,64]{0,1:T(8,128)S(1)}, f32[64,64]{0,1:T(8,128)S(1)}, u32[]{:S(2)}, u32[]{:S(2)}) collective-permute-start(f32[64,64]{0,1:T(8,128)S(1)} %add.102), channel_id=1, source_target_pairs={{0,4},{1,5},{2,6},{3,7},{4,0},{5,1},{6,2},{7,3},{8,12},{9,13},{10,... | collective-permute-start | bytes 49160 | tf_op jit(solution)/shard_map/ppermute | solution.py:19
  158.4 3.1 %collective-permute-done.2 = f32[64,64]{0,1:T(8,128)S(1)} collective-permute-done((f32[64,64]{0,1:T(8,128)S(1)}, f32[64,64]{0,1:T(8,128)S(1)}, u32[]{:S(2)}, u32[]{:S(2)}) %collective-permute-start.2) | collective-permute-done | bytes 16416 | tf_op jit(solution)/shard_map/ppermute | solution.py:19
  161.6 5.8 %cholesky.44 = f32[64,64]{1,0:T(8,128)S(1)} custom-call(f32[64,64]{1,0:T(8,128)S(1)} %fusion.40), custom_call_target="Cholesky" | custom-call | tf_op jit(solution)/shard_map/jit(cholesky)/cholesky | solution.py:59
  168.8 4.9 %custom-call.8 = f32[1,64,64]{1,2,0:T(8,128)S(1)} custom-call(f32[1,64,64]{2,1,0:T(8,128)S(1)} %get-tuple-element.7), custom_call_target="InvertDiagBlocksLowerTriangular" | custom-call | tf_op jit(solution)/shard_map/triangular_solve | solution.py:12
  173.7 1.9 fusion.4
  175.6 1.3 copy-done.1
  177.3 2.0 gather_fusion.1
  179.3 10.1 %fusion.20 = f32[64,64,128]{2,0,1:T(8,128)S(1)} fusion(f32[1,1,64,128,128]{4,3,2,1,0:T(8,128)} %param.8, f32[64,64,128]{2,1,0:T(8,128)} %gather_fusion.1, pred[64]{0:T(512)(128)(4,1)S(1)} %compare_and_fusion.1), kind=kOutput, calls=%fused_computation.20 | convolution fusion | flops 805830656 | bytes 8388672 | tf_op jit(solution)/shard_map/stb,tab->sta/dot_general | solution.py:67
  189.4 2.0 fusion.28
  191.8 1.0 copy.53
  192.8 4.7 %all-to-all-start.2 = ((f32[8,64,256]{2,1,0:T(8,128)}), f32[8,64,256]{2,1,0:T(8,128)S(1)}, u32[]{:S(2)}, u32[]{:S(2)}) async-start(f32[8,64,256]{2,1,0:T(8,128)} %copy.53), calls=%async_computation.2 | async-start | bytes 1048576 | tf_op jit(solution)/shard_map/all_to_all | solution.py:71
  197.4 8.9 %all-to-all-done.2 = f32[8,64,256]{2,1,0:T(8,128)S(1)} async-done(((f32[8,64,256]{2,1,0:T(8,128)}), f32[8,64,256]{2,1,0:T(8,128)S(1)}, u32[]{:S(2)}, u32[]{:S(2)}) %all-to-all-start.2) | async-done | bytes 524320 | tf_op jit(solution)/shard_map/all_to_all | solution.py:71
  206.9 1.9 collective-permute-start.3
  208.8 1.2 collective-permute-done.3
  210.0 3.4 %collective-permute-start.4 = (f32[64,64]{0,1:T(8,128)S(1)}, f32[64,64]{0,1:T(8,128)S(1)}, u32[]{:S(2)}, u32[]{:S(2)}) collective-permute-start(f32[64,64]{0,1:T(8,128)S(1)} %add.107), channel_id=1, source_target_pairs={{0,2},{1,3},{2,0},{3,1},{4,6},{5,7},{6,4},{7,5},{8,10},{9,11},{10,... | collective-permute-start | bytes 49160 | tf_op jit(solution)/shard_map/ppermute | solution.py:19
  213.3 2.4 collective-permute-done.4
  215.8 3.4 %collective-permute-start.5 = (f32[64,64]{0,1:T(8,128)S(1)}, f32[64,64]{0,1:T(8,128)S(1)}, u32[]{:S(2)}, u32[]{:S(2)}) collective-permute-start(f32[64,64]{0,1:T(8,128)S(1)} %add.108), channel_id=1, source_target_pairs={{0,4},{1,5},{2,6},{3,7},{4,0},{5,1},{6,2},{7,3},{8,12},{9,13},{10,... | collective-permute-start | bytes 49160 | tf_op jit(solution)/shard_map/ppermute | solution.py:19
  219.1 3.9 %collective-permute-done.5 = f32[64,64]{0,1:T(8,128)S(1)} collective-permute-done((f32[64,64]{0,1:T(8,128)S(1)}, f32[64,64]{0,1:T(8,128)S(1)}, u32[]{:S(2)}, u32[]{:S(2)}) %collective-permute-start.5) | collective-permute-done | bytes 16416 | tf_op jit(solution)/shard_map/ppermute | solution.py:19
  223.1 2.9 %collective-permute-start.6 = (f32[64,64]{0,1:T(8,128)S(1)}, f32[64,64]{0,1:T(8,128)S(1)}, u32[]{:S(2)}, u32[]{:S(2)}) collective-permute-start(f32[64,64]{0,1:T(8,128)S(1)} %add.109), channel_id=1, source_target_pairs={{0,8},{8,0},{16,24},{24,16},{32,40},{40,32},{48,56},{56,48},{64,72... | collective-permute-start | bytes 49160 | tf_op jit(solution)/shard_map/ppermute | solution.py:19
  225.9 2.9 %collective-permute-done.6 = f32[64,64]{0,1:T(8,128)S(1)} collective-permute-done((f32[64,64]{0,1:T(8,128)S(1)}, f32[64,64]{0,1:T(8,128)S(1)}, u32[]{:S(2)}, u32[]{:S(2)}) %collective-permute-start.6) | collective-permute-done | bytes 16416 | tf_op jit(solution)/shard_map/ppermute | solution.py:19
  228.9 2.8 %collective-permute-start.7 = (f32[64,64]{0,1:T(8,128)S(1)}, f32[64,64]{0,1:T(8,128)S(1)}, u32[]{:S(2)}, u32[]{:S(2)}) collective-permute-start(f32[64,64]{0,1:T(8,128)S(1)} %add.110), channel_id=1, source_target_pairs={{0,16},{8,24},{16,0},{24,8},{32,48},{40,56},{48,32},{56,40},{64,80... | collective-permute-start | bytes 49160 | tf_op jit(solution)/shard_map/ppermute | solution.py:19
  231.7 3.8 %collective-permute-done.7 = f32[64,64]{0,1:T(8,128)S(1)} collective-permute-done((f32[64,64]{0,1:T(8,128)S(1)}, f32[64,64]{0,1:T(8,128)S(1)}, u32[]{:S(2)}, u32[]{:S(2)}) %collective-permute-start.7) | collective-permute-done | bytes 16416 | tf_op jit(solution)/shard_map/ppermute | solution.py:19
  235.6 4.7 %collective-permute-start.8 = (f32[64,64]{0,1:T(8,128)S(1)}, f32[64,64]{0,1:T(8,128)S(1)}, u32[]{:S(2)}, u32[]{:S(2)}) collective-permute-start(f32[64,64]{0,1:T(8,128)S(1)} %add.111), channel_id=1, source_target_pairs={{0,32},{8,40},{16,48},{24,56},{32,0},{40,8},{48,16},{56,24},{64,96... | collective-permute-start | bytes 49160 | tf_op jit(solution)/shard_map/ppermute | solution.py:19
  240.3 5.3 %collective-permute-done.8 = f32[64,64]{0,1:T(8,128)S(1)} collective-permute-done((f32[64,64]{0,1:T(8,128)S(1)}, f32[64,64]{0,1:T(8,128)S(1)}, u32[]{:S(2)}, u32[]{:S(2)}) %collective-permute-start.8) | collective-permute-done | bytes 16416 | tf_op jit(solution)/shard_map/ppermute | solution.py:19
  245.6 2.6 collective-permute-start.9
  248.2 3.2 %collective-permute-done.9 = f32[64,64]{0,1:T(8,128)S(1)} collective-permute-done((f32[64,64]{0,1:T(8,128)S(1)}, f32[64,64]{0,1:T(8,128)S(1)}, u32[]{:S(2)}, u32[]{:S(2)}) %collective-permute-start.9) | collective-permute-done | bytes 16416 | tf_op jit(solution)/shard_map/ppermute | solution.py:19
  251.4 3.4 %collective-permute-start.10 = (f32[64,64]{0,1:T(8,128)S(1)}, f32[64,64]{0,1:T(8,128)S(1)}, u32[]{:S(2)}, u32[]{:S(2)}) collective-permute-start(f32[64,64]{0,1:T(8,128)S(1)} %add.113), channel_id=1, source_target_pairs={{0,128},{8,136},{16,144},{24,152},{32,160},{40,168},{48,176},{56,1... | collective-permute-start | bytes 49160 | tf_op jit(solution)/shard_map/ppermute | solution.py:19
  254.8 4.0 %collective-permute-done.10 = f32[64,64]{0,1:T(8,128)S(1)} collective-permute-done((f32[64,64]{0,1:T(8,128)S(1)}, f32[64,64]{0,1:T(8,128)S(1)}, u32[]{:S(2)}, u32[]{:S(2)}) %collective-permute-start.10) | collective-permute-done | bytes 16416 | tf_op jit(solution)/shard_map/ppermute | solution.py:19
  258.9 2.8 %collective-permute-start.11 = (f32[64,64]{0,1:T(8,128)S(1)}, f32[64,64]{0,1:T(8,128)S(1)}, u32[]{:S(2)}, u32[]{:S(2)}) collective-permute-start(f32[64,64]{0,1:T(8,128)S(1)} %add.114), channel_id=1, source_target_pairs={{0,256},{8,264},{16,272},{24,280},{32,288},{40,296},{48,304},{56,3... | collective-permute-start | bytes 49160 | tf_op jit(solution)/shard_map/ppermute | solution.py:19
  261.7 1.4 constant_dynamic-slice_fusion
  263.1 5.5 %collective-permute-done.11 = f32[64,64]{0,1:T(8,128)S(1)} collective-permute-done((f32[64,64]{0,1:T(8,128)S(1)}, f32[64,64]{0,1:T(8,128)S(1)}, u32[]{:S(2)}, u32[]{:S(2)}) %collective-permute-start.11) | collective-permute-done | bytes 16416 | tf_op jit(solution)/shard_map/ppermute | solution.py:19
  268.7 5.8 %cholesky.55 = f32[64,64]{1,0:T(8,128)S(1)} custom-call(f32[64,64]{1,0:T(8,128)S(1)} %fusion.38), custom_call_target="Cholesky" | custom-call | tf_op jit(solution)/shard_map/jit(cholesky)/cholesky | solution.py:76
  275.2 1.3 select_bitcast_fusion
  276.5 4.9 %custom-call.9 = f32[1,64,64]{1,2,0:T(8,128)S(1)} custom-call(f32[1,64,64]{2,1,0:T(8,128)S(1)} %get-tuple-element.5), custom_call_target="InvertDiagBlocksLowerTriangular" | custom-call | tf_op jit(solution)/shard_map/triangular_solve | solution.py:12
  281.4 0.9 fusion.36
  (48 shorter events, 5.4 us)
Async XLA Ops:
  0.6 2.2 copy-start
  3.6 5.7 %copy-start.5 = (s32[1,1,64]{2,1,0:T(1,128)S(1)}, s32[1,1,64]{2,1,0:T(1,128)}, u32[]{:S(2)}) copy-start(s32[1,1,64]{2,1,0:T(1,128)} %param.10) | copy-start | bytes 772
  81.8 0.8 copy-start.3
  81.8 0.8 copy-start.4
  145.3 3.1 %collective-permute-start = (f32[64,64]{0,1:T(8,128)S(1)}, f32[64,64]{0,1:T(8,128)S(1)}, u32[]{:S(2)}, u32[]{:S(2)}) collective-permute-start(f32[64,64]{0,1:T(8,128)S(1)} %convolution_bitcast_fusion), channel_id=1, source_target_pairs={{0,1},{1,0},{2,3},{3,2},{4,5},{5,4},{6,7},{7,6},{8,9},{9,8},{10,11... | collective-permute-start | bytes 49160 | tf_op jit(solution)/shard_map/ppermute | solution.py:19
  148.4 5.8 %collective-permute-start.1 = (f32[64,64]{0,1:T(8,128)S(1)}, f32[64,64]{0,1:T(8,128)S(1)}, u32[]{:S(2)}, u32[]{:S(2)}) collective-permute-start(f32[64,64]{0,1:T(8,128)S(1)} %add.101), channel_id=1, source_target_pairs={{0,2},{1,3},{2,0},{3,1},{4,6},{5,7},{6,4},{7,5},{8,10},{9,11},{10,... | collective-permute-start | bytes 49160 | tf_op jit(solution)/shard_map/ppermute | solution.py:19
  154.2 7.3 %collective-permute-start.2 = (f32[64,64]{0,1:T(8,128)S(1)}, f32[64,64]{0,1:T(8,128)S(1)}, u32[]{:S(2)}, u32[]{:S(2)}) collective-permute-start(f32[64,64]{0,1:T(8,128)S(1)} %add.102), channel_id=1, source_target_pairs={{0,4},{1,5},{2,6},{3,7},{4,0},{5,1},{6,2},{7,3},{8,12},{9,13},{10,... | collective-permute-start | bytes 49160 | tf_op jit(solution)/shard_map/ppermute | solution.py:19
  168.8 37.6 %copy-start.2 = (f32[64,64]{1,0:T(8,128)}, f32[64,64]{1,0:T(8,128)S(1)}, u32[]{:S(2)}) copy-start(f32[64,64]{1,0:T(8,128)S(1)} %get-tuple-element.8) | copy-start | bytes 49156
  175.6 1.4 copy-start.1
  179.3 10.1 %copy-start.6 = (s32[1,1,64]{2,1,0:T(1,128)S(1)}, s32[1,1,64]{2,1,0:T(1,128)}, u32[]{:S(2)}) copy-start(s32[1,1,64]{2,1,0:T(1,128)} %param.9) | copy-start | bytes 772
  192.8 13.6 %all-to-all-start.2 = ((f32[8,64,256]{2,1,0:T(8,128)}), f32[8,64,256]{2,1,0:T(8,128)S(1)}, u32[]{:S(2)}, u32[]{:S(2)}) async-start(f32[8,64,256]{2,1,0:T(8,128)} %copy.53), calls=%async_computation.2 | async-start | bytes 1048576 | tf_op jit(solution)/shard_map/all_to_all | solution.py:71
  206.9 3.1 %collective-permute-start.3 = (f32[64,64]{0,1:T(8,128)S(1)}, f32[64,64]{0,1:T(8,128)S(1)}, u32[]{:S(2)}, u32[]{:S(2)}) collective-permute-start(f32[64,64]{0,1:T(8,128)S(1)} %fusion.58), channel_id=1, source_target_pairs={{0,1},{1,0},{2,3},{3,2},{4,5},{5,4},{6,7},{7,6},{8,9},{9,8},{10,11... | collective-permute-start | bytes 49160 | tf_op jit(solution)/shard_map/ppermute | solution.py:19
  210.0 5.8 %collective-permute-start.4 = (f32[64,64]{0,1:T(8,128)S(1)}, f32[64,64]{0,1:T(8,128)S(1)}, u32[]{:S(2)}, u32[]{:S(2)}) collective-permute-start(f32[64,64]{0,1:T(8,128)S(1)} %add.107), channel_id=1, source_target_pairs={{0,2},{1,3},{2,0},{3,1},{4,6},{5,7},{6,4},{7,5},{8,10},{9,11},{10,... | collective-permute-start | bytes 49160 | tf_op jit(solution)/shard_map/ppermute | solution.py:19
  215.8 7.3 %collective-permute-start.5 = (f32[64,64]{0,1:T(8,128)S(1)}, f32[64,64]{0,1:T(8,128)S(1)}, u32[]{:S(2)}, u32[]{:S(2)}) collective-permute-start(f32[64,64]{0,1:T(8,128)S(1)} %add.108), channel_id=1, source_target_pairs={{0,4},{1,5},{2,6},{3,7},{4,0},{5,1},{6,2},{7,3},{8,12},{9,13},{10,... | collective-permute-start | bytes 49160 | tf_op jit(solution)/shard_map/ppermute | solution.py:19
  223.1 5.8 %collective-permute-start.6 = (f32[64,64]{0,1:T(8,128)S(1)}, f32[64,64]{0,1:T(8,128)S(1)}, u32[]{:S(2)}, u32[]{:S(2)}) collective-permute-start(f32[64,64]{0,1:T(8,128)S(1)} %add.109), channel_id=1, source_target_pairs={{0,8},{8,0},{16,24},{24,16},{32,40},{40,32},{48,56},{56,48},{64,72... | collective-permute-start | bytes 49160 | tf_op jit(solution)/shard_map/ppermute | solution.py:19
  228.9 6.7 %collective-permute-start.7 = (f32[64,64]{0,1:T(8,128)S(1)}, f32[64,64]{0,1:T(8,128)S(1)}, u32[]{:S(2)}, u32[]{:S(2)}) collective-permute-start(f32[64,64]{0,1:T(8,128)S(1)} %add.110), channel_id=1, source_target_pairs={{0,16},{8,24},{16,0},{24,8},{32,48},{40,56},{48,32},{56,40},{64,80... | collective-permute-start | bytes 49160 | tf_op jit(solution)/shard_map/ppermute | solution.py:19
  235.6 10.1 %collective-permute-start.8 = (f32[64,64]{0,1:T(8,128)S(1)}, f32[64,64]{0,1:T(8,128)S(1)}, u32[]{:S(2)}, u32[]{:S(2)}) collective-permute-start(f32[64,64]{0,1:T(8,128)S(1)} %add.111), channel_id=1, source_target_pairs={{0,32},{8,40},{16,48},{24,56},{32,0},{40,8},{48,16},{56,24},{64,96... | collective-permute-start | bytes 49160 | tf_op jit(solution)/shard_map/ppermute | solution.py:19
  245.6 5.8 %collective-permute-start.9 = (f32[64,64]{0,1:T(8,128)S(1)}, f32[64,64]{0,1:T(8,128)S(1)}, u32[]{:S(2)}, u32[]{:S(2)}) collective-permute-start(f32[64,64]{0,1:T(8,128)S(1)} %add.112), channel_id=1, source_target_pairs={{0,64},{8,72},{16,80},{24,88},{32,96},{40,104},{48,112},{56,120},{... | collective-permute-start | bytes 49160 | tf_op jit(solution)/shard_map/ppermute | solution.py:19
  251.4 7.4 %collective-permute-start.10 = (f32[64,64]{0,1:T(8,128)S(1)}, f32[64,64]{0,1:T(8,128)S(1)}, u32[]{:S(2)}, u32[]{:S(2)}) collective-permute-start(f32[64,64]{0,1:T(8,128)S(1)} %add.113), channel_id=1, source_target_pairs={{0,128},{8,136},{16,144},{24,152},{32,160},{40,168},{48,176},{56,1... | collective-permute-start | bytes 49160 | tf_op jit(solution)/shard_map/ppermute | solution.py:19
  258.9 9.7 %collective-permute-start.11 = (f32[64,64]{0,1:T(8,128)S(1)}, f32[64,64]{0,1:T(8,128)S(1)}, u32[]{:S(2)}, u32[]{:S(2)}) collective-permute-start(f32[64,64]{0,1:T(8,128)S(1)} %add.114), channel_id=1, source_target_pairs={{0,256},{8,264},{16,272},{24,280},{32,288},{40,296},{48,304},{56,3... | collective-permute-start | bytes 49160 | tf_op jit(solution)/shard_map/ppermute | solution.py:19

commit v2 on v1

--- a/solution.py
+++ b/solution.py
@@ -12,13 +12,12 @@
     return lax.linalg.triangular_solve(factor, rhs, left_side=True, lower=True)
 
 
-def butterfly_sum(x, axis):
+ROW = ("row_hi", "row_lo")
+
+
+def gather_sum(x, axis):
     n = lax.axis_size(axis)
-    k = 1
-    while k < n:
-        x = x + lax.ppermute(x, axis, [(i, i ^ k) for i in range(n)])
-        k *= 2
-    return x
+    return lax.all_to_all(jnp.broadcast_to(x[None], (n,) + x.shape), axis, 0, 0, tiled=True).sum(0)
 
 
 def per_device(tiles, tile_rows, tile_cols, exponents, u_basis, v_basis, prior):
@@ -30,7 +29,7 @@
     block_cols = exponents.shape[0]
     rows_tiles = block_rows // tl
     cols_tiles = block_cols // tl
-    n_row = lax.axis_size("row")
+    n_row = lax.axis_size(ROW)
     n_col = lax.axis_size("col")
     total_rows = block_rows * n_row
     total_cols = block_cols * n_col
@@ -51,15 +50,15 @@
     )
     partial = (partial * col_scale.reshape(n_row, v_piece // tl, 1, tl)).transpose(0, 2, 1, 3)
     partial = partial.reshape(n_row, width, v_piece)
-    received = lax.all_to_all(partial, "row", 0, 0, tiled=True)
+    received = lax.all_to_all(partial, ROW, 0, 0, tiled=True)
     pt_piece = received.sum(0) - jnp.dot(lowtri, v_basis, precision=HIGH)
     spread = jnp.broadcast_to(pt_piece[None], (n_row, width, v_piece))
-    column = lax.all_to_all(spread, "row", 0, 0, tiled=True)
-    gram = butterfly_sum(jnp.einsum("jsb,jtb->st", column, column, precision=HIGH), "col")
+    column = lax.all_to_all(spread, ROW, 0, 0, tiled=True)
+    gram = gather_sum(jnp.einsum("jsb,jtb->st", column, column, precision=HIGH), "col")
     v_factor = jnp.linalg.cholesky(gram / total_cols)
     pt_column = column.transpose(1, 0, 2).reshape(width, block_cols)
     v_column = lower_solve(v_factor, pt_column)
-    offset = lax.axis_index("row") * v_piece
+    offset = lax.axis_index(ROW) * v_piece
     v_next = lax.dynamic_slice_in_dim(v_column, offset, v_piece, 1)
     factor = math.sqrt(total_rows / total_cols)
     scaled = (v_column * col_scale).reshape(width, cols_tiles, tl)
@@ -72,26 +71,32 @@
     u_own = lax.dynamic_slice_in_dim(u_basis, lax.axis_index("col") * u_piece, u_piece, 1)
     qt_piece = summed - jnp.dot(v_factor.T, u_own, precision=HIGH)
     ugram = jnp.dot(qt_piece, qt_piece.T, precision=HIGH)
-    ugram = butterfly_sum(butterfly_sum(ugram, "col"), "row")
+    ugram = gather_sum(gather_sum(gather_sum(ugram, "col"), "row_lo"), "row_hi")
     u_factor = jnp.linalg.cholesky(ugram / total_rows)
     u_next = lower_solve(u_factor, qt_piece)
     return (u_next, v_next, v_factor, u_factor)
 
 
 def solution(mesh):
+    n_row = mesh.shape["row"]
+    n_col = mesh.shape["col"]
+    lo = 1
+    while lo * lo < n_row:
+        lo *= 2
+    grid = jax.sharding.Mesh(mesh.devices.reshape(n_row // lo, lo, n_col), ROW + ("col",))
     placed = (
-        P("row", "col", None, None, None),
-        P("row", "col", None),
-        P("row", "col", None),
+        P(ROW, "col", None, None, None),
+        P(ROW, "col", None),
+        P(ROW, "col", None),
         P("col"),
-        P(None, "row"),
-        P(None, ("col", "row")),
+        P(None, ROW),
+        P(None, ("col",) + ROW),
         P(),
     )
     return jax.shard_map(
         per_device,
-        mesh=mesh,
+        mesh=grid,
         in_specs=placed,
-        out_specs=(P(None, ("row", "col")), P(None, ("col", "row")), P(), P()),
+        out_specs=(P(None, ROW + ("col",)), P(None, ("col",) + ROW), P(), P()),
         check_vma=False,
     )

time: 283 us -> 258 us (0.912)
  blocking collectives: 129 us -> 89.9 us
  waiting for transfers between devices: 48.8 us -> 72.9 us
  starting transfers between devices: 41.1 us -> 22.5 us
  local copies, waits for them, and re-layouts: 9.12 us -> 13.6 us
  other arithmetic: 27.5 us -> 31.4 us
    all_to_all x0 -> x3, waiting for transfers between devices: none -> 63.9 us  [the longest x1 51.6 us: per_device(): column = lax.all_to_all(spread, ROW, 0, 0, tiled=True)]
    ppermute x12 -> x0, waiting for transfers between devices: 39.9 us -> none  [butterfly_sum(): x = x + lax.ppermute(x, axis, [(i, i ^ k) for i in range(n)])]
    all_to_all x2 -> x3, blocking collectives: 129 us -> 89.9 us  [the longest x1 68.8 us: per_device(): received = lax.all_to_all(partial, ROW, 0, 0, tiled=True)]
    ppermute x12 -> x0, starting transfers between devices: 36.4 us -> none  [butterfly_sum(): x = x + lax.ppermute(x, axis, [(i, i ^ k) for i in range(n)])]
    all_to_all x0 -> x3, starting transfers between devices: none -> 17.7 us  [the longest x1 9.13 us: per_device(): column = lax.all_to_all(spread, ROW, 0, 0, tiled=True)]
    all_to_all x0 -> x4, other arithmetic: none -> 3.81 us  [gather_sum(): lax.all_to_all(jnp.broadcast_to(x[None], (n,) + x.shape), axis, 0, 0, til...]
  transfers between devices with their start and end apart: 13 -> 4, of which waited for: 13 -> 4; matrix products, arithmetic and copies ran while one was open for 0% -> 1% of each run, Pallas kernels for 0% -> 0%
where the time goes in v2:
time: 258 us; the launch traced here: 257 us
  blocking collectives  89.9 us (35%)
  waiting for transfers between devices  72.9 us (28%)
  other arithmetic  31.4 us (12%)
  matrix products  25.5 us (10%)
  starting transfers between devices  22.5 us (9%)
  local copies, waits for them, and re-layouts  13.6 us (5%)
    all_to_all x1, blocking collectives, per_device(): received = lax.all_to_all(partial, ROW, 0, 0, tiled=True)  68.8 us
    all_to_all x1, waiting for transfers between devices, per_device(): column = lax.all_to_all(spread, ROW, 0, 0, tiled=True)  51.6 us
    all_to_all x2, blocking collectives, gather_sum(): lax.all_to_all(jnp.broadcast_to(x[None], (n,) + x.shape), axis, 0, 0, til...  21.2 us
    all_to_all x2, waiting for transfers between devices, gather_sum(): lax.all_to_all(jnp.broadcast_to(x[None], (n,) + x.shape), axis, 0, 0, til...  12.4 us
    another operation x4, other arithmetic, lower_solve(): return lax.linalg.triangular_solve(factor, rhs, left_side=True, lower=True)  11.7 us
    dot_general x1, matrix products, per_device(): products = jnp.einsum('stb,tab->sta', chosen, local_tiles, precision=HIGH)  10.1 us
    all_to_all x1, starting transfers between devices, per_device(): column = lax.all_to_all(spread, ROW, 0, 0, tiled=True)  9.13 us
    all_to_all x1, waiting for transfers between devices, per_device(): summed = lax.all_to_all(terms, 'col', 0, 0, tiled=True).sum(0)  8.92 us
  transfers between devices with their start and end apart: 4, of which 4 were waited for; matrix products, arithmetic and copies ran while one was open for 1% of the time, Pallas kernels for 0%

profile of v2, /device:TPU:2, one launch (start us, length us, event | category | flops | bytes accessed | tf_op | source)
XLA Modules:
  0.0 256.8 jit_solution(15706063894640314263)
XLA Ops:
  0.6 0.7 compare_and_fusion
  1.4 0.7 fusion.51
  2.0 0.8 multiply_exponential_fusion
  2.9 0.7 gather_fusion
  3.6 5.7 %fusion.15 = f32[64,64,128]{2,0,1:T(8,128)S(1)} fusion(f32[1,1,64,128,128]{4,3,2,1,0:T(8,128)} %param.8, f32[64,64,128]{2,1,0:T(8,128)S(1)} %gather_fusion, pred[64]{0:T(512)(128)(4,1)S(1)} %compare_and_fusion), kind=kOutput, calls=%fused_computation.19 | convolution fusion | flops 805830656 | bytes 8388672 | tf_op jit(solution)/shard_map/sta,tab->stb/dot_general | solution.py:47
  9.3 2.5 fusion.25
  11.8 1.2 copy.35
  13.0 68.8 %all_to_all.35 = f32[64,64,128]{2,1,0:T(8,128)S(1)} all-to-all(f32[64,64,128]{2,1,0:T(8,128)S(1)} %copy.35), channel_id=1, replica_groups=mesh['row_hi'=8,'row_lo'=8,'col'=8] {'row_hi','row_lo'}, dimensions={0} | all-to-all | bytes 4194304 | tf_op jit(solution)/shard_map/all_to_all | solution.py:53
  81.9 0.6 copy-done.3
  82.7 1.6 broadcast_in_dim.37
  84.3 9.1 %all-to-all-start.1 = ((f32[64,64,128]{2,1,0:T(8,128)}), f32[64,64,128]{2,1,0:T(8,128)S(1)}, u32[]{:S(2)}, u32[]{:S(2)}) async-start(f32[64,64,128]{2,1,0:T(8,128)} %broadcast_in_dim.37), calls=%async_computation.1 | async-start | bytes 4194304 | tf_op jit(solution)/shard_map/all_to_all | solution.py:56
  93.5 51.6 %all-to-all-done.1 = f32[64,64,128]{2,1,0:T(8,128)S(1)} async-done(((f32[64,64,128]{2,1,0:T(8,128)}), f32[64,64,128]{2,1,0:T(8,128)S(1)}, u32[]{:S(2)}, u32[]{:S(2)}) %all-to-all-start.1) | async-done | bytes 2097184 | tf_op jit(solution)/shard_map/all_to_all | solution.py:56
  145.1 1.8 convolution_bitcast_fusion
  146.9 0.8 reshape.142
  147.7 4.7 %all-to-all-start.2 = ((f32[8,1,4096]{2,1,0:T(1,128)}), f32[8,1,4096]{2,1,0:T(1,128)S(1)}, u32[]{:S(2)}, u32[]{:S(2)}) async-start(f32[8,1,4096]{2,1,0:T(1,128)} %reshape.142), calls=%async_computation.2 | async-start | bytes 262144 | tf_op jit(solution)/shard_map/all_to_all | solution.py:20
  152.4 4.7 %all-to-all-done.2 = f32[8,1,4096]{2,1,0:T(1,128)S(1)} async-done(((f32[8,1,4096]{2,1,0:T(1,128)}), f32[8,1,4096]{2,1,0:T(1,128)S(1)}, u32[]{:S(2)}, u32[]{:S(2)}) %all-to-all-start.2) | async-done | bytes 131104 | tf_op jit(solution)/shard_map/all_to_all | solution.py:20
  157.1 0.5 broadcast.135
  157.6 1.0 reduce.4
  158.8 5.8 %cholesky.44 = f32[64,64]{1,0:T(8,128)S(1)} custom-call(f32[64,64]{1,0:T(8,128)S(1)} %fusion.40), custom_call_target="Cholesky" | custom-call | tf_op jit(solution)/shard_map/jit(cholesky)/cholesky | solution.py:58
  164.7 0.6 compare_reduce_fusion.1
  165.4 0.7 select_bitcast_fusion.1
  166.0 4.9 %custom-call.8 = f32[1,64,64]{1,2,0:T(8,128)S(1)} custom-call(f32[1,64,64]{2,1,0:T(8,128)S(1)} %get-tuple-element.7), custom_call_target="InvertDiagBlocksLowerTriangular" | custom-call | tf_op jit(solution)/shard_map/triangular_solve | solution.py:12
  170.9 1.9 fusion.4
  172.9 1.3 copy-done.1
  174.2 0.3 copy_bitcast_fusion
  174.5 2.0 gather_fusion.1
  176.5 10.1 %fusion.20 = f32[64,64,128]{2,0,1:T(8,128)S(1)} fusion(f32[1,1,64,128,128]{4,3,2,1,0:T(8,128)} %param.8, f32[64,64,128]{2,1,0:T(8,128)} %gather_fusion.1, pred[64]{0:T(512)(128)(4,1)S(1)} %compare_and_fusion.1), kind=kOutput, calls=%fused_computation.20 | convolution fusion | flops 805830656 | bytes 8388672 | tf_op jit(solution)/shard_map/stb,tab->sta/dot_general | solution.py:66
  186.6 2.0 fusion.28
  188.6 0.4 reshape.141
  189.0 1.0 copy.44
  190.0 4.9 %all-to-all-start.3 = ((f32[8,64,256]{2,1,0:T(8,128)}), f32[8,64,256]{2,1,0:T(8,128)S(1)}, u32[]{:S(2)}, u32[]{:S(2)}) async-start(f32[8,64,256]{2,1,0:T(8,128)} %copy.44), calls=%async_computation.3 | async-start | bytes 1048576 | tf_op jit(solution)/shard_map/all_to_all | solution.py:70
  194.8 8.9 %all-to-all-done.3 = f32[8,64,256]{2,1,0:T(8,128)S(1)} async-done(((f32[8,64,256]{2,1,0:T(8,128)}), f32[8,64,256]{2,1,0:T(8,128)S(1)}, u32[]{:S(2)}, u32[]{:S(2)}) %all-to-all-start.3) | async-done | bytes 524320 | tf_op jit(solution)/shard_map/all_to_all | solution.py:70
  203.8 0.3 convolution_subtract_fusion
  204.1 0.2 fusion.58
  204.5 8.5 %all_to_all.36 = f32[8,1,4096]{2,1,0:T(1,128)S(1)} all-to-all(f32[8,1,4096]{2,1,0:T(1,128)S(1)} %reshape.144), channel_id=1, replica_groups=mesh['row_hi'=8,'row_lo'=8,'col'=8] {'col'}, dimensions={0} | all-to-all | bytes 262144 | tf_op jit(solution)/shard_map/all_to_all | solution.py:20
  213.0 1.0 reduce.5
  214.3 12.7 %all_to_all.37 = f32[8,1,4096]{2,1,0:T(1,128)S(1)} all-to-all(f32[8,1,4096]{2,1,0:T(1,128)S(1)} %reshape.146), channel_id=1, replica_groups=mesh['row_hi'=8,'row_lo'=8,'col'=8] {'row_lo'}, dimensions={0} | all-to-all | bytes 262144 | tf_op jit(solution)/shard_map/all_to_all | solution.py:20
  227.0 1.0 reduce.6
  228.1 0.8 reshape.148
  228.9 3.9 %all-to-all-start.6 = ((f32[8,1,4096]{2,1,0:T(1,128)}), f32[8,1,4096]{2,1,0:T(1,128)S(1)}, u32[]{:S(2)}, u32[]{:S(2)}) async-start(f32[8,1,4096]{2,1,0:T(1,128)} %reshape.148), calls=%async_computation.6 | async-start | bytes 262144 | tf_op jit(solution)/shard_map/all_to_all | solution.py:20
  232.8 1.4 constant_dynamic-slice_fusion
  234.2 7.7 %all-to-all-done.6 = f32[8,1,4096]{2,1,0:T(1,128)S(1)} async-done(((f32[8,1,4096]{2,1,0:T(1,128)}), f32[8,1,4096]{2,1,0:T(1,128)S(1)}, u32[]{:S(2)}, u32[]{:S(2)}) %all-to-all-start.6) | async-done | bytes 131104 | tf_op jit(solution)/shard_map/all_to_all | solution.py:20
  241.9 1.0 reduce.7
  243.2 5.8 %cholesky.55 = f32[64,64]{1,0:T(8,128)S(1)} custom-call(f32[64,64]{1,0:T(8,128)S(1)} %fusion.38), custom_call_target="Cholesky" | custom-call | tf_op jit(solution)/shard_map/jit(cholesky)/cholesky | solution.py:75
  249.0 0.6 compare_reduce_fusion
  249.7 1.3 select_bitcast_fusion
  251.0 4.9 %custom-call.9 = f32[1,64,64]{1,2,0:T(8,128)S(1)} custom-call(f32[1,64,64]{2,1,0:T(8,128)S(1)} %get-tuple-element.5), custom_call_target="InvertDiagBlocksLowerTriangular" | custom-call | tf_op jit(solution)/shard_map/triangular_solve | solution.py:12
  255.8 0.9 fusion.36
  (44 shorter events, 1.8 us)
Async XLA Ops:
  0.6 2.2 copy-start
  3.6 5.7 %copy-start.5 = (s32[1,1,64]{2,1,0:T(1,128)S(1)}, s32[1,1,64]{2,1,0:T(1,128)}, u32[]{:S(2)}) copy-start(s32[1,1,64]{2,1,0:T(1,128)} %param.10) | copy-start | bytes 772
  81.8 0.8 copy-start.3
  81.8 0.8 copy-start.4
  84.3 60.7 %all-to-all-start.1 = ((f32[64,64,128]{2,1,0:T(8,128)}), f32[64,64,128]{2,1,0:T(8,128)S(1)}, u32[]{:S(2)}, u32[]{:S(2)}) async-start(f32[64,64,128]{2,1,0:T(8,128)} %broadcast_in_dim.37), calls=%async_computation.1 | async-start | bytes 4194304 | tf_op jit(solution)/shard_map/all_to_all | solution.py:56
  147.7 9.4 %all-to-all-start.2 = ((f32[8,1,4096]{2,1,0:T(1,128)}), f32[8,1,4096]{2,1,0:T(1,128)S(1)}, u32[]{:S(2)}, u32[]{:S(2)}) async-start(f32[8,1,4096]{2,1,0:T(1,128)} %reshape.142), calls=%async_computation.2 | async-start | bytes 262144 | tf_op jit(solution)/shard_map/all_to_all | solution.py:20
  166.0 37.8 %copy-start.2 = (f32[64,64]{1,0:T(8,128)}, f32[64,64]{1,0:T(8,128)S(1)}, u32[]{:S(2)}) copy-start(f32[64,64]{1,0:T(8,128)S(1)} %get-tuple-element.8) | copy-start | bytes 49156
  172.9 1.4 copy-start.1
  176.5 10.1 %copy-start.6 = (s32[1,1,64]{2,1,0:T(1,128)S(1)}, s32[1,1,64]{2,1,0:T(1,128)}, u32[]{:S(2)}) copy-start(s32[1,1,64]{2,1,0:T(1,128)} %param.9) | copy-start | bytes 772
  190.0 13.8 %all-to-all-start.3 = ((f32[8,64,256]{2,1,0:T(8,128)}), f32[8,64,256]{2,1,0:T(8,128)S(1)}, u32[]{:S(2)}, u32[]{:S(2)}) async-start(f32[8,64,256]{2,1,0:T(8,128)} %copy.44), calls=%async_computation.3 | async-start | bytes 1048576 | tf_op jit(solution)/shard_map/all_to_all | solution.py:70
  228.9 12.9 %all-to-all-start.6 = ((f32[8,1,4096]{2,1,0:T(1,128)}), f32[8,1,4096]{2,1,0:T(1,128)S(1)}, u32[]{:S(2)}, u32[]{:S(2)}) async-start(f32[8,1,4096]{2,1,0:T(1,128)} %reshape.148), calls=%async_computation.6 | async-start | bytes 262144 | tf_op jit(solution)/shard_map/all_to_all | solution.py:20

commit v3 on v2

--- a/solution.py
+++ b/solution.py
@@ -6,6 +6,7 @@
 from jax.sharding import PartitionSpec as P
 
 HIGH = lax.Precision.HIGHEST
+FAST = lax.Precision.HIGH
 
 
 def lower_solve(factor, rhs):
@@ -44,8 +45,8 @@
         jnp.float32
     )
     picked = jnp.take(u_basis.reshape(width, rows_tiles, tl), rows_here, axis=1)
-    prod = jnp.einsum("sta,tab->stb", picked, local_tiles, precision=HIGH)
-    partial = jnp.einsum("stb,tc->csb", prod, col_hits, precision=HIGH).reshape(
+    prod = jnp.einsum("sta,tab->stb", picked, local_tiles, precision=FAST)
+    partial = jnp.einsum("stb,tc->csb", prod, col_hits, precision=FAST).reshape(
         n_row, v_piece // tl, width, tl
     )
     partial = (partial * col_scale.reshape(n_row, v_piece // tl, 1, tl)).transpose(0, 2, 1, 3)
@@ -63,8 +64,8 @@
     factor = math.sqrt(total_rows / total_cols)
     scaled = (v_column * col_scale).reshape(width, cols_tiles, tl)
     chosen = jnp.take(scaled, cols_here, axis=1)
-    products = jnp.einsum("stb,tab->sta", chosen, local_tiles, precision=HIGH)
-    terms = factor * jnp.einsum("sta,tr->rsa", products, row_hits, precision=HIGH)
+    products = jnp.einsum("stb,tab->sta", chosen, local_tiles, precision=FAST)
+    terms = factor * jnp.einsum("sta,tr->rsa", products, row_hits, precision=FAST)
     terms = terms.reshape(n_col, u_piece // tl, width, tl).transpose(0, 2, 1, 3)
     terms = terms.reshape(n_col, width, u_piece)
     summed = lax.all_to_all(terms, "col", 0, 0, tiled=True).sum(0)

time: 258 us -> 251 us (0.973)
  matrix products: 25.5 us -> 19.5 us
    dot_general x4, matrix products: 20.2 us -> 14.3 us  [the longest x1 7.02 us: per_device(): products = jnp.einsum('stb,tab->sta', chosen, local_tiles, precision=FAST)]
where the time goes in v3:
time: 251 us; the launch traced here: 250 us
  blocking collectives  90.5 us (36%)
  waiting for transfers between devices  71.8 us (29%)
  other arithmetic  31.4 us (13%)
  starting transfers between devices  22.7 us (9%)
  matrix products  19.5 us (8%)
  local copies, waits for them, and re-layouts  13.6 us (5%)
    all_to_all x1, blocking collectives, per_device(): received = lax.all_to_all(partial, ROW, 0, 0, tiled=True)  68.8 us
    all_to_all x1, waiting for transfers between devices, per_device(): column = lax.all_to_all(spread, ROW, 0, 0, tiled=True)  50.5 us
    all_to_all x2, blocking collectives, gather_sum(): lax.all_to_all(jnp.broadcast_to(x[None], (n,) + x.shape), axis, 0, 0, til...  21.7 us
    all_to_all x2, waiting for transfers between devices, gather_sum(): lax.all_to_all(jnp.broadcast_to(x[None], (n,) + x.shape), axis, 0, 0, til...  12.4 us
    another operation x4, other arithmetic, lower_solve(): return lax.linalg.triangular_solve(factor, rhs, left_side=True, lower=True)  11.7 us
    all_to_all x1, starting transfers between devices, per_device(): column = lax.all_to_all(spread, ROW, 0, 0, tiled=True)  9.44 us
    all_to_all x1, waiting for transfers between devices, per_device(): summed = lax.all_to_all(terms, 'col', 0, 0, tiled=True).sum(0)  8.92 us
    all_to_all x2, starting transfers between devices, gather_sum(): lax.all_to_all(jnp.broadcast_to(x[None], (n,) + x.shape), axis, 0, 0, til...  8.4 us
  transfers between devices with their start and end apart: 4, of which 4 were waited for; matrix products, arithmetic and copies ran while one was open for 1% of the time, Pallas kernels for 0%

profile of v3, /device:TPU:2, one launch (start us, length us, event | category | flops | bytes accessed | tf_op | source)
XLA Modules:
  0.0 250.4 jit_solution(11848745284343654054)
XLA Ops:
  0.6 0.7 compare_and_fusion
  1.4 0.7 fusion.51
  2.0 0.8 multiply_exponential_fusion
  2.9 0.7 gather_fusion
  3.6 3.7 %fusion.15 = f32[64,64,128]{2,0,1:T(8,128)S(1)} fusion(f32[1,1,64,128,128]{4,3,2,1,0:T(8,128)} %param.8, f32[64,64,128]{2,1,0:T(8,128)S(1)} %gather_fusion, pred[64]{0:T(512)(128)(4,1)S(1)} %compare_and_fusion), kind=kOutput, calls=%fused_computation.19 | convolution fusion | flops 403177472 | bytes 8388672 | tf_op jit(solution)/shard_map/sta,tab->stb/dot_general | solution.py:48
  7.3 2.0 fusion.25
  9.3 1.2 copy.35
  10.5 68.8 %all_to_all.35 = f32[64,64,128]{2,1,0:T(8,128)S(1)} all-to-all(f32[64,64,128]{2,1,0:T(8,128)S(1)} %copy.35), channel_id=1, replica_groups=mesh['row_hi'=8,'row_lo'=8,'col'=8] {'row_hi','row_lo'}, dimensions={0} | all-to-all | bytes 4194304 | tf_op jit(solution)/shard_map/all_to_all | solution.py:54
  79.4 0.6 copy-done.3
  80.2 1.6 broadcast_in_dim.37
  81.8 9.4 %all-to-all-start.1 = ((f32[64,64,128]{2,1,0:T(8,128)}), f32[64,64,128]{2,1,0:T(8,128)S(1)}, u32[]{:S(2)}, u32[]{:S(2)}) async-start(f32[64,64,128]{2,1,0:T(8,128)} %broadcast_in_dim.37), calls=%async_computation.1 | async-start | bytes 4194304 | tf_op jit(solution)/shard_map/all_to_all | solution.py:57
  91.3 50.5 %all-to-all-done.1 = f32[64,64,128]{2,1,0:T(8,128)S(1)} async-done(((f32[64,64,128]{2,1,0:T(8,128)}), f32[64,64,128]{2,1,0:T(8,128)S(1)}, u32[]{:S(2)}, u32[]{:S(2)}) %all-to-all-start.1) | async-done | bytes 2097184 | tf_op jit(solution)/shard_map/all_to_all | solution.py:57
  141.7 1.8 convolution_bitcast_fusion
  143.5 0.8 reshape.142
  144.4 4.8 %all-to-all-start.2 = ((f32[8,1,4096]{2,1,0:T(1,128)}), f32[8,1,4096]{2,1,0:T(1,128)S(1)}, u32[]{:S(2)}, u32[]{:S(2)}) async-start(f32[8,1,4096]{2,1,0:T(1,128)} %reshape.142), calls=%async_computation.2 | async-start | bytes 262144 | tf_op jit(solution)/shard_map/all_to_all | solution.py:21
  149.2 4.7 %all-to-all-done.2 = f32[8,1,4096]{2,1,0:T(1,128)S(1)} async-done(((f32[8,1,4096]{2,1,0:T(1,128)}), f32[8,1,4096]{2,1,0:T(1,128)S(1)}, u32[]{:S(2)}, u32[]{:S(2)}) %all-to-all-start.2) | async-done | bytes 131104 | tf_op jit(solution)/shard_map/all_to_all | solution.py:21
  153.8 0.5 broadcast.135
  154.3 1.0 reduce.4
  155.6 5.8 %cholesky.44 = f32[64,64]{1,0:T(8,128)S(1)} custom-call(f32[64,64]{1,0:T(8,128)S(1)} %fusion.40), custom_call_target="Cholesky" | custom-call | tf_op jit(solution)/shard_map/jit(cholesky)/cholesky | solution.py:59
  161.5 0.6 compare_reduce_fusion.1
  162.2 0.7 select_bitcast_fusion.1
  162.8 4.9 %custom-call.8 = f32[1,64,64]{1,2,0:T(8,128)S(1)} custom-call(f32[1,64,64]{2,1,0:T(8,128)S(1)} %get-tuple-element.7), custom_call_target="InvertDiagBlocksLowerTriangular" | custom-call | tf_op jit(solution)/shard_map/triangular_solve | solution.py:13
  167.7 1.9 fusion.4
  169.7 1.3 copy-done.1
  171.0 0.3 copy_bitcast_fusion
  171.3 2.0 gather_fusion.1
  173.3 7.0 %fusion.20 = f32[64,64,128]{2,0,1:T(8,128)S(1)} fusion(f32[1,1,64,128,128]{4,3,2,1,0:T(8,128)} %param.8, f32[64,64,128]{2,1,0:T(8,128)} %gather_fusion.1, pred[64]{0:T(512)(128)(4,1)S(1)} %compare_and_fusion.1), kind=kOutput, calls=%fused_computation.20 | convolution fusion | flops 403177472 | bytes 8388672 | tf_op jit(solution)/shard_map/stb,tab->sta/dot_general | solution.py:67
  180.3 1.6 fusion.28
  181.9 0.4 reshape.141
  182.4 1.0 copy.44
  183.3 4.9 %all-to-all-start.3 = ((f32[8,64,256]{2,1,0:T(8,128)}), f32[8,64,256]{2,1,0:T(8,128)S(1)}, u32[]{:S(2)}, u32[]{:S(2)}) async-start(f32[8,64,256]{2,1,0:T(8,128)} %copy.44), calls=%async_computation.3 | async-start | bytes 1048576 | tf_op jit(solution)/shard_map/all_to_all | solution.py:71
  188.2 8.9 %all-to-all-done.3 = f32[8,64,256]{2,1,0:T(8,128)S(1)} async-done(((f32[8,64,256]{2,1,0:T(8,128)}), f32[8,64,256]{2,1,0:T(8,128)S(1)}, u32[]{:S(2)}, u32[]{:S(2)}) %all-to-all-start.3) | async-done | bytes 524320 | tf_op jit(solution)/shard_map/all_to_all | solution.py:71
  197.2 0.3 convolution_subtract_fusion
  197.4 0.2 fusion.58
  197.8 8.5 %all_to_all.36 = f32[8,1,4096]{2,1,0:T(1,128)S(1)} all-to-all(f32[8,1,4096]{2,1,0:T(1,128)S(1)} %reshape.144), channel_id=1, replica_groups=mesh['row_hi'=8,'row_lo'=8,'col'=8] {'col'}, dimensions={0} | all-to-all | bytes 262144 | tf_op jit(solution)/shard_map/all_to_all | solution.py:21
  206.4 1.0 reduce.5
  207.7 13.2 %all_to_all.37 = f32[8,1,4096]{2,1,0:T(1,128)S(1)} all-to-all(f32[8,1,4096]{2,1,0:T(1,128)S(1)} %reshape.146), channel_id=1, replica_groups=mesh['row_hi'=8,'row_lo'=8,'col'=8] {'row_lo'}, dimensions={0} | all-to-all | bytes 262144 | tf_op jit(solution)/shard_map/all_to_all | solution.py:21
  220.8 1.0 reduce.6
  222.0 0.8 reshape.148
  222.8 3.6 %all-to-all-start.6 = ((f32[8,1,4096]{2,1,0:T(1,128)}), f32[8,1,4096]{2,1,0:T(1,128)S(1)}, u32[]{:S(2)}, u32[]{:S(2)}) async-start(f32[8,1,4096]{2,1,0:T(1,128)} %reshape.148), calls=%async_computation.6 | async-start | bytes 262144 | tf_op jit(solution)/shard_map/all_to_all | solution.py:21
  226.4 1.4 constant_dynamic-slice_fusion
  227.8 7.7 %all-to-all-done.6 = f32[8,1,4096]{2,1,0:T(1,128)S(1)} async-done(((f32[8,1,4096]{2,1,0:T(1,128)}), f32[8,1,4096]{2,1,0:T(1,128)S(1)}, u32[]{:S(2)}, u32[]{:S(2)}) %all-to-all-start.6) | async-done | bytes 131104 | tf_op jit(solution)/shard_map/all_to_all | solution.py:21
  235.5 1.0 reduce.7
  236.8 5.8 %cholesky.55 = f32[64,64]{1,0:T(8,128)S(1)} custom-call(f32[64,64]{1,0:T(8,128)S(1)} %fusion.38), custom_call_target="Cholesky" | custom-call | tf_op jit(solution)/shard_map/jit(cholesky)/cholesky | solution.py:76
  242.7 0.6 compare_reduce_fusion
  243.3 1.3 select_bitcast_fusion
  244.6 4.9 %custom-call.9 = f32[1,64,64]{1,2,0:T(8,128)S(1)} custom-call(f32[1,64,64]{2,1,0:T(8,128)S(1)} %get-tuple-element.5), custom_call_target="InvertDiagBlocksLowerTriangular" | custom-call | tf_op jit(solution)/shard_map/triangular_solve | solution.py:13
  249.5 0.9 fusion.36
  (44 shorter events, 1.8 us)
Async XLA Ops:
  0.6 2.2 copy-start
  3.6 3.7 %copy-start.5 = (s32[1,1,64]{2,1,0:T(1,128)S(1)}, s32[1,1,64]{2,1,0:T(1,128)}, u32[]{:S(2)}) copy-start(s32[1,1,64]{2,1,0:T(1,128)} %param.10) | copy-start | bytes 772
  79.3 0.8 copy-start.3
  79.3 0.8 copy-start.4
  81.8 59.9 %all-to-all-start.1 = ((f32[64,64,128]{2,1,0:T(8,128)}), f32[64,64,128]{2,1,0:T(8,128)S(1)}, u32[]{:S(2)}, u32[]{:S(2)}) async-start(f32[64,64,128]{2,1,0:T(8,128)} %broadcast_in_dim.37), calls=%async_computation.1 | async-start | bytes 4194304 | tf_op jit(solution)/shard_map/all_to_all | solution.py:57
  144.4 9.5 %all-to-all-start.2 = ((f32[8,1,4096]{2,1,0:T(1,128)}), f32[8,1,4096]{2,1,0:T(1,128)S(1)}, u32[]{:S(2)}, u32[]{:S(2)}) async-start(f32[8,1,4096]{2,1,0:T(1,128)} %reshape.142), calls=%async_computation.2 | async-start | bytes 262144 | tf_op jit(solution)/shard_map/all_to_all | solution.py:21
  162.8 34.3 %copy-start.2 = (f32[64,64]{1,0:T(8,128)}, f32[64,64]{1,0:T(8,128)S(1)}, u32[]{:S(2)}) copy-start(f32[64,64]{1,0:T(8,128)S(1)} %get-tuple-element.8) | copy-start | bytes 49156
  169.7 1.4 copy-start.1
  173.3 7.0 %copy-start.6 = (s32[1,1,64]{2,1,0:T(1,128)S(1)}, s32[1,1,64]{2,1,0:T(1,128)}, u32[]{:S(2)}) copy-start(s32[1,1,64]{2,1,0:T(1,128)} %param.9) | copy-start | bytes 772
  183.3 13.8 %all-to-all-start.3 = ((f32[8,64,256]{2,1,0:T(8,128)}), f32[8,64,256]{2,1,0:T(8,128)S(1)}, u32[]{:S(2)}, u32[]{:S(2)}) async-start(f32[8,64,256]{2,1,0:T(8,128)} %copy.44), calls=%async_computation.3 | async-start | bytes 1048576 | tf_op jit(solution)/shard_map/all_to_all | solution.py:71
  222.8 12.7 %all-to-all-start.6 = ((f32[8,1,4096]{2,1,0:T(1,128)}), f32[8,1,4096]{2,1,0:T(1,128)S(1)}, u32[]{:S(2)}, u32[]{:S(2)}) async-start(f32[8,1,4096]{2,1,0:T(1,128)} %reshape.148), calls=%async_computation.6 | async-start | bytes 262144 | tf_op jit(solution)/shard_map/all_to_all | solution.py:21

commit v4 on v3

--- a/solution.py
+++ b/solution.py
@@ -57,20 +57,17 @@
     column = lax.all_to_all(spread, ROW, 0, 0, tiled=True)
     gram = gather_sum(jnp.einsum("jsb,jtb->st", column, column, precision=HIGH), "col")
     v_factor = jnp.linalg.cholesky(gram / total_cols)
-    pt_column = column.transpose(1, 0, 2).reshape(width, block_cols)
-    v_column = lower_solve(v_factor, pt_column)
-    offset = lax.axis_index(ROW) * v_piece
-    v_next = lax.dynamic_slice_in_dim(v_column, offset, v_piece, 1)
+    v_next = lower_solve(v_factor, pt_piece)
     factor = math.sqrt(total_rows / total_cols)
-    scaled = (v_column * col_scale).reshape(width, cols_tiles, tl)
-    chosen = jnp.take(scaled, cols_here, axis=1)
+    scaled = column.transpose(1, 0, 2).reshape(width, block_cols) * col_scale
+    chosen = jnp.take(scaled.reshape(width, cols_tiles, tl), cols_here, axis=1)
     products = jnp.einsum("stb,tab->sta", chosen, local_tiles, precision=FAST)
-    terms = factor * jnp.einsum("sta,tr->rsa", products, row_hits, precision=FAST)
+    terms = jnp.einsum("sta,tr->rsa", products, row_hits, precision=FAST)
     terms = terms.reshape(n_col, u_piece // tl, width, tl).transpose(0, 2, 1, 3)
     terms = terms.reshape(n_col, width, u_piece)
     summed = lax.all_to_all(terms, "col", 0, 0, tiled=True).sum(0)
     u_own = lax.dynamic_slice_in_dim(u_basis, lax.axis_index("col") * u_piece, u_piece, 1)
-    qt_piece = summed - jnp.dot(v_factor.T, u_own, precision=HIGH)
+    qt_piece = factor * lower_solve(v_factor, summed) - jnp.dot(v_factor.T, u_own, precision=HIGH)
     ugram = jnp.dot(qt_piece, qt_piece.T, precision=HIGH)
     ugram = gather_sum(gather_sum(gather_sum(ugram, "col"), "row_lo"), "row_hi")
     u_factor = jnp.linalg.cholesky(ugram / total_rows)

time: 251 us -> 238 us (0.948)
  waiting for transfers between devices: 71.8 us -> 58.7 us
    all_to_all x1, waiting for transfers between devices: 8.92 us -> 0.01 us  [per_device(): summed = lax.all_to_all(terms, 'col', 0, 0, tiled=True).sum(0)]
    all_to_all x2, waiting for transfers between devices: 12.4 us -> 8.23 us  [gather_sum(): lax.all_to_all(jnp.broadcast_to(x[None], (n,) + x.shape), axis, 0, 0, til...]
    mul x0 -> x1, local copies, waits for them, and re-layouts: none -> 2.57 us  [per_device(): scaled = column.transpose(1, 0, 2).reshape(width, block_cols) * col_scale]
  transfers between devices with their start and end apart: 4 -> 4, of which waited for: 4 -> 2; matrix products, arithmetic and copies ran while one was open for 1% -> 11% of each run, Pallas kernels for 0% -> 0%
where the time goes in v4:
time: 238 us; the launch traced here: 237 us
  blocking collectives  91.2 us (38%)
  waiting for transfers between devices  58.7 us (25%)
  other arithmetic  32.3 us (14%)
  starting transfers between devices  22.7 us (10%)
  matrix products  17.5 us (7%)
  local copies, waits for them, and re-layouts  13.7 us (6%)
    all_to_all x1, blocking collectives, per_device(): received = lax.all_to_all(partial, ROW, 0, 0, tiled=True)  68.8 us
    all_to_all x1, waiting for transfers between devices, per_device(): column = lax.all_to_all(spread, ROW, 0, 0, tiled=True)  50.4 us
    all_to_all x2, blocking collectives, gather_sum(): lax.all_to_all(jnp.broadcast_to(x[None], (n,) + x.shape), axis, 0, 0, til...  22.5 us
    another operation x4, other arithmetic, lower_solve(): return lax.linalg.triangular_solve(factor, rhs, left_side=True, lower=True)  11.7 us
    all_to_all x1, starting transfers between devices, per_device(): column = lax.all_to_all(spread, ROW, 0, 0, tiled=True)  9.44 us
    all_to_all x2, starting transfers between devices, gather_sum(): lax.all_to_all(jnp.broadcast_to(x[None], (n,) + x.shape), axis, 0, 0, til...  8.4 us
    all_to_all x2, waiting for transfers between devices, gather_sum(): lax.all_to_all(jnp.broadcast_to(x[None], (n,) + x.shape), axis, 0, 0, til...  8.23 us
    another operation x3, other arithmetic, per_device(): v_factor = jnp.linalg.cholesky(gram / total_cols)  6.52 us
  transfers between devices with their start and end apart: 4, of which 2 were waited for; matrix products, arithmetic and copies ran while one was open for 11% of the time, Pallas kernels for 0%

profile of v4, /device:TPU:2, one launch (start us, length us, event | category | flops | bytes accessed | tf_op | source)
XLA Modules:
  0.0 237.1 jit_solution(13728089931743617891)
XLA Ops:
  0.6 0.7 compare_and_fusion.1
  1.4 0.7 fusion.53
  2.0 0.8 exponential_bitcast_fusion
  2.9 0.7 gather_fusion
  3.6 3.7 %fusion.13 = f32[64,64,128]{2,0,1:T(8,128)S(1)} fusion(f32[1,1,64,128,128]{4,3,2,1,0:T(8,128)} %param.10, f32[64,64,128]{2,1,0:T(8,128)S(1)} %gather_fusion, pred[64]{0:T(512)(128)(4,1)S(1)} %compare_and_fusion.1), kind=kOutput, calls=%fused_computation.16 | convolution fusion | flops 403177472 | bytes 8388672 | tf_op jit(solution)/shard_map/sta,tab->stb/dot_general | solution.py:48
  7.3 2.0 fusion.23
  9.3 1.2 copy.39
  10.5 68.8 %all_to_all.35 = f32[64,64,128]{2,1,0:T(8,128)S(1)} all-to-all(f32[64,64,128]{2,1,0:T(8,128)S(1)} %copy.39), channel_id=1, replica_groups=mesh['row_hi'=8,'row_lo'=8,'col'=8] {'row_hi','row_lo'}, dimensions={0} | all-to-all | bytes 4194304 | tf_op jit(solution)/shard_map/all_to_all | solution.py:54
  79.4 0.6 copy-done.2
  80.2 1.6 broadcast_in_dim.36
  81.8 9.4 %all-to-all-start.1 = ((f32[64,64,128]{2,1,0:T(8,128)}), f32[64,64,128]{2,1,0:T(8,128)S(1)}, u32[]{:S(2)}, u32[]{:S(2)}) async-start(f32[64,64,128]{2,1,0:T(8,128)} %broadcast_in_dim.36), calls=%async_computation.1 | async-start | bytes 4194304 | tf_op jit(solution)/shard_map/all_to_all | solution.py:57
  91.3 50.4 %all-to-all-done.1 = f32[64,64,128]{2,1,0:T(8,128)S(1)} async-done(((f32[64,64,128]{2,1,0:T(8,128)}), f32[64,64,128]{2,1,0:T(8,128)S(1)}, u32[]{:S(2)}, u32[]{:S(2)}) %all-to-all-start.1) | async-done | bytes 2097184 | tf_op jit(solution)/shard_map/all_to_all | solution.py:57
  141.7 1.2 fusion.8
  143.0 2.6 %copy.43 = f32[64,64,128]{2,0,1:T(8,128)} copy(f32[64,64,128]{2,1,0:T(8,128)S(1)} %fusion.8) | data formatting | bytes 4194304 | tf_op jit(solution)/shard_map/mul | solution.py:62
  145.5 1.8 convolution_bitcast_fusion
  147.3 0.8 reshape.150
  148.2 4.8 %all-to-all-start.2 = ((f32[8,1,4096]{2,1,0:T(1,128)}), f32[8,1,4096]{2,1,0:T(1,128)S(1)}, u32[]{:S(2)}, u32[]{:S(2)}) async-start(f32[8,1,4096]{2,1,0:T(1,128)} %reshape.150), calls=%async_computation.2 | async-start | bytes 262144 | tf_op jit(solution)/shard_map/all_to_all | solution.py:21
  153.0 2.3 gather_fusion.1
  155.3 5.9 %fusion.18 = f32[64,64,128]{2,0,1:T(8,128)S(1)} fusion(f32[1,1,64,128,128]{4,3,2,1,0:T(8,128)} %param.10, f32[64,64,128]{2,1,0:T(8,128)S(1)} %gather_fusion.1, pred[64]{0:T(512)(128)(4,1)S(1)} %compare_and_fusion), kind=kOutput, calls=%fused_computation.17 | convolution fusion | flops 403177472 | bytes 8388672 | tf_op jit(solution)/shard_map/stb,tab->sta/dot_general | solution.py:64
  161.1 1.6 fusion.6
  162.7 0.4 reshape.149
  163.2 1.0 copy.48
  164.1 4.8 %all-to-all-start.3 = ((f32[8,64,256]{2,1,0:T(8,128)}), f32[8,64,256]{2,1,0:T(8,128)S(1)}, u32[]{:S(2)}, u32[]{:S(2)}) async-start(f32[8,64,256]{2,1,0:T(8,128)} %copy.48), calls=%async_computation.3 | async-start | bytes 1048576 | tf_op jit(solution)/shard_map/all_to_all | solution.py:68
  168.9 0.5 broadcast.136
  169.4 1.0 reduce.4
  170.7 5.8 %cholesky.44 = f32[64,64]{1,0:T(8,128)S(1)} custom-call(f32[64,64]{1,0:T(8,128)S(1)} %fusion.37), custom_call_target="Cholesky" | custom-call | tf_op jit(solution)/shard_map/jit(cholesky)/cholesky | solution.py:59
  176.6 0.6 compare_reduce_fusion.1
  177.2 0.7 fusion.42
  177.9 4.9 %custom-call.10 = f32[1,64,64]{1,2,0:T(8,128)S(1)} custom-call(f32[1,64,64]{2,1,0:T(8,128)S(1)} %get-tuple-element.8), custom_call_target="InvertDiagBlocksLowerTriangular" | custom-call | tf_op jit(solution)/shard_map/triangular_solve/custom-call.0 | solution.py:13
  182.9 0.3 convolution_multiply_fusion
  183.1 0.3 convolution_subtract_fusion
  183.4 0.2 fusion.61
  183.6 0.2 reshape.152
  183.8 9.3 %all_to_all.36 = f32[8,1,4096]{2,1,0:T(1,128)S(1)} all-to-all(f32[8,1,4096]{2,1,0:T(1,128)S(1)} %reshape.152), channel_id=1, replica_groups=mesh['row_hi'=8,'row_lo'=8,'col'=8] {'col'}, dimensions={0} | all-to-all | bytes 262144 | tf_op jit(solution)/shard_map/all_to_all | solution.py:21
  193.1 1.0 reduce.5
  194.2 0.2 reshape.154
  194.4 13.2 %all_to_all.37 = f32[8,1,4096]{2,1,0:T(1,128)S(1)} all-to-all(f32[8,1,4096]{2,1,0:T(1,128)S(1)} %reshape.154), channel_id=1, replica_groups=mesh['row_hi'=8,'row_lo'=8,'col'=8] {'row_lo'}, dimensions={0} | all-to-all | bytes 262144 | tf_op jit(solution)/shard_map/all_to_all | solution.py:21
  207.6 1.0 reduce.6
  208.7 0.8 reshape.156
  209.5 3.6 %all-to-all-start.6 = ((f32[8,1,4096]{2,1,0:T(1,128)}), f32[8,1,4096]{2,1,0:T(1,128)S(1)}, u32[]{:S(2)}, u32[]{:S(2)}) async-start(f32[8,1,4096]{2,1,0:T(1,128)} %reshape.156), calls=%async_computation.6 | async-start | bytes 262144 | tf_op jit(solution)/shard_map/all_to_all | solution.py:21
  213.2 0.9 fusion.34
  214.0 8.2 %all-to-all-done.6 = f32[8,1,4096]{2,1,0:T(1,128)S(1)} async-done(((f32[8,1,4096]{2,1,0:T(1,128)}), f32[8,1,4096]{2,1,0:T(1,128)S(1)}, u32[]{:S(2)}, u32[]{:S(2)}) %all-to-all-start.6) | async-done | bytes 131104 | tf_op jit(solution)/shard_map/all_to_all | solution.py:21
  222.2 1.0 reduce.7
  223.5 5.8 %cholesky.55 = f32[64,64]{1,0:T(8,128)S(1)} custom-call(f32[64,64]{1,0:T(8,128)S(1)} %fusion.33), custom_call_target="Cholesky" | custom-call | tf_op jit(solution)/shard_map/jit(cholesky)/cholesky | solution.py:73
  229.4 0.6 compare_reduce_fusion
  230.0 1.3 select_bitcast_fusion
  231.3 4.9 %custom-call.11 = f32[1,64,64]{1,2,0:T(8,128)S(1)} custom-call(f32[1,64,64]{2,1,0:T(8,128)S(1)} %get-tuple-element.6), custom_call_target="InvertDiagBlocksLowerTriangular" | custom-call | tf_op jit(solution)/shard_map/triangular_solve/custom-call.0 | solution.py:13
  236.2 0.9 fusion.31
  (43 shorter events, 1.5 us)
Async XLA Ops:
  0.6 2.2 copy-start
  3.6 3.7 %copy-start.4 = (s32[1,1,64]{2,1,0:T(1,128)S(1)}, s32[1,1,64]{2,1,0:T(1,128)}, u32[]{:S(2)}) copy-start(s32[1,1,64]{2,1,0:T(1,128)} %param.12) | copy-start | bytes 772
  79.3 0.8 copy-start.2
  79.3 0.8 copy-start.3
  81.8 59.9 %all-to-all-start.1 = ((f32[64,64,128]{2,1,0:T(8,128)}), f32[64,64,128]{2,1,0:T(8,128)S(1)}, u32[]{:S(2)}, u32[]{:S(2)}) async-start(f32[64,64,128]{2,1,0:T(8,128)} %broadcast_in_dim.36), calls=%async_computation.1 | async-start | bytes 4194304 | tf_op jit(solution)/shard_map/all_to_all | solution.py:57
  148.2 15.9 %all-to-all-start.2 = ((f32[8,1,4096]{2,1,0:T(1,128)}), f32[8,1,4096]{2,1,0:T(1,128)S(1)}, u32[]{:S(2)}, u32[]{:S(2)}) async-start(f32[8,1,4096]{2,1,0:T(1,128)} %reshape.150), calls=%async_computation.2 | async-start | bytes 262144 | tf_op jit(solution)/shard_map/all_to_all | solution.py:21
  155.2 5.9 %copy-start.5 = (s32[1,1,64]{2,1,0:T(1,128)S(1)}, s32[1,1,64]{2,1,0:T(1,128)}, u32[]{:S(2)}) copy-start(s32[1,1,64]{2,1,0:T(1,128)} %param.11) | copy-start | bytes 772
  164.1 18.7 %all-to-all-start.3 = ((f32[8,64,256]{2,1,0:T(8,128)}), f32[8,64,256]{2,1,0:T(8,128)S(1)}, u32[]{:S(2)}, u32[]{:S(2)}) async-start(f32[8,64,256]{2,1,0:T(8,128)} %copy.48), calls=%async_computation.3 | async-start | bytes 1048576 | tf_op jit(solution)/shard_map/all_to_all | solution.py:68
  177.9 30.7 %copy-start.1 = (f32[64,64]{1,0:T(8,128)}, f32[64,64]{1,0:T(8,128)S(1)}, u32[]{:S(2)}) copy-start(f32[64,64]{1,0:T(8,128)S(1)} %get-tuple-element.9) | copy-start | bytes 49156
  209.5 12.7 %all-to-all-start.6 = ((f32[8,1,4096]{2,1,0:T(1,128)}), f32[8,1,4096]{2,1,0:T(1,128)S(1)}, u32[]{:S(2)}, u32[]{:S(2)}) async-start(f32[8,1,4096]{2,1,0:T(1,128)} %reshape.156), calls=%async_computation.6 | async-start | bytes 262144 | tf_op jit(solution)/shard_map/all_to_all | solution.py:21

commit v5 on v4

--- a/solution.py
+++ b/solution.py
@@ -3,14 +3,47 @@
 import jax
 import jax.numpy as jnp
 from jax import lax
+from jax.experimental import pallas as pl
+from jax.experimental.pallas import tpu as pltpu
 from jax.sharding import PartitionSpec as P
 
 HIGH = lax.Precision.HIGHEST
 FAST = lax.Precision.HIGH
 
 
-def lower_solve(factor, rhs):
-    return lax.linalg.triangular_solve(factor, rhs, left_side=True, lower=True)
+def _factor_kernel(aug_ref, low_ref, inv_ref, work_ref):
+    n = aug_ref.shape[0]
+    work_ref[...] = aug_ref[...]
+    lane = lax.broadcasted_iota(jnp.int32, aug_ref.shape, 1)
+    sub = lax.broadcasted_iota(jnp.int32, (n, 1), 0)
+    lane_row = lax.broadcasted_iota(jnp.int32, (1, aug_ref.shape[1]), 1)
+
+    def step(j, low):
+        whole = work_ref[...]
+        row = work_ref[pl.ds(j, 1), :]
+        pivot = jnp.sum(jnp.where(lane_row == j, row, 0.0), axis=1, keepdims=True)
+        scale = 1.0 / jnp.sqrt(pivot)
+        scaled_row = row * scale
+        inv_ref[pl.ds(j, 1), :] = scaled_row
+        column = jnp.sum(jnp.where(lane == j, whole, 0.0), axis=1, keepdims=True) * scale
+        work_ref[...] = whole - jnp.where(sub > j, column, 0.0) * scaled_row
+        return jnp.where(lane == j, jnp.where(sub >= j, column, 0.0), low)
+
+    low_ref[...] = lax.fori_loop(0, n, step, jnp.zeros(aug_ref.shape, jnp.float32))
+
+
+def cholesky_and_inverse(gram):
+    n = gram.shape[0]
+    aug = jnp.concatenate([gram, jnp.eye(n, dtype=jnp.float32)], axis=1)
+    low, inv = pl.pallas_call(
+        _factor_kernel,
+        out_shape=(
+            jax.ShapeDtypeStruct(aug.shape, jnp.float32),
+            jax.ShapeDtypeStruct(aug.shape, jnp.float32),
+        ),
+        scratch_shapes=[pltpu.VMEM(aug.shape, jnp.float32)],
+    )(aug)
+    return low[:, :n], inv[:, n:]
 
 
 ROW = ("row_hi", "row_lo")
@@ -56,8 +89,8 @@
     spread = jnp.broadcast_to(pt_piece[None], (n_row, width, v_piece))
     column = lax.all_to_all(spread, ROW, 0, 0, tiled=True)
     gram = gather_sum(jnp.einsum("jsb,jtb->st", column, column, precision=HIGH), "col")
-    v_factor = jnp.linalg.cholesky(gram / total_cols)
-    v_next = lower_solve(v_factor, pt_piece)
+    v_factor, v_inverse = cholesky_and_inverse(gram / total_cols)
+    v_next = jnp.dot(v_inverse, pt_piece, precision=HIGH)
     factor = math.sqrt(total_rows / total_cols)
     scaled = column.transpose(1, 0, 2).reshape(width, block_cols) * col_scale
     chosen = jnp.take(scaled.reshape(width, cols_tiles, tl), cols_here, axis=1)
@@ -67,11 +100,11 @@
     terms = terms.reshape(n_col, width, u_piece)
     summed = lax.all_to_all(terms, "col", 0, 0, tiled=True).sum(0)
     u_own = lax.dynamic_slice_in_dim(u_basis, lax.axis_index("col") * u_piece, u_piece, 1)
-    qt_piece = factor * lower_solve(v_factor, summed) - jnp.dot(v_factor.T, u_own, precision=HIGH)
+    qt_piece = factor * jnp.dot(v_inverse, summed, precision=HIGH) - jnp.dot(v_factor.T, u_own, precision=HIGH)
     ugram = jnp.dot(qt_piece, qt_piece.T, precision=HIGH)
     ugram = gather_sum(gather_sum(gather_sum(ugram, "col"), "row_lo"), "row_hi")
-    u_factor = jnp.linalg.cholesky(ugram / total_rows)
-    u_next = lower_solve(u_factor, qt_piece)
+    u_factor, u_inverse = cholesky_and_inverse(ugram / total_rows)
+    u_next = jnp.dot(u_inverse, qt_piece, precision=HIGH)
     return (u_next, v_next, v_factor, u_factor)
 
 

time: 238 us -> 233 us (0.979)
  other arithmetic: 32.3 us -> 8.89 us
  Pallas kernels: 0 us -> 16.3 us
    another operation x10 -> x0, other arithmetic: 24.8 us -> none  [the longest x4 11.7 us: lower_solve(): return lax.linalg.triangular_solve(factor, rhs, left_side=True, lower=True)]
    pallas_call x0 -> x2, Pallas kernels: none -> 16.3 us  [cholesky_and_inverse(): pl.pallas_call(_factor_kernel, out_shape=(jax.ShapeDtypeStruct(aug.shape,...]
    dot_general x0 -> x3, matrix products: none -> 3.5 us  [the longest x1 1.64 us: per_device(): u_next = jnp.dot(u_inverse, qt_piece, precision=HIGH)]
  transfers between devices with their start and end apart: 4 -> 4, of which waited for: 2 -> 2; matrix products, arithmetic and copies ran while one was open for 11% -> 6% of each run, Pallas kernels for 0% -> 4%
where the time goes in v5:
time: 233 us; the launch traced here: 232 us
  blocking collectives  91.2 us (39%)
  waiting for transfers between devices  58.7 us (25%)
  starting transfers between devices  22.7 us (10%)
  matrix products  19.8 us (8%)
  Pallas kernels  16.3 us (7%)
  local copies, waits for them, and re-layouts  13.4 us (6%)
  other arithmetic  8.89 us (4%)
    all_to_all x1, blocking collectives, per_device(): received = lax.all_to_all(partial, ROW, 0, 0, tiled=True)  68.8 us
    all_to_all x1, waiting for transfers between devices, per_device(): column = lax.all_to_all(spread, ROW, 0, 0, tiled=True)  50.4 us
    all_to_all x2, blocking collectives, gather_sum(): lax.all_to_all(jnp.broadcast_to(x[None], (n,) + x.shape), axis, 0, 0, til...  22.5 us
    pallas_call x2, Pallas kernels, cholesky_and_inverse(): pl.pallas_call(_factor_kernel, out_shape=(jax.ShapeDtypeStruct(aug.shape,...  16.3 us
    all_to_all x1, starting transfers between devices, per_device(): column = lax.all_to_all(spread, ROW, 0, 0, tiled=True)  9.45 us
    all_to_all x2, starting transfers between devices, gather_sum(): lax.all_to_all(jnp.broadcast_to(x[None], (n,) + x.shape), axis, 0, 0, til...  8.4 us
    all_to_all x2, waiting for transfers between devices, gather_sum(): lax.all_to_all(jnp.broadcast_to(x[None], (n,) + x.shape), axis, 0, 0, til...  8.23 us
    dot_general x1, matrix products, per_device(): products = jnp.einsum('stb,tab->sta', chosen, local_tiles, precision=FAST)  5.85 us
  transfers between devices with their start and end apart: 4, of which 2 were waited for; matrix products, arithmetic and copies ran while one was open for 6% of the time, Pallas kernels for 4%

profile of v5, /device:TPU:2, one launch (start us, length us, event | category | flops | bytes accessed | tf_op | source)
XLA Modules:
  0.0 231.9 jit_solution(17774843349665135600)
XLA Ops:
  0.6 0.7 compare_and_fusion.1
  1.4 0.7 fusion.45
  2.0 0.8 exponential_bitcast_fusion
  2.9 0.7 gather_fusion
  3.6 3.7 %fusion.13 = f32[64,64,128]{2,0,1:T(8,128)S(1)} fusion(f32[1,1,64,128,128]{4,3,2,1,0:T(8,128)} %param.7, f32[64,64,128]{2,1,0:T(8,128)S(1)} %gather_fusion, pred[64]{0:T(512)(128)(4,1)S(1)} %compare_and_fusion.1), kind=kOutput, calls=%fused_computation.16 | convolution fusion | flops 403177472 | bytes 8388672 | tf_op jit(solution)/shard_map/sta,tab->stb/dot_general | solution.py:81
  7.3 2.0 fusion.23
  9.3 1.2 copy.31
  10.5 68.8 %all_to_all.35 = f32[64,64,128]{2,1,0:T(8,128)S(1)} all-to-all(f32[64,64,128]{2,1,0:T(8,128)S(1)} %copy.31), channel_id=1, replica_groups=mesh['row_hi'=8,'row_lo'=8,'col'=8] {'row_hi','row_lo'}, dimensions={0} | all-to-all | bytes 4194304 | tf_op jit(solution)/shard_map/all_to_all | solution.py:87
  79.3 0.1 reduce_sum.54
  79.4 0.6 copy-done.2
  80.0 0.2 convolution_subtract_fusion.1
  80.2 1.6 broadcast_in_dim.35
  81.8 9.4 %all-to-all-start.1 = ((f32[64,64,128]{2,1,0:T(8,128)}), f32[64,64,128]{2,1,0:T(8,128)S(1)}, u32[]{:S(2)}, u32[]{:S(2)}) async-start(f32[64,64,128]{2,1,0:T(8,128)} %broadcast_in_dim.35), calls=%async_computation.1 | async-start | bytes 4194304 | tf_op jit(solution)/shard_map/all_to_all | solution.py:90
  91.3 50.4 %all-to-all-done.1 = f32[64,64,128]{2,1,0:T(8,128)S(1)} async-done(((f32[64,64,128]{2,1,0:T(8,128)}), f32[64,64,128]{2,1,0:T(8,128)S(1)}, u32[]{:S(2)}, u32[]{:S(2)}) %all-to-all-start.1) | async-done | bytes 2097184 | tf_op jit(solution)/shard_map/all_to_all | solution.py:90
  141.7 1.2 fusion.8
  143.0 2.6 %copy.33 = f32[64,64,128]{2,0,1:T(8,128)} copy(f32[64,64,128]{2,1,0:T(8,128)S(1)} %fusion.8) | data formatting | bytes 4194304 | tf_op jit(solution)/shard_map/mul | solution.py:95
  145.5 1.8 convolution_bitcast_fusion
  147.3 0.8 reshape.130
  148.2 4.8 %all-to-all-start.2 = ((f32[8,1,4096]{2,1,0:T(1,128)}), f32[8,1,4096]{2,1,0:T(1,128)S(1)}, u32[]{:S(2)}, u32[]{:S(2)}) async-start(f32[8,1,4096]{2,1,0:T(1,128)} %reshape.130), calls=%async_computation.2 | async-start | bytes 262144 | tf_op jit(solution)/shard_map/all_to_all | solution.py:54
  153.0 2.3 gather_fusion.1
  155.3 5.8 %fusion.18 = f32[64,64,128]{2,0,1:T(8,128)S(1)} fusion(f32[1,1,64,128,128]{4,3,2,1,0:T(8,128)} %param.7, f32[64,64,128]{2,1,0:T(8,128)S(1)} %gather_fusion.1, pred[64]{0:T(512)(128)(4,1)S(1)} %compare_and_fusion), kind=kOutput, calls=%fused_computation.17 | convolution fusion | flops 403177472 | bytes 8388672 | tf_op jit(solution)/shard_map/stb,tab->sta/dot_general | solution.py:97
  161.1 1.6 fusion.6
  162.7 0.4 reshape.129
  163.2 1.0 copy.36
  164.1 4.8 %all-to-all-start.3 = ((f32[8,64,256]{2,1,0:T(8,128)}), f32[8,64,256]{2,1,0:T(8,128)S(1)}, u32[]{:S(2)}, u32[]{:S(2)}) async-start(f32[8,64,256]{2,1,0:T(8,128)} %copy.36), calls=%async_computation.3 | async-start | bytes 1048576 | tf_op jit(solution)/shard_map/all_to_all | solution.py:101
  168.9 0.5 broadcast.89
  169.4 1.0 reduce
  170.4 0.1 reshape.131
  170.5 0.7 pad_maximum_fusion.aug_ref
  171.2 8.1 %shard_map.102 = (f32[64,128]{1,0:T(8,128)}, f32[64,128]{1,0:T(8,128)}) custom-call(f32[64,128]{1,0:T(8,128)} %pad_maximum_fusion.aug_ref), custom_call_target="tpu_custom_call" | custom-call | tf_op jit(solution)/shard_map/pallas_call | solution.py:38
  179.4 1.0 convolution_multiply_fusion
  180.4 1.0 convolution_subtract_fusion
  181.5 0.2 fusion.51
  181.7 0.2 reshape.132
  181.9 9.3 %all_to_all.36 = f32[8,1,4096]{2,1,0:T(1,128)S(1)} all-to-all(f32[8,1,4096]{2,1,0:T(1,128)S(1)} %reshape.132), channel_id=1, replica_groups=mesh['row_hi'=8,'row_lo'=8,'col'=8] {'col'}, dimensions={0} | all-to-all | bytes 262144 | tf_op jit(solution)/shard_map/all_to_all | solution.py:54
  191.2 1.0 reduce.1
  192.3 0.2 reshape.134
  192.5 13.2 %all_to_all.37 = f32[8,1,4096]{2,1,0:T(1,128)S(1)} all-to-all(f32[8,1,4096]{2,1,0:T(1,128)S(1)} %reshape.134), channel_id=1, replica_groups=mesh['row_hi'=8,'row_lo'=8,'col'=8] {'row_lo'}, dimensions={0} | all-to-all | bytes 262144 | tf_op jit(solution)/shard_map/all_to_all | solution.py:54
  205.7 1.0 reduce.2
  206.8 0.8 reshape.136
  207.6 3.6 %all-to-all-start.6 = ((f32[8,1,4096]{2,1,0:T(1,128)}), f32[8,1,4096]{2,1,0:T(1,128)S(1)}, u32[]{:S(2)}, u32[]{:S(2)}) async-start(f32[8,1,4096]{2,1,0:T(1,128)} %reshape.136), calls=%async_computation.6 | async-start | bytes 262144 | tf_op jit(solution)/shard_map/all_to_all | solution.py:54
  211.2 0.8 fusion.37
  212.1 8.2 %all-to-all-done.6 = f32[8,1,4096]{2,1,0:T(1,128)S(1)} async-done(((f32[8,1,4096]{2,1,0:T(1,128)}), f32[8,1,4096]{2,1,0:T(1,128)S(1)}, u32[]{:S(2)}, u32[]{:S(2)}) %all-to-all-start.6) | async-done | bytes 131104 | tf_op jit(solution)/shard_map/all_to_all | solution.py:54
  220.3 1.0 reduce.3
  221.3 0.1 reshape.137
  221.4 0.7 pad_maximum_fusion.1.aug_ref
  222.1 8.1 %shard_map.103 = (f32[64,128]{1,0:T(8,128)}, f32[64,128]{1,0:T(8,128)}) custom-call(f32[64,128]{1,0:T(8,128)} %pad_maximum_fusion.1.aug_ref), custom_call_target="tpu_custom_call" | custom-call | tf_op jit(solution)/shard_map/pallas_call | solution.py:38
  230.2 1.6 fusion.31
  (32 shorter events, 0.6 us)
Async XLA Ops:
  0.6 2.2 copy-start
  3.6 3.7 %copy-start.4 = (s32[1,1,64]{2,1,0:T(1,128)S(1)}, s32[1,1,64]{2,1,0:T(1,128)}, u32[]{:S(2)}) copy-start(s32[1,1,64]{2,1,0:T(1,128)} %param.9) | copy-start | bytes 772
  79.3 0.8 copy-start.2
  79.3 0.8 copy-start.3
  81.8 59.9 %all-to-all-start.1 = ((f32[64,64,128]{2,1,0:T(8,128)}), f32[64,64,128]{2,1,0:T(8,128)S(1)}, u32[]{:S(2)}, u32[]{:S(2)}) async-start(f32[64,64,128]{2,1,0:T(8,128)} %broadcast_in_dim.35), calls=%async_computation.1 | async-start | bytes 4194304 | tf_op jit(solution)/shard_map/all_to_all | solution.py:90
  148.2 15.9 %all-to-all-start.2 = ((f32[8,1,4096]{2,1,0:T(1,128)}), f32[8,1,4096]{2,1,0:T(1,128)S(1)}, u32[]{:S(2)}, u32[]{:S(2)}) async-start(f32[8,1,4096]{2,1,0:T(1,128)} %reshape.130), calls=%async_computation.2 | async-start | bytes 262144 | tf_op jit(solution)/shard_map/all_to_all | solution.py:54
  155.2 5.9 %copy-start.5 = (s32[1,1,64]{2,1,0:T(1,128)S(1)}, s32[1,1,64]{2,1,0:T(1,128)}, u32[]{:S(2)}) copy-start(s32[1,1,64]{2,1,0:T(1,128)} %param.8) | copy-start | bytes 772
  164.1 15.3 %all-to-all-start.3 = ((f32[8,64,256]{2,1,0:T(8,128)}), f32[8,64,256]{2,1,0:T(8,128)S(1)}, u32[]{:S(2)}, u32[]{:S(2)}) async-start(f32[8,64,256]{2,1,0:T(8,128)} %copy.36), calls=%async_computation.3 | async-start | bytes 1048576 | tf_op jit(solution)/shard_map/all_to_all | solution.py:101
  181.9 29.3 %copy-start.1 = (f32[64,128]{1,0:T(8,128)S(1)}, f32[64,128]{1,0:T(8,128)}, u32[]{:S(2)}) copy-start(f32[64,128]{1,0:T(8,128)} %get-tuple-element.8) | copy-start | bytes 98308
  207.6 12.7 %all-to-all-start.6 = ((f32[8,1,4096]{2,1,0:T(1,128)}), f32[8,1,4096]{2,1,0:T(1,128)S(1)}, u32[]{:S(2)}, u32[]{:S(2)}) async-start(f32[8,1,4096]{2,1,0:T(1,128)} %reshape.136), calls=%async_computation.6 | async-start | bytes 262144 | tf_op jit(solution)/shard_map/all_to_all | solution.py:54

commit v6 on v5

--- a/solution.py
+++ b/solution.py
@@ -4,32 +4,27 @@
 import jax.numpy as jnp
 from jax import lax
 from jax.experimental import pallas as pl
-from jax.experimental.pallas import tpu as pltpu
 from jax.sharding import PartitionSpec as P
 
 HIGH = lax.Precision.HIGHEST
 FAST = lax.Precision.HIGH
 
 
-def _factor_kernel(aug_ref, low_ref, inv_ref, work_ref):
+def _factor_kernel(aug_ref, low_ref, inv_ref):
     n = aug_ref.shape[0]
-    work_ref[...] = aug_ref[...]
+    whole = aug_ref[...]
     lane = lax.broadcasted_iota(jnp.int32, aug_ref.shape, 1)
     sub = lax.broadcasted_iota(jnp.int32, (n, 1), 0)
-    lane_row = lax.broadcasted_iota(jnp.int32, (1, aug_ref.shape[1]), 1)
-
-    def step(j, low):
-        whole = work_ref[...]
-        row = work_ref[pl.ds(j, 1), :]
-        pivot = jnp.sum(jnp.where(lane_row == j, row, 0.0), axis=1, keepdims=True)
-        scale = 1.0 / jnp.sqrt(pivot)
+    low = jnp.zeros(aug_ref.shape, jnp.float32)
+    for j in range(n):
+        row = whole[j : j + 1, :]
+        scale = lax.rsqrt(row[:, j : j + 1])
         scaled_row = row * scale
-        inv_ref[pl.ds(j, 1), :] = scaled_row
-        column = jnp.sum(jnp.where(lane == j, whole, 0.0), axis=1, keepdims=True) * scale
-        work_ref[...] = whole - jnp.where(sub > j, column, 0.0) * scaled_row
-        return jnp.where(lane == j, jnp.where(sub >= j, column, 0.0), low)
-
-    low_ref[...] = lax.fori_loop(0, n, step, jnp.zeros(aug_ref.shape, jnp.float32))
+        inv_ref[j : j + 1, :] = scaled_row
+        column = whole[:, j : j + 1] * scale
+        whole = whole - jnp.where(sub > j, column, 0.0) * scaled_row
+        low = jnp.where(lane == j, jnp.where(sub >= j, column, 0.0), low)
+    low_ref[...] = low
 
 
 def cholesky_and_inverse(gram):
@@ -41,7 +36,6 @@
             jax.ShapeDtypeStruct(aug.shape, jnp.float32),
             jax.ShapeDtypeStruct(aug.shape, jnp.float32),
         ),
-        scratch_shapes=[pltpu.VMEM(aug.shape, jnp.float32)],
     )(aug)
     return low[:, :n], inv[:, n:]
 

time: 233 us -> 230 us (0.987)
  Pallas kernels: 16.3 us -> 13.3 us
    pallas_call x2, Pallas kernels: 16.3 us -> 13.3 us  [cholesky_and_inverse(): pl.pallas_call(_factor_kernel, out_shape=(jax.ShapeDtypeStruct(aug.shape,...]
  transfers between devices with their start and end apart: 4 -> 4, of which waited for: 2 -> 2; matrix products, arithmetic and copies ran while one was open for 6% -> 6% of each run, Pallas kernels for 4% -> 3%
where the time goes in v6:
time: 230 us; the launch traced here: 229 us
  blocking collectives  91.2 us (40%)
  waiting for transfers between devices  58.7 us (26%)
  starting transfers between devices  22.7 us (10%)
  matrix products  19.8 us (9%)
  local copies, waits for them, and re-layouts  13.4 us (6%)
  Pallas kernels  13.3 us (6%)
  other arithmetic  8.89 us (4%)
    all_to_all x1, blocking collectives, per_device(): received = lax.all_to_all(partial, ROW, 0, 0, tiled=True)  68.8 us
    all_to_all x1, waiting for transfers between devices, per_device(): column = lax.all_to_all(spread, ROW, 0, 0, tiled=True)  50.4 us
    all_to_all x2, blocking collectives, gather_sum(): lax.all_to_all(jnp.broadcast_to(x[None], (n,) + x.shape), axis, 0, 0, til...  22.5 us
    pallas_call x2, Pallas kernels, cholesky_and_inverse(): pl.pallas_call(_factor_kernel, out_shape=(jax.ShapeDtypeStruct(aug.shape,...  13.3 us
    all_to_all x1, starting transfers between devices, per_device(): column = lax.all_to_all(spread, ROW, 0, 0, tiled=True)  9.45 us
    all_to_all x2, starting transfers between devices, gather_sum(): lax.all_to_all(jnp.broadcast_to(x[None], (n,) + x.shape), axis, 0, 0, til...  8.4 us
    all_to_all x2, waiting for transfers between devices, gather_sum(): lax.all_to_all(jnp.broadcast_to(x[None], (n,) + x.shape), axis, 0, 0, til...  8.23 us
    dot_general x1, matrix products, per_device(): products = jnp.einsum('stb,tab->sta', chosen, local_tiles, precision=FAST)  5.85 us
  transfers between devices with their start and end apart: 4, of which 2 were waited for; matrix products, arithmetic and copies ran while one was open for 6% of the time, Pallas kernels for 3%

profile of v6, /device:TPU:2, one launch (start us, length us, event | category | flops | bytes accessed | tf_op | source)
XLA Modules:
  0.0 228.9 jit_solution(1433115556476479681)
XLA Ops:
  0.6 0.7 compare_and_fusion.1
  1.4 0.7 fusion.45
  2.0 0.8 exponential_bitcast_fusion
  2.9 0.7 gather_fusion
  3.6 3.7 %fusion.13 = f32[64,64,128]{2,0,1:T(8,128)S(1)} fusion(f32[1,1,64,128,128]{4,3,2,1,0:T(8,128)} %param.7, f32[64,64,128]{2,1,0:T(8,128)S(1)} %gather_fusion, pred[64]{0:T(512)(128)(4,1)S(1)} %compare_and_fusion.1), kind=kOutput, calls=%fused_computation.16 | convolution fusion | flops 403177472 | bytes 8388672 | tf_op jit(solution)/shard_map/sta,tab->stb/dot_general | solution.py:75
  7.3 2.0 fusion.23
  9.3 1.2 copy.31
  10.5 68.8 %all_to_all.35 = f32[64,64,128]{2,1,0:T(8,128)S(1)} all-to-all(f32[64,64,128]{2,1,0:T(8,128)S(1)} %copy.31), channel_id=1, replica_groups=mesh['row_hi'=8,'row_lo'=8,'col'=8] {'row_hi','row_lo'}, dimensions={0} | all-to-all | bytes 4194304 | tf_op jit(solution)/shard_map/all_to_all | solution.py:81
  79.3 0.1 reduce_sum.54
  79.4 0.6 copy-done.2
  80.0 0.2 convolution_subtract_fusion.1
  80.2 1.6 broadcast_in_dim.35
  81.8 9.4 %all-to-all-start.1 = ((f32[64,64,128]{2,1,0:T(8,128)}), f32[64,64,128]{2,1,0:T(8,128)S(1)}, u32[]{:S(2)}, u32[]{:S(2)}) async-start(f32[64,64,128]{2,1,0:T(8,128)} %broadcast_in_dim.35), calls=%async_computation.1 | async-start | bytes 4194304 | tf_op jit(solution)/shard_map/all_to_all | solution.py:84
  91.3 50.4 %all-to-all-done.1 = f32[64,64,128]{2,1,0:T(8,128)S(1)} async-done(((f32[64,64,128]{2,1,0:T(8,128)}), f32[64,64,128]{2,1,0:T(8,128)S(1)}, u32[]{:S(2)}, u32[]{:S(2)}) %all-to-all-start.1) | async-done | bytes 2097184 | tf_op jit(solution)/shard_map/all_to_all | solution.py:84
  141.7 1.2 fusion.8
  143.0 2.6 %copy.33 = f32[64,64,128]{2,0,1:T(8,128)} copy(f32[64,64,128]{2,1,0:T(8,128)S(1)} %fusion.8) | data formatting | bytes 4194304 | tf_op jit(solution)/shard_map/mul | solution.py:89
  145.5 1.8 convolution_bitcast_fusion
  147.3 0.8 reshape.130
  148.2 4.8 %all-to-all-start.2 = ((f32[8,1,4096]{2,1,0:T(1,128)}), f32[8,1,4096]{2,1,0:T(1,128)S(1)}, u32[]{:S(2)}, u32[]{:S(2)}) async-start(f32[8,1,4096]{2,1,0:T(1,128)} %reshape.130), calls=%async_computation.2 | async-start | bytes 262144 | tf_op jit(solution)/shard_map/all_to_all | solution.py:48
  153.0 2.3 gather_fusion.1
  155.3 5.8 %fusion.18 = f32[64,64,128]{2,0,1:T(8,128)S(1)} fusion(f32[1,1,64,128,128]{4,3,2,1,0:T(8,128)} %param.7, f32[64,64,128]{2,1,0:T(8,128)S(1)} %gather_fusion.1, pred[64]{0:T(512)(128)(4,1)S(1)} %compare_and_fusion), kind=kOutput, calls=%fused_computation.17 | convolution fusion | flops 403177472 | bytes 8388672 | tf_op jit(solution)/shard_map/stb,tab->sta/dot_general | solution.py:91
  161.1 1.6 fusion.6
  162.7 0.4 reshape.129
  163.2 1.0 copy.36
  164.1 4.8 %all-to-all-start.3 = ((f32[8,64,256]{2,1,0:T(8,128)}), f32[8,64,256]{2,1,0:T(8,128)S(1)}, u32[]{:S(2)}, u32[]{:S(2)}) async-start(f32[8,64,256]{2,1,0:T(8,128)} %copy.36), calls=%async_computation.3 | async-start | bytes 1048576 | tf_op jit(solution)/shard_map/all_to_all | solution.py:95
  168.9 0.5 broadcast.89
  169.4 1.0 reduce
  170.4 0.1 reshape.131
  170.5 0.7 pad_maximum_fusion.aug_ref
  171.2 6.7 %shard_map.102 = (f32[64,128]{1,0:T(8,128)}, f32[64,128]{1,0:T(8,128)}) custom-call(f32[64,128]{1,0:T(8,128)} %pad_maximum_fusion.aug_ref), custom_call_target="tpu_custom_call" | custom-call | tf_op jit(solution)/shard_map/pallas_call | solution.py:33
  177.9 1.0 convolution_multiply_fusion
  179.0 1.0 convolution_subtract_fusion
  180.0 0.2 fusion.51
  180.2 0.2 reshape.132
  180.4 9.3 %all_to_all.36 = f32[8,1,4096]{2,1,0:T(1,128)S(1)} all-to-all(f32[8,1,4096]{2,1,0:T(1,128)S(1)} %reshape.132), channel_id=1, replica_groups=mesh['row_hi'=8,'row_lo'=8,'col'=8] {'col'}, dimensions={0} | all-to-all | bytes 262144 | tf_op jit(solution)/shard_map/all_to_all | solution.py:48
  189.7 1.0 reduce.1
  190.7 0.1 reshape.133
  190.8 0.2 reshape.134
  191.0 13.2 %all_to_all.37 = f32[8,1,4096]{2,1,0:T(1,128)S(1)} all-to-all(f32[8,1,4096]{2,1,0:T(1,128)S(1)} %reshape.134), channel_id=1, replica_groups=mesh['row_hi'=8,'row_lo'=8,'col'=8] {'row_lo'}, dimensions={0} | all-to-all | bytes 262144 | tf_op jit(solution)/shard_map/all_to_all | solution.py:48
  204.2 1.0 reduce.2
  205.3 0.8 reshape.136
  206.1 3.6 %all-to-all-start.6 = ((f32[8,1,4096]{2,1,0:T(1,128)}), f32[8,1,4096]{2,1,0:T(1,128)S(1)}, u32[]{:S(2)}, u32[]{:S(2)}) async-start(f32[8,1,4096]{2,1,0:T(1,128)} %reshape.136), calls=%async_computation.6 | async-start | bytes 262144 | tf_op jit(solution)/shard_map/all_to_all | solution.py:48
  209.8 0.8 fusion.37
  210.6 8.2 %all-to-all-done.6 = f32[8,1,4096]{2,1,0:T(1,128)S(1)} async-done(((f32[8,1,4096]{2,1,0:T(1,128)}), f32[8,1,4096]{2,1,0:T(1,128)S(1)}, u32[]{:S(2)}, u32[]{:S(2)}) %all-to-all-start.6) | async-done | bytes 131104 | tf_op jit(solution)/shard_map/all_to_all | solution.py:48
  218.8 1.0 reduce.3
  219.9 0.7 pad_maximum_fusion.1.aug_ref
  220.6 6.7 %shard_map.103 = (f32[64,128]{1,0:T(8,128)}, f32[64,128]{1,0:T(8,128)}) custom-call(f32[64,128]{1,0:T(8,128)} %pad_maximum_fusion.1.aug_ref), custom_call_target="tpu_custom_call" | custom-call | tf_op jit(solution)/shard_map/pallas_call | solution.py:33
  227.3 1.6 fusion.31
  (32 shorter events, 0.6 us)
Async XLA Ops:
  0.6 2.2 copy-start
  3.6 3.7 %copy-start.4 = (s32[1,1,64]{2,1,0:T(1,128)S(1)}, s32[1,1,64]{2,1,0:T(1,128)}, u32[]{:S(2)}) copy-start(s32[1,1,64]{2,1,0:T(1,128)} %param.9) | copy-start | bytes 772
  79.3 0.8 copy-start.2
  79.3 0.8 copy-start.3
  81.8 59.9 %all-to-all-start.1 = ((f32[64,64,128]{2,1,0:T(8,128)}), f32[64,64,128]{2,1,0:T(8,128)S(1)}, u32[]{:S(2)}, u32[]{:S(2)}) async-start(f32[64,64,128]{2,1,0:T(8,128)} %broadcast_in_dim.35), calls=%async_computation.1 | async-start | bytes 4194304 | tf_op jit(solution)/shard_map/all_to_all | solution.py:84
  148.2 15.9 %all-to-all-start.2 = ((f32[8,1,4096]{2,1,0:T(1,128)}), f32[8,1,4096]{2,1,0:T(1,128)S(1)}, u32[]{:S(2)}, u32[]{:S(2)}) async-start(f32[8,1,4096]{2,1,0:T(1,128)} %reshape.130), calls=%async_computation.2 | async-start | bytes 262144 | tf_op jit(solution)/shard_map/all_to_all | solution.py:48
  155.2 5.9 %copy-start.5 = (s32[1,1,64]{2,1,0:T(1,128)S(1)}, s32[1,1,64]{2,1,0:T(1,128)}, u32[]{:S(2)}) copy-start(s32[1,1,64]{2,1,0:T(1,128)} %param.8) | copy-start | bytes 772
  164.1 13.8 %all-to-all-start.3 = ((f32[8,64,256]{2,1,0:T(8,128)}), f32[8,64,256]{2,1,0:T(8,128)S(1)}, u32[]{:S(2)}, u32[]{:S(2)}) async-start(f32[8,64,256]{2,1,0:T(8,128)} %copy.36), calls=%async_computation.3 | async-start | bytes 1048576 | tf_op jit(solution)/shard_map/all_to_all | solution.py:95
  180.4 29.3 %copy-start.1 = (f32[64,128]{1,0:T(8,128)S(1)}, f32[64,128]{1,0:T(8,128)}, u32[]{:S(2)}) copy-start(f32[64,128]{1,0:T(8,128)} %get-tuple-element.8) | copy-start | bytes 98308
  206.1 12.7 %all-to-all-start.6 = ((f32[8,1,4096]{2,1,0:T(1,128)}), f32[8,1,4096]{2,1,0:T(1,128)S(1)}, u32[]{:S(2)}, u32[]{:S(2)}) async-start(f32[8,1,4096]{2,1,0:T(1,128)} %reshape.136), calls=%async_computation.6 | async-start | bytes 262144 | tf_op jit(solution)/shard_map/all_to_all | solution.py:48

commit v7 on v6

--- a/solution.py
+++ b/solution.py
@@ -65,17 +65,15 @@
     u_piece = block_rows // n_col
     col_scale = jnp.exp2(-exponents.astype(jnp.float32))
     lowtri = jnp.tril(prior)
-    col_hits = (cols_here[:, None] == jnp.arange(cols_tiles, dtype=jnp.int32)[None, :]).astype(
-        jnp.float32
-    )
     row_hits = (rows_here[:, None] == jnp.arange(rows_tiles, dtype=jnp.int32)[None, :]).astype(
         jnp.float32
     )
-    picked = jnp.take(u_basis.reshape(width, rows_tiles, tl), rows_here, axis=1)
-    prod = jnp.einsum("sta,tab->stb", picked, local_tiles, precision=FAST)
-    partial = jnp.einsum("stb,tc->csb", prod, col_hits, precision=FAST).reshape(
-        n_row, v_piece // tl, width, tl
-    )
+    col_match = cols_here[:, None] == jnp.arange(cols_tiles, dtype=jnp.int32)[None, :]
+    order = jnp.sum(jnp.where(col_match, jnp.arange(count, dtype=jnp.int32)[:, None], 0), axis=0)
+    u_tiles = u_basis.reshape(width, rows_tiles, tl).transpose(1, 0, 2)
+    picked = jnp.take(u_tiles, rows_here, axis=0)
+    prod = jnp.einsum("tsa,tab->tsb", picked, local_tiles, precision=FAST)
+    partial = jnp.take(prod, order, axis=0).reshape(n_row, v_piece // tl, width, tl)
     partial = (partial * col_scale.reshape(n_row, v_piece // tl, 1, tl)).transpose(0, 2, 1, 3)
     partial = partial.reshape(n_row, width, v_piece)
     received = lax.all_to_all(partial, ROW, 0, 0, tiled=True)
@@ -86,10 +84,11 @@
     v_factor, v_inverse = cholesky_and_inverse(gram / total_cols)
     v_next = jnp.dot(v_inverse, pt_piece, precision=HIGH)
     factor = math.sqrt(total_rows / total_cols)
-    scaled = column.transpose(1, 0, 2).reshape(width, block_cols) * col_scale
-    chosen = jnp.take(scaled.reshape(width, cols_tiles, tl), cols_here, axis=1)
-    products = jnp.einsum("stb,tab->sta", chosen, local_tiles, precision=FAST)
-    terms = jnp.einsum("sta,tr->rsa", products, row_hits, precision=FAST)
+    scaled = column * col_scale.reshape(n_row, 1, v_piece)
+    scaled = scaled.reshape(n_row, width, v_piece // tl, tl).transpose(0, 2, 1, 3)
+    chosen = jnp.take(scaled.reshape(cols_tiles, width, tl), cols_here, axis=0)
+    products = jnp.einsum("tsb,tab->tsa", chosen, local_tiles, precision=FAST)
+    terms = jnp.einsum("tsa,tr->rsa", products, row_hits, precision=FAST)
     terms = terms.reshape(n_col, u_piece // tl, width, tl).transpose(0, 2, 1, 3)
     terms = terms.reshape(n_col, width, u_piece)
     summed = lax.all_to_all(terms, "col", 0, 0, tiled=True).sum(0)

time: 230 us -> 230 us (level)
    mul x2 -> x0, local copies, waits for them, and re-layouts: 3.79 us -> none  [the longest x1 2.57 us: per_device(): scaled = column.transpose(1, 0, 2).reshape(width, block_cols) * col_scale]
    gather x2 -> x3, local copies, waits for them, and re-layouts: 2.95 us -> 5.22 us  [the longest x1 2.27 us: per_device(): jnp.take(prod, order, axis=0).reshape(n_row, v_piece // tl, width, tl)]
    dot_general x4 -> x3, matrix products: 13.1 us -> 12.8 us  [the longest x1 5.85 us: per_device(): products = jnp.einsum('tsb,tab->tsa', chosen, local_tiles, precision=FAST)]
  transfers between devices with their start and end apart: 4 -> 4, of which waited for: 2 -> 2; matrix products, arithmetic and copies ran while one was open for 6% -> 7% of each run, Pallas kernels for 3% -> 3%
where the time goes in v7:
time: 230 us; the launch traced here: 229 us
  blocking collectives  90.6 us (39%)
  waiting for transfers between devices  59.7 us (26%)
  starting transfers between devices  22.5 us (10%)
  matrix products  19.5 us (8%)
  Pallas kernels  13.3 us (6%)
  local copies, waits for them, and re-layouts  11.9 us (5%)
  other arithmetic  10.3 us (4%)
    all_to_all x1, blocking collectives, per_device(): received = lax.all_to_all(partial, ROW, 0, 0, tiled=True)  68.8 us
    all_to_all x1, waiting for transfers between devices, per_device(): column = lax.all_to_all(spread, ROW, 0, 0, tiled=True)  51.5 us
    all_to_all x2, blocking collectives, gather_sum(): lax.all_to_all(jnp.broadcast_to(x[None], (n,) + x.shape), axis, 0, 0, til...  21.9 us
    pallas_call x2, Pallas kernels, cholesky_and_inverse(): pl.pallas_call(_factor_kernel, out_shape=(jax.ShapeDtypeStruct(aug.shape,...  13.3 us
    all_to_all x1, starting transfers between devices, per_device(): column = lax.all_to_all(spread, ROW, 0, 0, tiled=True)  9.23 us
    all_to_all x2, starting transfers between devices, gather_sum(): lax.all_to_all(jnp.broadcast_to(x[None], (n,) + x.shape), axis, 0, 0, til...  8.51 us
    all_to_all x2, waiting for transfers between devices, gather_sum(): lax.all_to_all(jnp.broadcast_to(x[None], (n,) + x.shape), axis, 0, 0, til...  8.23 us
    dot_general x1, matrix products, per_device(): products = jnp.einsum('tsb,tab->tsa', chosen, local_tiles, precision=FAST)  5.85 us
  transfers between devices with their start and end apart: 4, of which 2 were waited for; matrix products, arithmetic and copies ran while one was open for 7% of the time, Pallas kernels for 3%

profile of v7, /device:TPU:2, one launch (start us, length us, event | category | flops | bytes accessed | tf_op | source)
XLA Modules:
  0.0 228.9 jit_solution(11437227787528394103)
XLA Ops:
  0.6 0.8 select_reduce_fusion
  1.5 0.7 compare_and_fusion.2
  2.1 0.7 fusion.24
  2.8 0.8 exponential_bitcast_fusion
  3.7 0.7 gather_fusion
  4.3 5.4 %fusion.2 = f32[64,64,128]{2,1,0:T(8,128)} fusion(f32[1,1,64,128,128]{4,3,2,1,0:T(8,128)} %param.9, f32[64,64,128]{2,1,0:T(8,128)S(1)} %gather_fusion, pred[64]{0:T(512)(128)(4,1)S(1)} %compare_and_fusion.2), kind=kOutput, calls=%fused_computation.5 | convolution fusion | flops 403177472 | bytes 8388672 | tf_op jit(solution)/shard_map/tsa,tab->tsb/dot_general | solution.py:75
  9.7 2.3 gather_fusion.1
  12.0 0.2 select_multiply_fusion
  12.3 68.8 %all_to_all.35 = f32[64,64,128]{2,1,0:T(8,128)S(1)} all-to-all(f32[64,64,128]{2,1,0:T(8,128)S(1)} %select_multiply_fusion), channel_id=1, replica_groups=mesh['row_hi'=8,'row_lo'=8,'col'=8] {'row_hi','row_lo'}, dimensions={0} | all-to-all | bytes 4194304 | tf_op jit(solution)/shard_map/all_to_all | solution.py:79
  81.0 0.1 reduce_sum.64
  81.2 0.6 copy-done.2
  81.8 0.2 convolution_subtract_fusion.1
  82.0 1.6 broadcast_in_dim.73
  83.6 9.2 %all-to-all-start.1 = ((f32[64,64,128]{2,1,0:T(8,128)}), f32[64,64,128]{2,1,0:T(8,128)S(1)}, u32[]{:S(2)}, u32[]{:S(2)}) async-start(f32[64,64,128]{2,1,0:T(8,128)} %broadcast_in_dim.73), calls=%async_computation.1 | async-start | bytes 4194304 | tf_op jit(solution)/shard_map/all_to_all | solution.py:82
  92.9 51.5 %all-to-all-done.1 = f32[64,64,128]{2,1,0:T(8,128)S(1)} async-done(((f32[64,64,128]{2,1,0:T(8,128)}), f32[64,64,128]{2,1,0:T(8,128)S(1)}, u32[]{:S(2)}, u32[]{:S(2)}) %all-to-all-start.1) | async-done | bytes 2097184 | tf_op jit(solution)/shard_map/all_to_all | solution.py:82
  144.4 1.8 convolution_bitcast_fusion
  146.2 0.8 reshape.108
  147.0 4.8 %all-to-all-start.2 = ((f32[8,1,4096]{2,1,0:T(1,128)}), f32[8,1,4096]{2,1,0:T(1,128)S(1)}, u32[]{:S(2)}, u32[]{:S(2)}) async-start(f32[8,1,4096]{2,1,0:T(1,128)} %reshape.108), calls=%async_computation.2 | async-start | bytes 262144 | tf_op jit(solution)/shard_map/all_to_all | solution.py:48
  151.8 1.6 broadcast_multiply_fusion
  153.5 2.3 gather_fusion.2
  155.7 5.8 %fusion = f32[64,64,128]{2,1,0:T(8,128)S(1)} fusion(f32[1,1,64,128,128]{4,3,2,1,0:T(8,128)} %param.9, f32[64,64,128]{2,1,0:T(8,128)S(1)} %gather_fusion.2, pred[64]{0:T(512)(128)(4,1)S(1)} %compare_and_fusion), kind=kOutput, calls=%fused_computation.3 | convolution fusion | flops 403177472 | bytes 8388672 | tf_op jit(solution)/shard_map/tsb,tab->tsa/dot_general | solution.py:90
  161.6 1.6 fusion.4
  163.2 0.4 reshape.107
  163.6 1.0 copy.19
  164.6 4.8 %all-to-all-start.3 = ((f32[8,64,256]{2,1,0:T(8,128)}), f32[8,64,256]{2,1,0:T(8,128)S(1)}, u32[]{:S(2)}, u32[]{:S(2)}) async-start(f32[8,64,256]{2,1,0:T(8,128)} %copy.19), calls=%async_computation.3 | async-start | bytes 1048576 | tf_op jit(solution)/shard_map/all_to_all | solution.py:94
  169.4 0.5 broadcast.48
  169.9 1.0 reduce
  171.0 0.7 pad_maximum_fusion.aug_ref
  171.7 6.7 %shard_map.102 = (f32[64,128]{1,0:T(8,128)}, f32[64,128]{1,0:T(8,128)}) custom-call(f32[64,128]{1,0:T(8,128)} %pad_maximum_fusion.aug_ref), custom_call_target="tpu_custom_call" | custom-call | tf_op jit(solution)/shard_map/pallas_call | solution.py:33
  178.4 1.0 convolution_multiply_fusion
  179.5 1.0 convolution_subtract_fusion
  180.5 0.2 fusion.29
  180.7 0.2 reshape.110
  180.9 9.3 %all_to_all.36 = f32[8,1,4096]{2,1,0:T(1,128)S(1)} all-to-all(f32[8,1,4096]{2,1,0:T(1,128)S(1)} %reshape.110), channel_id=1, replica_groups=mesh['row_hi'=8,'row_lo'=8,'col'=8] {'col'}, dimensions={0} | all-to-all | bytes 262144 | tf_op jit(solution)/shard_map/all_to_all | solution.py:48
  190.2 1.0 reduce.1
  191.2 0.1 reshape.111
  191.3 0.2 reshape.112
  191.5 12.6 %all_to_all.37 = f32[8,1,4096]{2,1,0:T(1,128)S(1)} all-to-all(f32[8,1,4096]{2,1,0:T(1,128)S(1)} %reshape.112), channel_id=1, replica_groups=mesh['row_hi'=8,'row_lo'=8,'col'=8] {'row_lo'}, dimensions={0} | all-to-all | bytes 262144 | tf_op jit(solution)/shard_map/all_to_all | solution.py:48
  204.1 1.0 reduce.2
  205.2 0.8 reshape.114
  206.1 3.7 %all-to-all-start.6 = ((f32[8,1,4096]{2,1,0:T(1,128)}), f32[8,1,4096]{2,1,0:T(1,128)S(1)}, u32[]{:S(2)}, u32[]{:S(2)}) async-start(f32[8,1,4096]{2,1,0:T(1,128)} %reshape.114), calls=%async_computation.6 | async-start | bytes 262144 | tf_op jit(solution)/shard_map/all_to_all | solution.py:48
  209.7 0.8 fusion.17
  210.6 8.2 %all-to-all-done.6 = f32[8,1,4096]{2,1,0:T(1,128)S(1)} async-done(((f32[8,1,4096]{2,1,0:T(1,128)}), f32[8,1,4096]{2,1,0:T(1,128)S(1)}, u32[]{:S(2)}, u32[]{:S(2)}) %all-to-all-start.6) | async-done | bytes 131104 | tf_op jit(solution)/shard_map/all_to_all | solution.py:48
  218.8 1.0 reduce.3
  219.8 0.1 reshape.115
  219.9 0.7 pad_maximum_fusion.1.aug_ref
  220.6 6.7 %shard_map.103 = (f32[64,128]{1,0:T(8,128)}, f32[64,128]{1,0:T(8,128)}) custom-call(f32[64,128]{1,0:T(8,128)} %pad_maximum_fusion.1.aug_ref), custom_call_target="tpu_custom_call" | custom-call | tf_op jit(solution)/shard_map/pallas_call | solution.py:33
  227.3 1.6 fusion.13
  (35 shorter events, 0.6 us)
Async XLA Ops:
  0.6 3.0 %copy-start = (f32[64,2048]{1,0:T(8,128)S(1)}, f32[64,2048]{1,0:T(8,128)}, u32[]{:S(2)}) copy-start(f32[64,2048]{1,0:T(8,128)} %param.13) | copy-start | bytes 1572868
  81.0 0.8 copy-start.2
  81.0 0.8 copy-start.3
  83.6 9.2 %copy-start.5 = (s32[1,1,64]{2,1,0:T(1,128)S(1)}, s32[1,1,64]{2,1,0:T(1,128)}, u32[]{:S(2)}) copy-start(s32[1,1,64]{2,1,0:T(1,128)} %param.11) | copy-start | bytes 772
  83.6 60.8 %all-to-all-start.1 = ((f32[64,64,128]{2,1,0:T(8,128)}), f32[64,64,128]{2,1,0:T(8,128)S(1)}, u32[]{:S(2)}, u32[]{:S(2)}) async-start(f32[64,64,128]{2,1,0:T(8,128)} %broadcast_in_dim.73), calls=%async_computation.1 | async-start | bytes 4194304 | tf_op jit(solution)/shard_map/all_to_all | solution.py:82
  147.0 17.6 %all-to-all-start.2 = ((f32[8,1,4096]{2,1,0:T(1,128)}), f32[8,1,4096]{2,1,0:T(1,128)S(1)}, u32[]{:S(2)}, u32[]{:S(2)}) async-start(f32[8,1,4096]{2,1,0:T(1,128)} %reshape.108), calls=%async_computation.2 | async-start | bytes 262144 | tf_op jit(solution)/shard_map/all_to_all | solution.py:48
  155.7 5.9 %copy-start.4 = (s32[1,1,64]{2,1,0:T(1,128)S(1)}, s32[1,1,64]{2,1,0:T(1,128)}, u32[]{:S(2)}) copy-start(s32[1,1,64]{2,1,0:T(1,128)} %param.10) | copy-start | bytes 772
  164.6 13.8 %all-to-all-start.3 = ((f32[8,64,256]{2,1,0:T(8,128)}), f32[8,64,256]{2,1,0:T(8,128)S(1)}, u32[]{:S(2)}, u32[]{:S(2)}) async-start(f32[8,64,256]{2,1,0:T(8,128)} %copy.19), calls=%async_computation.3 | async-start | bytes 1048576 | tf_op jit(solution)/shard_map/all_to_all | solution.py:94
  180.9 28.8 %copy-start.1 = (f32[64,128]{1,0:T(8,128)S(1)}, f32[64,128]{1,0:T(8,128)}, u32[]{:S(2)}) copy-start(f32[64,128]{1,0:T(8,128)} %get-tuple-element.9) | copy-start | bytes 98308
  206.1 12.8 %all-to-all-start.6 = ((f32[8,1,4096]{2,1,0:T(1,128)}), f32[8,1,4096]{2,1,0:T(1,128)S(1)}, u32[]{:S(2)}, u32[]{:S(2)}) async-start(f32[8,1,4096]{2,1,0:T(1,128)} %reshape.114), calls=%async_computation.6 | async-start | bytes 262144 | tf_op jit(solution)/shard_map/all_to_all | solution.py:48

commit v8 on v7

--- a/solution.py
+++ b/solution.py
@@ -13,9 +13,9 @@
 def _factor_kernel(aug_ref, low_ref, inv_ref):
     n = aug_ref.shape[0]
     whole = aug_ref[...]
-    lane = lax.broadcasted_iota(jnp.int32, aug_ref.shape, 1)
+    lane = lax.broadcasted_iota(jnp.int32, low_ref.shape, 1)
     sub = lax.broadcasted_iota(jnp.int32, (n, 1), 0)
-    low = jnp.zeros(aug_ref.shape, jnp.float32)
+    low = jnp.zeros(low_ref.shape, jnp.float32)
     for j in range(n):
         row = whole[j : j + 1, :]
         scale = lax.rsqrt(row[:, j : j + 1])
@@ -27,17 +27,17 @@
     low_ref[...] = low
 
 
-def cholesky_and_inverse(gram):
+def cholesky_and_solve(gram, rhs):
     n = gram.shape[0]
-    aug = jnp.concatenate([gram, jnp.eye(n, dtype=jnp.float32)], axis=1)
-    low, inv = pl.pallas_call(
+    aug = jnp.concatenate([gram, rhs], axis=1)
+    low, solved = pl.pallas_call(
         _factor_kernel,
         out_shape=(
-            jax.ShapeDtypeStruct(aug.shape, jnp.float32),
+            jax.ShapeDtypeStruct((n, max(n, 128)), jnp.float32),
             jax.ShapeDtypeStruct(aug.shape, jnp.float32),
         ),
     )(aug)
-    return low[:, :n], inv[:, n:]
+    return low[:, :n], solved[:, n:]
 
 
 ROW = ("row_hi", "row_lo")
@@ -81,7 +81,7 @@
     spread = jnp.broadcast_to(pt_piece[None], (n_row, width, v_piece))
     column = lax.all_to_all(spread, ROW, 0, 0, tiled=True)
     gram = gather_sum(jnp.einsum("jsb,jtb->st", column, column, precision=HIGH), "col")
-    v_factor, v_inverse = cholesky_and_inverse(gram / total_cols)
+    v_factor, v_inverse = cholesky_and_solve(gram / total_cols, jnp.eye(width, dtype=jnp.float32))
     v_next = jnp.dot(v_inverse, pt_piece, precision=HIGH)
     factor = math.sqrt(total_rows / total_cols)
     scaled = column * col_scale.reshape(n_row, 1, v_piece)
@@ -96,8 +96,7 @@
     qt_piece = factor * jnp.dot(v_inverse, summed, precision=HIGH) - jnp.dot(v_factor.T, u_own, precision=HIGH)
     ugram = jnp.dot(qt_piece, qt_piece.T, precision=HIGH)
     ugram = gather_sum(gather_sum(gather_sum(ugram, "col"), "row_lo"), "row_hi")
-    u_factor, u_inverse = cholesky_and_inverse(ugram / total_rows)
-    u_next = jnp.dot(u_inverse, qt_piece, precision=HIGH)
+    u_factor, u_next = cholesky_and_solve(ugram / total_rows, qt_piece)
     return (u_next, v_next, v_factor, u_factor)
 
 

time: 230 us -> 230 us (level)
  no operation moved by 1% of the time
where the time goes in v8:
time: 230 us; the launch traced here: 229 us
  blocking collectives  90.6 us (39%)
  waiting for transfers between devices  59.7 us (26%)
  starting transfers between devices  22.5 us (10%)
  matrix products  17.9 us (8%)
  local copies, waits for them, and re-layouts  13.5 us (6%)
  Pallas kernels  13.5 us (6%)
  other arithmetic  10.3 us (4%)
    all_to_all x1, blocking collectives, per_device(): received = lax.all_to_all(partial, ROW, 0, 0, tiled=True)  68.8 us
    all_to_all x1, waiting for transfers between devices, per_device(): column = lax.all_to_all(spread, ROW, 0, 0, tiled=True)  51.5 us
    all_to_all x2, blocking collectives, gather_sum(): lax.all_to_all(jnp.broadcast_to(x[None], (n,) + x.shape), axis, 0, 0, til...  21.9 us
    pallas_call x2, Pallas kernels, cholesky_and_solve(): pl.pallas_call(_factor_kernel, out_shape=(jax.ShapeDtypeStruct((n, max(n,...  13.5 us
    all_to_all x1, starting transfers between devices, per_device(): column = lax.all_to_all(spread, ROW, 0, 0, tiled=True)  9.23 us
    all_to_all x2, starting transfers between devices, gather_sum(): lax.all_to_all(jnp.broadcast_to(x[None], (n,) + x.shape), axis, 0, 0, til...  8.51 us
    all_to_all x2, waiting for transfers between devices, gather_sum(): lax.all_to_all(jnp.broadcast_to(x[None], (n,) + x.shape), axis, 0, 0, til...  8.23 us
    dot_general x1, matrix products, per_device(): products = jnp.einsum('tsb,tab->tsa', chosen, local_tiles, precision=FAST)  5.85 us
  transfers between devices with their start and end apart: 4, of which 2 were waited for; matrix products, arithmetic and copies ran while one was open for 7% of the time, Pallas kernels for 3%

profile of v8, /device:TPU:2, one launch (start us, length us, event | category | flops | bytes accessed | tf_op | source)
XLA Modules:
  0.0 229.1 jit_solution(9445625059590023506)
XLA Ops:
  0.6 0.7 fusion.22
  1.4 0.7 compare_and_fusion.2
  2.0 0.7 select_reduce_fusion
  2.9 0.8 exponential_bitcast_fusion
  3.7 0.7 gather_fusion
  4.4 5.4 %fusion.2 = f32[64,64,128]{2,1,0:T(8,128)} fusion(f32[1,1,64,128,128]{4,3,2,1,0:T(8,128)} %param.9, f32[64,64,128]{2,1,0:T(8,128)S(1)} %gather_fusion, pred[64]{0:T(512)(128)(4,1)S(1)} %compare_and_fusion.2), kind=kOutput, calls=%fused_computation.5 | convolution fusion | flops 403177472 | bytes 8388672 | tf_op jit(solution)/shard_map/tsa,tab->tsb/dot_general | solution.py:75
  9.8 2.3 gather_fusion.1
  12.0 0.2 select_multiply_fusion
  12.3 68.8 %all_to_all.35 = f32[64,64,128]{2,1,0:T(8,128)S(1)} all-to-all(f32[64,64,128]{2,1,0:T(8,128)S(1)} %select_multiply_fusion), channel_id=1, replica_groups=mesh['row_hi'=8,'row_lo'=8,'col'=8] {'row_hi','row_lo'}, dimensions={0} | all-to-all | bytes 4194304 | tf_op jit(solution)/shard_map/all_to_all | solution.py:79
  81.0 0.1 reduce_sum.64
  81.2 0.6 copy-done.2
  81.8 0.2 convolution_subtract_fusion.1
  82.0 1.6 broadcast_in_dim.73
  83.6 9.2 %all-to-all-start.1 = ((f32[64,64,128]{2,1,0:T(8,128)}), f32[64,64,128]{2,1,0:T(8,128)S(1)}, u32[]{:S(2)}, u32[]{:S(2)}) async-start(f32[64,64,128]{2,1,0:T(8,128)} %broadcast_in_dim.73), calls=%async_computation.1 | async-start | bytes 4194304 | tf_op jit(solution)/shard_map/all_to_all | solution.py:82
  92.9 51.5 %all-to-all-done.1 = f32[64,64,128]{2,1,0:T(8,128)S(1)} async-done(((f32[64,64,128]{2,1,0:T(8,128)}), f32[64,64,128]{2,1,0:T(8,128)S(1)}, u32[]{:S(2)}, u32[]{:S(2)}) %all-to-all-start.1) | async-done | bytes 2097184 | tf_op jit(solution)/shard_map/all_to_all | solution.py:82
  144.4 1.8 convolution_bitcast_fusion
  146.2 0.8 reshape.108
  147.0 4.8 %all-to-all-start.2 = ((f32[8,1,4096]{2,1,0:T(1,128)}), f32[8,1,4096]{2,1,0:T(1,128)S(1)}, u32[]{:S(2)}, u32[]{:S(2)}) async-start(f32[8,1,4096]{2,1,0:T(1,128)} %reshape.108), calls=%async_computation.2 | async-start | bytes 262144 | tf_op jit(solution)/shard_map/all_to_all | solution.py:48
  151.8 1.6 broadcast_multiply_fusion
  153.5 2.3 gather_fusion.2
  155.8 5.8 %fusion = f32[64,64,128]{2,1,0:T(8,128)S(1)} fusion(f32[1,1,64,128,128]{4,3,2,1,0:T(8,128)} %param.9, f32[64,64,128]{2,1,0:T(8,128)S(1)} %gather_fusion.2, pred[64]{0:T(512)(128)(4,1)S(1)} %compare_and_fusion), kind=kOutput, calls=%fused_computation.3 | convolution fusion | flops 403177472 | bytes 8388672 | tf_op jit(solution)/shard_map/tsb,tab->tsa/dot_general | solution.py:90
  161.6 1.6 fusion.4
  163.2 0.4 reshape.107
  163.7 1.0 copy.19
  164.6 4.8 %all-to-all-start.3 = ((f32[8,64,256]{2,1,0:T(8,128)}), f32[8,64,256]{2,1,0:T(8,128)S(1)}, u32[]{:S(2)}, u32[]{:S(2)}) async-start(f32[8,64,256]{2,1,0:T(8,128)} %copy.19), calls=%async_computation.3 | async-start | bytes 1048576 | tf_op jit(solution)/shard_map/all_to_all | solution.py:94
  169.4 0.5 broadcast.48
  169.9 1.0 reduce
  170.9 0.1 reshape.109
  171.0 0.7 pad_maximum_fusion.1.aug_ref
  171.7 6.7 %shard_map.102 = (f32[64,128]{1,0:T(8,128)}, f32[64,128]{1,0:T(8,128)}) custom-call(f32[64,128]{1,0:T(8,128)} %pad_maximum_fusion.1.aug_ref), custom_call_target="tpu_custom_call" | custom-call | tf_op jit(solution)/shard_map/pallas_call | solution.py:33
  178.4 1.0 convolution_multiply_fusion
  179.5 1.0 convolution_subtract_fusion
  180.5 0.2 fusion.27
  180.7 0.2 reshape.110
  180.9 9.3 %all_to_all.36 = f32[8,1,4096]{2,1,0:T(1,128)S(1)} all-to-all(f32[8,1,4096]{2,1,0:T(1,128)S(1)} %reshape.110), channel_id=1, replica_groups=mesh['row_hi'=8,'row_lo'=8,'col'=8] {'col'}, dimensions={0} | all-to-all | bytes 262144 | tf_op jit(solution)/shard_map/all_to_all | solution.py:48
  190.2 1.0 reduce.1
  191.2 0.1 reshape.111
  191.3 0.2 reshape.112
  191.5 12.6 %all_to_all.37 = f32[8,1,4096]{2,1,0:T(1,128)S(1)} all-to-all(f32[8,1,4096]{2,1,0:T(1,128)S(1)} %reshape.112), channel_id=1, replica_groups=mesh['row_hi'=8,'row_lo'=8,'col'=8] {'row_lo'}, dimensions={0} | all-to-all | bytes 262144 | tf_op jit(solution)/shard_map/all_to_all | solution.py:48
  204.1 1.0 reduce.2
  205.2 0.8 reshape.114
  206.1 3.7 %all-to-all-start.6 = ((f32[8,1,4096]{2,1,0:T(1,128)}), f32[8,1,4096]{2,1,0:T(1,128)S(1)}, u32[]{:S(2)}, u32[]{:S(2)}) async-start(f32[8,1,4096]{2,1,0:T(1,128)} %reshape.114), calls=%async_computation.6 | async-start | bytes 262144 | tf_op jit(solution)/shard_map/all_to_all | solution.py:48
  209.7 0.8 fusion.15
  210.6 8.2 %all-to-all-done.6 = f32[8,1,4096]{2,1,0:T(1,128)S(1)} async-done(((f32[8,1,4096]{2,1,0:T(1,128)}), f32[8,1,4096]{2,1,0:T(1,128)S(1)}, u32[]{:S(2)}, u32[]{:S(2)}) %all-to-all-start.6) | async-done | bytes 131104 | tf_op jit(solution)/shard_map/all_to_all | solution.py:48
  218.8 1.0 reduce.3
  219.9 0.7 pad_maximum_fusion.aug_ref
  220.6 6.8 %shard_map.103 = (f32[64,128]{1,0:T(8,128)}, f32[64,320]{1,0:T(8,128)}) custom-call(f32[64,320]{1,0:T(8,128)} %pad_maximum_fusion.aug_ref), custom_call_target="tpu_custom_call" | custom-call | tf_op jit(solution)/shard_map/pallas_call | solution.py:33
  227.5 1.6 slice.14
  (35 shorter events, 0.6 us)
Async XLA Ops:
  0.6 2.2 copy-start
  81.0 0.8 copy-start.2
  81.0 0.8 copy-start.3
  83.6 9.2 %copy-start.5 = (s32[1,1,64]{2,1,0:T(1,128)S(1)}, s32[1,1,64]{2,1,0:T(1,128)}, u32[]{:S(2)}) copy-start(s32[1,1,64]{2,1,0:T(1,128)} %param.11) | copy-start | bytes 772
  83.6 60.8 %all-to-all-start.1 = ((f32[64,64,128]{2,1,0:T(8,128)}), f32[64,64,128]{2,1,0:T(8,128)S(1)}, u32[]{:S(2)}, u32[]{:S(2)}) async-start(f32[64,64,128]{2,1,0:T(8,128)} %broadcast_in_dim.73), calls=%async_computation.1 | async-start | bytes 4194304 | tf_op jit(solution)/shard_map/all_to_all | solution.py:82
  147.0 17.6 %all-to-all-start.2 = ((f32[8,1,4096]{2,1,0:T(1,128)}), f32[8,1,4096]{2,1,0:T(1,128)S(1)}, u32[]{:S(2)}, u32[]{:S(2)}) async-start(f32[8,1,4096]{2,1,0:T(1,128)} %reshape.108), calls=%async_computation.2 | async-start | bytes 262144 | tf_op jit(solution)/shard_map/all_to_all | solution.py:48
  155.7 5.9 %copy-start.4 = (s32[1,1,64]{2,1,0:T(1,128)S(1)}, s32[1,1,64]{2,1,0:T(1,128)}, u32[]{:S(2)}) copy-start(s32[1,1,64]{2,1,0:T(1,128)} %param.10) | copy-start | bytes 772
  164.6 13.8 %all-to-all-start.3 = ((f32[8,64,256]{2,1,0:T(8,128)}), f32[8,64,256]{2,1,0:T(8,128)S(1)}, u32[]{:S(2)}, u32[]{:S(2)}) async-start(f32[8,64,256]{2,1,0:T(8,128)} %copy.19), calls=%async_computation.3 | async-start | bytes 1048576 | tf_op jit(solution)/shard_map/all_to_all | solution.py:94
  180.9 28.8 %copy-start.1 = (f32[64,128]{1,0:T(8,128)S(1)}, f32[64,128]{1,0:T(8,128)}, u32[]{:S(2)}) copy-start(f32[64,128]{1,0:T(8,128)} %get-tuple-element.9) | copy-start | bytes 98308
  206.1 12.8 %all-to-all-start.6 = ((f32[8,1,4096]{2,1,0:T(1,128)}), f32[8,1,4096]{2,1,0:T(1,128)S(1)}, u32[]{:S(2)}, u32[]{:S(2)}) async-start(f32[8,1,4096]{2,1,0:T(1,128)} %reshape.114), calls=%async_computation.6 | async-start | bytes 262144 | tf_op jit(solution)/shard_map/all_to_all | solution.py:48

commit v9 on v7

--- a/solution.py
+++ b/solution.py
@@ -84,9 +84,9 @@
     v_factor, v_inverse = cholesky_and_inverse(gram / total_cols)
     v_next = jnp.dot(v_inverse, pt_piece, precision=HIGH)
     factor = math.sqrt(total_rows / total_cols)
-    scaled = column * col_scale.reshape(n_row, 1, v_piece)
-    scaled = scaled.reshape(n_row, width, v_piece // tl, tl).transpose(0, 2, 1, 3)
-    chosen = jnp.take(scaled.reshape(cols_tiles, width, tl), cols_here, axis=0)
+    column_tiles = column.reshape(n_row, width, v_piece // tl, tl).transpose(0, 2, 1, 3)
+    chosen = jnp.take(column_tiles.reshape(cols_tiles, width, tl), cols_here, axis=0)
+    chosen = chosen * jnp.take(col_scale.reshape(cols_tiles, 1, tl), cols_here, axis=0)
     products = jnp.einsum("tsb,tab->tsa", chosen, local_tiles, precision=FAST)
     terms = jnp.einsum("tsa,tr->rsa", products, row_hits, precision=FAST)
     terms = terms.reshape(n_col, u_piece // tl, width, tl).transpose(0, 2, 1, 3)

time: 230 us -> 229 us (level)
  no operation moved by 1% of the time
where the time goes in v9:
time: 229 us; the launch traced here: 228 us
  blocking collectives  90.6 us (40%)
  waiting for transfers between devices  59 us (26%)
  starting transfers between devices  22.5 us (10%)
  matrix products  20.7 us (9%)
  Pallas kernels  13.3 us (6%)
  local copies, waits for them, and re-layouts  12.3 us (5%)
  other arithmetic  8.74 us (4%)
    all_to_all x1, blocking collectives, per_device(): received = lax.all_to_all(partial, ROW, 0, 0, tiled=True)  68.8 us
    all_to_all x1, waiting for transfers between devices, per_device(): column = lax.all_to_all(spread, ROW, 0, 0, tiled=True)  50.8 us
    all_to_all x2, blocking collectives, gather_sum(): lax.all_to_all(jnp.broadcast_to(x[None], (n,) + x.shape), axis, 0, 0, til...  21.9 us
    pallas_call x2, Pallas kernels, cholesky_and_inverse(): pl.pallas_call(_factor_kernel, out_shape=(jax.ShapeDtypeStruct(aug.shape,...  13.3 us
    all_to_all x1, starting transfers between devices, per_device(): column = lax.all_to_all(spread, ROW, 0, 0, tiled=True)  9.23 us
    all_to_all x2, starting transfers between devices, gather_sum(): lax.all_to_all(jnp.broadcast_to(x[None], (n,) + x.shape), axis, 0, 0, til...  8.51 us
    all_to_all x2, waiting for transfers between devices, gather_sum(): lax.all_to_all(jnp.broadcast_to(x[None], (n,) + x.shape), axis, 0, 0, til...  8.23 us
    dot_general x1, matrix products, per_device(): products = jnp.einsum('tsb,tab->tsa', chosen, local_tiles, precision=FAST)  7.02 us
  transfers between devices with their start and end apart: 4, of which 2 were waited for; matrix products, arithmetic and copies ran while one was open for 7% of the time, Pallas kernels for 3%

profile of v9, /device:TPU:2, one launch (start us, length us, event | category | flops | bytes accessed | tf_op | source)
XLA Modules:
  0.0 228.2 jit_solution(114033425715052806)
XLA Ops:
  0.6 0.8 select_reduce_fusion
  1.5 0.7 compare_and_fusion.2
  2.1 0.7 fusion.24
  2.8 0.8 exponential_bitcast_fusion
  3.7 0.7 gather_fusion
  4.3 5.4 %fusion.2 = f32[64,64,128]{2,1,0:T(8,128)} fusion(f32[1,1,64,128,128]{4,3,2,1,0:T(8,128)} %param.9, f32[64,64,128]{2,1,0:T(8,128)S(1)} %gather_fusion, pred[64]{0:T(512)(128)(4,1)S(1)} %compare_and_fusion.2), kind=kOutput, calls=%fused_computation.6 | convolution fusion | flops 403177472 | bytes 8388672 | tf_op jit(solution)/shard_map/tsa,tab->tsb/dot_general | solution.py:75
  9.7 2.3 gather_fusion.2
  12.0 0.2 select_multiply_fusion.2
  12.3 68.8 %all_to_all.35 = f32[64,64,128]{2,1,0:T(8,128)S(1)} all-to-all(f32[64,64,128]{2,1,0:T(8,128)S(1)} %select_multiply_fusion.2), channel_id=1, replica_groups=mesh['row_hi'=8,'row_lo'=8,'col'=8] {'row_hi','row_lo'}, dimensions={0} | all-to-all | bytes 4194304 | tf_op jit(solution)/shard_map/all_to_all | solution.py:79
  81.0 0.1 reduce_sum.64
  81.2 0.6 copy-done.2
  81.8 0.2 convolution_subtract_fusion.1
  82.0 1.6 broadcast_in_dim.83
  83.6 9.2 %all-to-all-start.1 = ((f32[64,64,128]{2,1,0:T(8,128)}), f32[64,64,128]{2,1,0:T(8,128)S(1)}, u32[]{:S(2)}, u32[]{:S(2)}) async-start(f32[64,64,128]{2,1,0:T(8,128)} %broadcast_in_dim.83), calls=%async_computation.1 | async-start | bytes 4194304 | tf_op jit(solution)/shard_map/all_to_all | solution.py:82
  92.8 0.6 gather_fusion.1
  93.6 50.8 %all-to-all-done.1 = f32[64,64,128]{2,1,0:T(8,128)S(1)} async-done(((f32[64,64,128]{2,1,0:T(8,128)}), f32[64,64,128]{2,1,0:T(8,128)S(1)}, u32[]{:S(2)}, u32[]{:S(2)}) %all-to-all-start.1) | async-done | bytes 2097184 | tf_op jit(solution)/shard_map/all_to_all | solution.py:82
  144.4 1.8 convolution_bitcast_fusion
  146.2 0.8 reshape.170
  147.0 4.8 %all-to-all-start.2 = ((f32[8,1,4096]{2,1,0:T(1,128)}), f32[8,1,4096]{2,1,0:T(1,128)S(1)}, u32[]{:S(2)}, u32[]{:S(2)}) async-start(f32[8,1,4096]{2,1,0:T(1,128)} %reshape.170), calls=%async_computation.2 | async-start | bytes 262144 | tf_op jit(solution)/shard_map/all_to_all | solution.py:48
  151.8 2.0 gather_fusion.3
  153.9 7.0 %fusion = f32[64,64,128]{2,1,0:T(8,128)S(1)} fusion(f32[1,1,64,128,128]{4,3,2,1,0:T(8,128)} %param.9, f32[64,64,128]{2,1,0:T(8,128)} %gather_fusion.3, f32[64,128]{1,0:T(8,128)S(1)} %broadcast_select_fusion, pred[64]{0:T(512)(128)(4,1)S(1)} %compare_and_fusion), kind=kOutput, calls=%fused_computation.4 | convolution fusion | flops 403701760 | bytes 8421440 | tf_op jit(solution)/shard_map/tsb,tab->tsa/dot_general | solution.py:90
  160.9 1.6 fusion.4
  162.5 0.4 reshape.169
  162.9 1.0 copy.19
  163.9 4.8 %all-to-all-start.3 = ((f32[8,64,256]{2,1,0:T(8,128)}), f32[8,64,256]{2,1,0:T(8,128)S(1)}, u32[]{:S(2)}, u32[]{:S(2)}) async-start(f32[8,64,256]{2,1,0:T(8,128)} %copy.19), calls=%async_computation.3 | async-start | bytes 1048576 | tf_op jit(solution)/shard_map/all_to_all | solution.py:94
  168.7 0.5 broadcast.89
  169.2 1.0 reduce
  170.2 0.1 reshape.171
  170.3 0.7 pad_maximum_fusion.aug_ref
  171.0 6.7 %shard_map.102 = (f32[64,128]{1,0:T(8,128)}, f32[64,128]{1,0:T(8,128)}) custom-call(f32[64,128]{1,0:T(8,128)} %pad_maximum_fusion.aug_ref), custom_call_target="tpu_custom_call" | custom-call | tf_op jit(solution)/shard_map/pallas_call | solution.py:33
  177.7 1.0 convolution_multiply_fusion
  178.8 1.0 convolution_subtract_fusion
  179.8 0.2 fusion.30
  180.0 0.2 reshape.172
  180.2 9.3 %all_to_all.36 = f32[8,1,4096]{2,1,0:T(1,128)S(1)} all-to-all(f32[8,1,4096]{2,1,0:T(1,128)S(1)} %reshape.172), channel_id=1, replica_groups=mesh['row_hi'=8,'row_lo'=8,'col'=8] {'col'}, dimensions={0} | all-to-all | bytes 262144 | tf_op jit(solution)/shard_map/all_to_all | solution.py:48
  189.5 1.0 reduce.1
  190.6 0.2 reshape.174
  190.8 12.6 %all_to_all.37 = f32[8,1,4096]{2,1,0:T(1,128)S(1)} all-to-all(f32[8,1,4096]{2,1,0:T(1,128)S(1)} %reshape.174), channel_id=1, replica_groups=mesh['row_hi'=8,'row_lo'=8,'col'=8] {'row_lo'}, dimensions={0} | all-to-all | bytes 262144 | tf_op jit(solution)/shard_map/all_to_all | solution.py:48
  203.4 1.0 reduce.2
  204.4 0.1 reshape.175
  204.5 0.8 reshape.176
  205.3 3.7 %all-to-all-start.6 = ((f32[8,1,4096]{2,1,0:T(1,128)}), f32[8,1,4096]{2,1,0:T(1,128)S(1)}, u32[]{:S(2)}, u32[]{:S(2)}) async-start(f32[8,1,4096]{2,1,0:T(1,128)} %reshape.176), calls=%async_computation.6 | async-start | bytes 262144 | tf_op jit(solution)/shard_map/all_to_all | solution.py:48
  209.0 0.8 fusion.17
  209.9 8.2 %all-to-all-done.6 = f32[8,1,4096]{2,1,0:T(1,128)S(1)} async-done(((f32[8,1,4096]{2,1,0:T(1,128)}), f32[8,1,4096]{2,1,0:T(1,128)S(1)}, u32[]{:S(2)}, u32[]{:S(2)}) %all-to-all-start.6) | async-done | bytes 131104 | tf_op jit(solution)/shard_map/all_to_all | solution.py:48
  218.1 1.0 reduce.3
  219.2 0.7 pad_maximum_fusion.1.aug_ref
  219.9 6.7 %shard_map.103 = (f32[64,128]{1,0:T(8,128)}, f32[64,128]{1,0:T(8,128)}) custom-call(f32[64,128]{1,0:T(8,128)} %pad_maximum_fusion.1.aug_ref), custom_call_target="tpu_custom_call" | custom-call | tf_op jit(solution)/shard_map/pallas_call | solution.py:33
  226.6 1.6 fusion.13
  (38 shorter events, 0.7 us)
Async XLA Ops:
  0.6 3.0 %copy-start = (f32[64,2048]{1,0:T(8,128)S(1)}, f32[64,2048]{1,0:T(8,128)}, u32[]{:S(2)}) copy-start(f32[64,2048]{1,0:T(8,128)} %param.13) | copy-start | bytes 1572868
  81.0 0.8 copy-start.2
  81.0 0.8 copy-start.3
  83.6 9.2 %copy-start.5 = (s32[1,1,64]{2,1,0:T(1,128)S(1)}, s32[1,1,64]{2,1,0:T(1,128)}, u32[]{:S(2)}) copy-start(s32[1,1,64]{2,1,0:T(1,128)} %param.11) | copy-start | bytes 772
  83.6 60.8 %all-to-all-start.1 = ((f32[64,64,128]{2,1,0:T(8,128)}), f32[64,64,128]{2,1,0:T(8,128)S(1)}, u32[]{:S(2)}, u32[]{:S(2)}) async-start(f32[64,64,128]{2,1,0:T(8,128)} %broadcast_in_dim.83), calls=%async_computation.1 | async-start | bytes 4194304 | tf_op jit(solution)/shard_map/all_to_all | solution.py:82
  147.0 16.9 %all-to-all-start.2 = ((f32[8,1,4096]{2,1,0:T(1,128)}), f32[8,1,4096]{2,1,0:T(1,128)S(1)}, u32[]{:S(2)}, u32[]{:S(2)}) async-start(f32[8,1,4096]{2,1,0:T(1,128)} %reshape.170), calls=%async_computation.2 | async-start | bytes 262144 | tf_op jit(solution)/shard_map/all_to_all | solution.py:48
  153.9 7.0 %copy-start.4 = (s32[1,1,64]{2,1,0:T(1,128)S(1)}, s32[1,1,64]{2,1,0:T(1,128)}, u32[]{:S(2)}) copy-start(s32[1,1,64]{2,1,0:T(1,128)} %param.10) | copy-start | bytes 772
  163.9 13.8 %all-to-all-start.3 = ((f32[8,64,256]{2,1,0:T(8,128)}), f32[8,64,256]{2,1,0:T(8,128)S(1)}, u32[]{:S(2)}, u32[]{:S(2)}) async-start(f32[8,64,256]{2,1,0:T(8,128)} %copy.19), calls=%async_computation.3 | async-start | bytes 1048576 | tf_op jit(solution)/shard_map/all_to_all | solution.py:94
  180.2 28.8 %copy-start.1 = (f32[64,128]{1,0:T(8,128)S(1)}, f32[64,128]{1,0:T(8,128)}, u32[]{:S(2)}) copy-start(f32[64,128]{1,0:T(8,128)} %get-tuple-element.9) | copy-start | bytes 98308
  205.3 12.8 %all-to-all-start.6 = ((f32[8,1,4096]{2,1,0:T(1,128)}), f32[8,1,4096]{2,1,0:T(1,128)S(1)}, u32[]{:S(2)}, u32[]{:S(2)}) async-start(f32[8,1,4096]{2,1,0:T(1,128)} %reshape.176), calls=%async_computation.6 | async-start | bytes 262144 | tf_op jit(solution)/shard_map/all_to_all | solution.py:48

commit v10 on v9

--- a/solution.py
+++ b/solution.py
@@ -65,9 +65,10 @@
     u_piece = block_rows // n_col
     col_scale = jnp.exp2(-exponents.astype(jnp.float32))
     lowtri = jnp.tril(prior)
-    row_hits = (rows_here[:, None] == jnp.arange(rows_tiles, dtype=jnp.int32)[None, :]).astype(
-        jnp.float32
-    )
+    tile_index = jnp.arange(count, dtype=jnp.int32)
+    earlier = (rows_here[:, None] == rows_here[None, :]) & (tile_index[None, :] < tile_index[:, None])
+    slot = rows_here * (count // rows_tiles) + jnp.sum(earlier.astype(jnp.int32), axis=1)
+    row_order = jnp.sum(jnp.where(slot[:, None] == tile_index[None, :], tile_index[:, None], 0), axis=0)
     col_match = cols_here[:, None] == jnp.arange(cols_tiles, dtype=jnp.int32)[None, :]
     order = jnp.sum(jnp.where(col_match, jnp.arange(count, dtype=jnp.int32)[:, None], 0), axis=0)
     u_tiles = u_basis.reshape(width, rows_tiles, tl).transpose(1, 0, 2)
@@ -88,12 +89,12 @@
     chosen = jnp.take(column_tiles.reshape(cols_tiles, width, tl), cols_here, axis=0)
     chosen = chosen * jnp.take(col_scale.reshape(cols_tiles, 1, tl), cols_here, axis=0)
     products = jnp.einsum("tsb,tab->tsa", chosen, local_tiles, precision=FAST)
-    terms = jnp.einsum("tsa,tr->rsa", products, row_hits, precision=FAST)
-    terms = terms.reshape(n_col, u_piece // tl, width, tl).transpose(0, 2, 1, 3)
-    terms = terms.reshape(n_col, width, u_piece)
-    summed = lax.all_to_all(terms, "col", 0, 0, tiled=True).sum(0)
+    reps = count // rows_tiles
+    terms = jnp.take(products, row_order, axis=0).reshape(rows_tiles, reps, width, tl).sum(1)
+    received_terms = lax.all_to_all(terms, "col", 0, 0, tiled=True)
+    summed = received_terms.reshape(n_col, u_piece // tl, width, tl).sum(0)
     u_own = lax.dynamic_slice_in_dim(u_basis, lax.axis_index("col") * u_piece, u_piece, 1)
-    qt_piece = factor * jnp.dot(v_inverse, summed, precision=HIGH) - jnp.dot(v_factor.T, u_own, precision=HIGH)
+    qt_piece = factor * jnp.einsum("ij,rjb->irb", v_inverse, summed, precision=HIGH).reshape(width, u_piece) - jnp.dot(v_factor.T, u_own, precision=HIGH)
     ugram = jnp.dot(qt_piece, qt_piece.T, precision=HIGH)
     ugram = gather_sum(gather_sum(gather_sum(ugram, "col"), "row_lo"), "row_hi")
     u_factor, u_inverse = cholesky_and_inverse(ugram / total_rows)

time: 229 us -> 231 us (level)
  transfers between devices with their start and end apart: 4 -> 4, of which waited for: 2 -> 2; matrix products, arithmetic and copies ran while one was open for 7% -> 8% of each run, Pallas kernels for 3% -> 3%
where the time goes in v10:
time: 231 us; the launch traced here: 230 us
  blocking collectives  90.6 us (39%)
  waiting for transfers between devices  58.7 us (25%)
  starting transfers between devices  22.5 us (10%)
  matrix products  20.4 us (9%)
  Pallas kernels  13.3 us (6%)
  local copies, waits for them, and re-layouts  13.2 us (6%)
  other arithmetic  10.1 us (4%)
    all_to_all x1, blocking collectives, per_device(): received = lax.all_to_all(partial, ROW, 0, 0, tiled=True)  68.8 us
    all_to_all x1, waiting for transfers between devices, per_device(): column = lax.all_to_all(spread, ROW, 0, 0, tiled=True)  50.5 us
    all_to_all x2, blocking collectives, gather_sum(): lax.all_to_all(jnp.broadcast_to(x[None], (n,) + x.shape), axis, 0, 0, til...  21.9 us
    pallas_call x2, Pallas kernels, cholesky_and_inverse(): pl.pallas_call(_factor_kernel, out_shape=(jax.ShapeDtypeStruct(aug.shape,...  13.3 us
    all_to_all x1, starting transfers between devices, per_device(): column = lax.all_to_all(spread, ROW, 0, 0, tiled=True)  9.23 us
    all_to_all x2, starting transfers between devices, gather_sum(): lax.all_to_all(jnp.broadcast_to(x[None], (n,) + x.shape), axis, 0, 0, til...  8.51 us
    dot_general x1, matrix products, per_device(): products = jnp.einsum('tsb,tab->tsa', chosen, local_tiles, precision=FAST)  8.31 us
    all_to_all x2, waiting for transfers between devices, gather_sum(): lax.all_to_all(jnp.broadcast_to(x[None], (n,) + x.shape), axis, 0, 0, til...  8.23 us
  transfers between devices with their start and end apart: 4, of which 2 were waited for; matrix products, arithmetic and copies ran while one was open for 8% of the time, Pallas kernels for 3%

profile of v10, /device:TPU:2, one launch (start us, length us, event | category | flops | bytes accessed | tf_op | source)
XLA Modules:
  0.0 229.8 jit_solution(11536757395937559348)
XLA Ops:
  0.6 0.8 select_reduce_fusion.1
  1.5 0.7 compare_and_fusion.3
  2.1 0.7 fusion.22
  2.8 0.8 exponential_bitcast_fusion
  3.7 0.7 gather_fusion
  4.3 5.4 %fusion.2 = f32[64,64,128]{2,1,0:T(8,128)} fusion(f32[1,1,64,128,128]{4,3,2,1,0:T(8,128)} %param.9, f32[64,64,128]{2,1,0:T(8,128)S(1)} %gather_fusion, pred[64]{0:T(512)(128)(4,1)S(1)} %compare_and_fusion.3), kind=kOutput, calls=%fused_computation.7 | convolution fusion | flops 403177472 | bytes 8388672 | tf_op jit(solution)/shard_map/tsa,tab->tsb/dot_general | solution.py:76
  9.7 2.3 gather_fusion.2
  12.0 0.2 select_multiply_fusion.2
  12.3 68.8 %all_to_all.35 = f32[64,64,128]{2,1,0:T(8,128)S(1)} all-to-all(f32[64,64,128]{2,1,0:T(8,128)S(1)} %select_multiply_fusion.2), channel_id=1, replica_groups=mesh['row_hi'=8,'row_lo'=8,'col'=8] {'row_hi','row_lo'}, dimensions={0} | all-to-all | bytes 4194304 | tf_op jit(solution)/shard_map/all_to_all | solution.py:80
  81.0 0.1 reduce_sum.91
  81.2 0.6 copy-done.2
  81.8 0.2 convolution_subtract_fusion.1
  82.0 1.6 broadcast_in_dim.95
  83.6 9.2 %all-to-all-start.1 = ((f32[64,64,128]{2,1,0:T(8,128)}), f32[64,64,128]{2,1,0:T(8,128)S(1)}, u32[]{:S(2)}, u32[]{:S(2)}) async-start(f32[64,64,128]{2,1,0:T(8,128)} %broadcast_in_dim.95), calls=%async_computation.1 | async-start | bytes 4194304 | tf_op jit(solution)/shard_map/all_to_all | solution.py:83
  92.8 0.6 gather_fusion.1
  93.5 0.2 convert_reduce_fusion
  93.9 50.5 %all-to-all-done.1 = f32[64,64,128]{2,1,0:T(8,128)S(1)} async-done(((f32[64,64,128]{2,1,0:T(8,128)}), f32[64,64,128]{2,1,0:T(8,128)S(1)}, u32[]{:S(2)}, u32[]{:S(2)}) %all-to-all-start.1) | async-done | bytes 2097184 | tf_op jit(solution)/shard_map/all_to_all | solution.py:83
  144.4 1.8 convolution_bitcast_fusion
  146.2 0.8 reshape.190
  147.0 4.8 %all-to-all-start.2 = ((f32[8,1,4096]{2,1,0:T(1,128)}), f32[8,1,4096]{2,1,0:T(1,128)S(1)}, u32[]{:S(2)}, u32[]{:S(2)}) async-start(f32[8,1,4096]{2,1,0:T(1,128)} %reshape.190), calls=%async_computation.2 | async-start | bytes 262144 | tf_op jit(solution)/shard_map/all_to_all | solution.py:48
  151.8 2.0 gather_fusion.3
  153.9 8.3 %fusion = f32[64,64,128]{2,1,0:T(8,128)} fusion(f32[1,1,64,128,128]{4,3,2,1,0:T(8,128)} %param.9, f32[64,64,128]{2,1,0:T(8,128)} %gather_fusion.3, f32[64,128]{1,0:T(8,128)S(1)} %broadcast_select_fusion.1, pred[64]{0:T(512)(128)(4,1)S(1)} %compare_and_fusion.1), kind=kOutput, calls=%fused_computation.5 | convolution fusion | flops 403701760 | bytes 8421440 | tf_op jit(solution)/shard_map/tsb,tab->tsa/dot_general | solution.py:91
  162.2 2.3 gather_fusion.4
  164.4 1.1 bitcast_reduce_fusion
  165.5 4.8 %all-to-all-start.3 = ((f32[16,64,128]{2,1,0:T(8,128)}), f32[16,64,128]{2,1,0:T(8,128)S(1)}, u32[]{:S(2)}, u32[]{:S(2)}) async-start(f32[16,64,128]{2,1,0:T(8,128)} %bitcast_reduce_fusion), calls=%async_computation.3 | async-start | bytes 1048576 | tf_op jit(solution)/shard_map/all_to_all | solution.py:94
  170.3 0.5 broadcast.97
  170.8 1.0 reduce
  171.8 0.1 reshape.191
  171.9 0.7 pad_maximum_fusion.aug_ref
  172.6 6.7 %shard_map.102 = (f32[64,128]{1,0:T(8,128)}, f32[64,128]{1,0:T(8,128)}) custom-call(f32[64,128]{1,0:T(8,128)} %pad_maximum_fusion.aug_ref), custom_call_target="tpu_custom_call" | custom-call | tf_op jit(solution)/shard_map/pallas_call | solution.py:33
  179.3 1.0 convolution_multiply_fusion
  180.4 1.0 convolution_subtract_fusion
  181.4 0.2 fusion.28
  181.6 0.2 reshape.192
  181.8 9.3 %all_to_all.36 = f32[8,1,4096]{2,1,0:T(1,128)S(1)} all-to-all(f32[8,1,4096]{2,1,0:T(1,128)S(1)} %reshape.192), channel_id=1, replica_groups=mesh['row_hi'=8,'row_lo'=8,'col'=8] {'col'}, dimensions={0} | all-to-all | bytes 262144 | tf_op jit(solution)/shard_map/all_to_all | solution.py:48
  191.1 1.0 reduce.1
  192.1 0.1 reshape.193
  192.2 0.2 reshape.194
  192.4 12.6 %all_to_all.37 = f32[8,1,4096]{2,1,0:T(1,128)S(1)} all-to-all(f32[8,1,4096]{2,1,0:T(1,128)S(1)} %reshape.194), channel_id=1, replica_groups=mesh['row_hi'=8,'row_lo'=8,'col'=8] {'row_lo'}, dimensions={0} | all-to-all | bytes 262144 | tf_op jit(solution)/shard_map/all_to_all | solution.py:48
  205.0 1.0 reduce.2
  206.1 0.8 reshape.196
  206.9 3.7 %all-to-all-start.6 = ((f32[8,1,4096]{2,1,0:T(1,128)}), f32[8,1,4096]{2,1,0:T(1,128)S(1)}, u32[]{:S(2)}, u32[]{:S(2)}) async-start(f32[8,1,4096]{2,1,0:T(1,128)} %reshape.196), calls=%async_computation.6 | async-start | bytes 262144 | tf_op jit(solution)/shard_map/all_to_all | solution.py:48
  210.6 0.8 fusion.18
  211.5 8.2 %all-to-all-done.6 = f32[8,1,4096]{2,1,0:T(1,128)S(1)} async-done(((f32[8,1,4096]{2,1,0:T(1,128)}), f32[8,1,4096]{2,1,0:T(1,128)S(1)}, u32[]{:S(2)}, u32[]{:S(2)}) %all-to-all-start.6) | async-done | bytes 131104 | tf_op jit(solution)/shard_map/all_to_all | solution.py:48
  219.7 1.0 reduce.3
  220.8 0.7 pad_maximum_fusion.1.aug_ref
  221.5 6.7 %shard_map.103 = (f32[64,128]{1,0:T(8,128)}, f32[64,128]{1,0:T(8,128)}) custom-call(f32[64,128]{1,0:T(8,128)} %pad_maximum_fusion.1.aug_ref), custom_call_target="tpu_custom_call" | custom-call | tf_op jit(solution)/shard_map/pallas_call | solution.py:33
  228.2 1.6 fusion.13
  (43 shorter events, 0.8 us)
Async XLA Ops:
  0.6 3.0 %copy-start = (f32[64,2048]{1,0:T(8,128)S(1)}, f32[64,2048]{1,0:T(8,128)}, u32[]{:S(2)}) copy-start(f32[64,2048]{1,0:T(8,128)} %param.13) | copy-start | bytes 1572868
  81.0 0.8 copy-start.2
  81.0 0.8 copy-start.3
  83.6 9.2 %copy-start.5 = (s32[1,1,64]{2,1,0:T(1,128)S(1)}, s32[1,1,64]{2,1,0:T(1,128)}, u32[]{:S(2)}) copy-start(s32[1,1,64]{2,1,0:T(1,128)} %param.11) | copy-start | bytes 772
  83.6 9.9 %copy-start.4 = (s32[1,1,64]{2,1,0:T(1,128)S(1)}, s32[1,1,64]{2,1,0:T(1,128)}, u32[]{:S(2)}) copy-start(s32[1,1,64]{2,1,0:T(1,128)} %param.10) | copy-start | bytes 772
  83.6 60.8 %all-to-all-start.1 = ((f32[64,64,128]{2,1,0:T(8,128)}), f32[64,64,128]{2,1,0:T(8,128)S(1)}, u32[]{:S(2)}, u32[]{:S(2)}) async-start(f32[64,64,128]{2,1,0:T(8,128)} %broadcast_in_dim.95), calls=%async_computation.1 | async-start | bytes 4194304 | tf_op jit(solution)/shard_map/all_to_all | solution.py:83
  147.0 18.5 %all-to-all-start.2 = ((f32[8,1,4096]{2,1,0:T(1,128)}), f32[8,1,4096]{2,1,0:T(1,128)S(1)}, u32[]{:S(2)}, u32[]{:S(2)}) async-start(f32[8,1,4096]{2,1,0:T(1,128)} %reshape.190), calls=%async_computation.2 | async-start | bytes 262144 | tf_op jit(solution)/shard_map/all_to_all | solution.py:48
  165.5 13.8 %all-to-all-start.3 = ((f32[16,64,128]{2,1,0:T(8,128)}), f32[16,64,128]{2,1,0:T(8,128)S(1)}, u32[]{:S(2)}, u32[]{:S(2)}) async-start(f32[16,64,128]{2,1,0:T(8,128)} %bitcast_reduce_fusion), calls=%async_computation.3 | async-start | bytes 1048576 | tf_op jit(solution)/shard_map/all_to_all | solution.py:94
  181.8 28.8 %copy-start.1 = (f32[64,128]{1,0:T(8,128)S(1)}, f32[64,128]{1,0:T(8,128)}, u32[]{:S(2)}) copy-start(f32[64,128]{1,0:T(8,128)} %get-tuple-element.9) | copy-start | bytes 98308
  206.9 12.8 %all-to-all-start.6 = ((f32[8,1,4096]{2,1,0:T(1,128)}), f32[8,1,4096]{2,1,0:T(1,128)S(1)}, u32[]{:S(2)}, u32[]{:S(2)}) async-start(f32[8,1,4096]{2,1,0:T(1,128)} %reshape.196), calls=%async_computation.6 | async-start | bytes 262144 | tf_op jit(solution)/shard_map/all_to_all | solution.py:48

commit v11 on v9

--- a/solution.py
+++ b/solution.py
@@ -80,7 +80,7 @@
     pt_piece = received.sum(0) - jnp.dot(lowtri, v_basis, precision=HIGH)
     spread = jnp.broadcast_to(pt_piece[None], (n_row, width, v_piece))
     column = lax.all_to_all(spread, ROW, 0, 0, tiled=True)
-    gram = gather_sum(jnp.einsum("jsb,jtb->st", column, column, precision=HIGH), "col")
+    gram = gather_sum(jnp.einsum("jsb,jtb->st", column, column, precision=FAST), "col")
     v_factor, v_inverse = cholesky_and_inverse(gram / total_cols)
     v_next = jnp.dot(v_inverse, pt_piece, precision=HIGH)
     factor = math.sqrt(total_rows / total_cols)

time: 229 us -> 229 us (level)
  no operation moved by 1% of the time
where the time goes in v11:
time: 229 us; the launch traced here: 227 us
  blocking collectives  90.7 us (40%)
  waiting for transfers between devices  59 us (26%)
  starting transfers between devices  22.5 us (10%)
  matrix products  19.9 us (9%)
  Pallas kernels  13.3 us (6%)
  local copies, waits for them, and re-layouts  12.3 us (5%)
  other arithmetic  8.74 us (4%)
    all_to_all x1, blocking collectives, per_device(): received = lax.all_to_all(partial, ROW, 0, 0, tiled=True)  68.8 us
    all_to_all x1, waiting for transfers between devices, per_device(): column = lax.all_to_all(spread, ROW, 0, 0, tiled=True)  50.8 us
    all_to_all x2, blocking collectives, gather_sum(): lax.all_to_all(jnp.broadcast_to(x[None], (n,) + x.shape), axis, 0, 0, til...  21.9 us
    pallas_call x2, Pallas kernels, cholesky_and_inverse(): pl.pallas_call(_factor_kernel, out_shape=(jax.ShapeDtypeStruct(aug.shape,...  13.3 us
    all_to_all x1, starting transfers between devices, per_device(): column = lax.all_to_all(spread, ROW, 0, 0, tiled=True)  9.23 us
    all_to_all x2, starting transfers between devices, gather_sum(): lax.all_to_all(jnp.broadcast_to(x[None], (n,) + x.shape), axis, 0, 0, til...  8.5 us
    all_to_all x2, waiting for transfers between devices, gather_sum(): lax.all_to_all(jnp.broadcast_to(x[None], (n,) + x.shape), axis, 0, 0, til...  8.23 us
    dot_general x1, matrix products, per_device(): products = jnp.einsum('tsb,tab->tsa', chosen, local_tiles, precision=FAST)  7.02 us
  transfers between devices with their start and end apart: 4, of which 2 were waited for; matrix products, arithmetic and copies ran while one was open for 7% of the time, Pallas kernels for 3%

profile of v11, /device:TPU:2, one launch (start us, length us, event | category | flops | bytes accessed | tf_op | source)
XLA Modules:
  0.0 227.4 jit_solution(976602624457519630)
XLA Ops:
  0.6 0.8 select_reduce_fusion
  1.5 0.7 compare_and_fusion.2
  2.1 0.7 fusion.24
  2.8 0.8 exponential_bitcast_fusion
  3.7 0.7 gather_fusion
  4.3 5.4 %fusion.2 = f32[64,64,128]{2,1,0:T(8,128)} fusion(f32[1,1,64,128,128]{4,3,2,1,0:T(8,128)} %param.9, f32[64,64,128]{2,1,0:T(8,128)S(1)} %gather_fusion, pred[64]{0:T(512)(128)(4,1)S(1)} %compare_and_fusion.2), kind=kOutput, calls=%fused_computation.6 | convolution fusion | flops 403177472 | bytes 8388672 | tf_op jit(solution)/shard_map/tsa,tab->tsb/dot_general | solution.py:75
  9.7 2.3 gather_fusion.2
  12.0 0.2 select_multiply_fusion.2
  12.3 68.8 %all_to_all.35 = f32[64,64,128]{2,1,0:T(8,128)S(1)} all-to-all(f32[64,64,128]{2,1,0:T(8,128)S(1)} %select_multiply_fusion.2), channel_id=1, replica_groups=mesh['row_hi'=8,'row_lo'=8,'col'=8] {'row_hi','row_lo'}, dimensions={0} | all-to-all | bytes 4194304 | tf_op jit(solution)/shard_map/all_to_all | solution.py:79
  81.0 0.1 reduce_sum.64
  81.2 0.6 copy-done.2
  81.8 0.2 convolution_subtract_fusion.1
  82.0 1.6 broadcast_in_dim.83
  83.6 9.2 %all-to-all-start.1 = ((f32[64,64,128]{2,1,0:T(8,128)}), f32[64,64,128]{2,1,0:T(8,128)S(1)}, u32[]{:S(2)}, u32[]{:S(2)}) async-start(f32[64,64,128]{2,1,0:T(8,128)} %broadcast_in_dim.83), calls=%async_computation.1 | async-start | bytes 4194304 | tf_op jit(solution)/shard_map/all_to_all | solution.py:82
  92.8 0.6 gather_fusion.1
  93.5 50.8 %all-to-all-done.1 = f32[64,64,128]{2,1,0:T(8,128)S(1)} async-done(((f32[64,64,128]{2,1,0:T(8,128)}), f32[64,64,128]{2,1,0:T(8,128)S(1)}, u32[]{:S(2)}, u32[]{:S(2)}) %all-to-all-start.1) | async-done | bytes 2097184 | tf_op jit(solution)/shard_map/all_to_all | solution.py:82
  144.4 1.0 convolution_bitcast_fusion
  145.4 0.8 reshape.170
  146.2 4.8 %all-to-all-start.2 = ((f32[8,1,4096]{2,1,0:T(1,128)}), f32[8,1,4096]{2,1,0:T(1,128)S(1)}, u32[]{:S(2)}, u32[]{:S(2)}) async-start(f32[8,1,4096]{2,1,0:T(1,128)} %reshape.170), calls=%async_computation.2 | async-start | bytes 262144 | tf_op jit(solution)/shard_map/all_to_all | solution.py:48
  151.0 2.0 gather_fusion.3
  153.1 7.0 %fusion = f32[64,64,128]{2,1,0:T(8,128)S(1)} fusion(f32[1,1,64,128,128]{4,3,2,1,0:T(8,128)} %param.9, f32[64,64,128]{2,1,0:T(8,128)} %gather_fusion.3, f32[64,128]{1,0:T(8,128)S(1)} %broadcast_select_fusion, pred[64]{0:T(512)(128)(4,1)S(1)} %compare_and_fusion), kind=kOutput, calls=%fused_computation.4 | convolution fusion | flops 403701760 | bytes 8421440 | tf_op jit(solution)/shard_map/tsb,tab->tsa/dot_general | solution.py:90
  160.1 1.6 fusion.4
  161.7 0.4 reshape.169
  162.1 1.0 copy.19
  163.1 4.8 %all-to-all-start.3 = ((f32[8,64,256]{2,1,0:T(8,128)}), f32[8,64,256]{2,1,0:T(8,128)S(1)}, u32[]{:S(2)}, u32[]{:S(2)}) async-start(f32[8,64,256]{2,1,0:T(8,128)} %copy.19), calls=%async_computation.3 | async-start | bytes 1048576 | tf_op jit(solution)/shard_map/all_to_all | solution.py:94
  167.9 0.5 broadcast.89
  168.4 1.0 reduce
  169.5 0.7 pad_maximum_fusion.aug_ref
  170.2 6.7 %shard_map.102 = (f32[64,128]{1,0:T(8,128)}, f32[64,128]{1,0:T(8,128)}) custom-call(f32[64,128]{1,0:T(8,128)} %pad_maximum_fusion.aug_ref), custom_call_target="tpu_custom_call" | custom-call | tf_op jit(solution)/shard_map/pallas_call | solution.py:33
  176.9 1.0 convolution_multiply_fusion
  177.9 1.0 convolution_subtract_fusion
  179.0 0.2 fusion.30
  179.2 0.2 reshape.172
  179.4 9.3 %all_to_all.36 = f32[8,1,4096]{2,1,0:T(1,128)S(1)} all-to-all(f32[8,1,4096]{2,1,0:T(1,128)S(1)} %reshape.172), channel_id=1, replica_groups=mesh['row_hi'=8,'row_lo'=8,'col'=8] {'col'}, dimensions={0} | all-to-all | bytes 262144 | tf_op jit(solution)/shard_map/all_to_all | solution.py:48
  188.7 1.0 reduce.1
  189.8 0.2 reshape.174
  190.0 12.6 %all_to_all.37 = f32[8,1,4096]{2,1,0:T(1,128)S(1)} all-to-all(f32[8,1,4096]{2,1,0:T(1,128)S(1)} %reshape.174), channel_id=1, replica_groups=mesh['row_hi'=8,'row_lo'=8,'col'=8] {'row_lo'}, dimensions={0} | all-to-all | bytes 262144 | tf_op jit(solution)/shard_map/all_to_all | solution.py:48
  202.6 1.0 reduce.2
  203.6 0.1 reshape.175
  203.7 0.8 reshape.176
  204.5 3.7 %all-to-all-start.6 = ((f32[8,1,4096]{2,1,0:T(1,128)}), f32[8,1,4096]{2,1,0:T(1,128)S(1)}, u32[]{:S(2)}, u32[]{:S(2)}) async-start(f32[8,1,4096]{2,1,0:T(1,128)} %reshape.176), calls=%async_computation.6 | async-start | bytes 262144 | tf_op jit(solution)/shard_map/all_to_all | solution.py:48
  208.2 0.8 fusion.17
  209.1 8.2 %all-to-all-done.6 = f32[8,1,4096]{2,1,0:T(1,128)S(1)} async-done(((f32[8,1,4096]{2,1,0:T(1,128)}), f32[8,1,4096]{2,1,0:T(1,128)S(1)}, u32[]{:S(2)}, u32[]{:S(2)}) %all-to-all-start.6) | async-done | bytes 131104 | tf_op jit(solution)/shard_map/all_to_all | solution.py:48
  217.3 1.0 reduce.3
  218.3 0.1 reshape.177
  218.4 0.7 pad_maximum_fusion.1.aug_ref
  219.1 6.7 %shard_map.103 = (f32[64,128]{1,0:T(8,128)}, f32[64,128]{1,0:T(8,128)}) custom-call(f32[64,128]{1,0:T(8,128)} %pad_maximum_fusion.1.aug_ref), custom_call_target="tpu_custom_call" | custom-call | tf_op jit(solution)/shard_map/pallas_call | solution.py:33
  225.8 1.6 fusion.13
  (38 shorter events, 0.7 us)
Async XLA Ops:
  0.6 3.0 %copy-start = (f32[64,2048]{1,0:T(8,128)S(1)}, f32[64,2048]{1,0:T(8,128)}, u32[]{:S(2)}) copy-start(f32[64,2048]{1,0:T(8,128)} %param.13) | copy-start | bytes 1572868
  81.0 0.8 copy-start.2
  81.0 0.8 copy-start.3
  83.6 9.2 %copy-start.5 = (s32[1,1,64]{2,1,0:T(1,128)S(1)}, s32[1,1,64]{2,1,0:T(1,128)}, u32[]{:S(2)}) copy-start(s32[1,1,64]{2,1,0:T(1,128)} %param.11) | copy-start | bytes 772
  83.6 60.8 %all-to-all-start.1 = ((f32[64,64,128]{2,1,0:T(8,128)}), f32[64,64,128]{2,1,0:T(8,128)S(1)}, u32[]{:S(2)}, u32[]{:S(2)}) async-start(f32[64,64,128]{2,1,0:T(8,128)} %broadcast_in_dim.83), calls=%async_computation.1 | async-start | bytes 4194304 | tf_op jit(solution)/shard_map/all_to_all | solution.py:82
  146.2 16.9 %all-to-all-start.2 = ((f32[8,1,4096]{2,1,0:T(1,128)}), f32[8,1,4096]{2,1,0:T(1,128)S(1)}, u32[]{:S(2)}, u32[]{:S(2)}) async-start(f32[8,1,4096]{2,1,0:T(1,128)} %reshape.170), calls=%async_computation.2 | async-start | bytes 262144 | tf_op jit(solution)/shard_map/all_to_all | solution.py:48
  153.1 7.0 %copy-start.4 = (s32[1,1,64]{2,1,0:T(1,128)S(1)}, s32[1,1,64]{2,1,0:T(1,128)}, u32[]{:S(2)}) copy-start(s32[1,1,64]{2,1,0:T(1,128)} %param.10) | copy-start | bytes 772
  163.1 13.8 %all-to-all-start.3 = ((f32[8,64,256]{2,1,0:T(8,128)}), f32[8,64,256]{2,1,0:T(8,128)S(1)}, u32[]{:S(2)}, u32[]{:S(2)}) async-start(f32[8,64,256]{2,1,0:T(8,128)} %copy.19), calls=%async_computation.3 | async-start | bytes 1048576 | tf_op jit(solution)/shard_map/all_to_all | solution.py:94
  179.4 28.8 %copy-start.1 = (f32[64,128]{1,0:T(8,128)S(1)}, f32[64,128]{1,0:T(8,128)}, u32[]{:S(2)}) copy-start(f32[64,128]{1,0:T(8,128)} %get-tuple-element.9) | copy-start | bytes 98308
  204.5 12.8 %all-to-all-start.6 = ((f32[8,1,4096]{2,1,0:T(1,128)}), f32[8,1,4096]{2,1,0:T(1,128)S(1)}, u32[]{:S(2)}, u32[]{:S(2)}) async-start(f32[8,1,4096]{2,1,0:T(1,128)} %reshape.176), calls=%async_computation.6 | async-start | bytes 262144 | tf_op jit(solution)/shard_map/all_to_all | solution.py:48

commit v12 on v11

--- a/solution.py
+++ b/solution.py
@@ -93,8 +93,8 @@
     terms = terms.reshape(n_col, width, u_piece)
     summed = lax.all_to_all(terms, "col", 0, 0, tiled=True).sum(0)
     u_own = lax.dynamic_slice_in_dim(u_basis, lax.axis_index("col") * u_piece, u_piece, 1)
-    qt_piece = factor * jnp.dot(v_inverse, summed, precision=HIGH) - jnp.dot(v_factor.T, u_own, precision=HIGH)
-    ugram = jnp.dot(qt_piece, qt_piece.T, precision=HIGH)
+    qt_piece = factor * jnp.dot(v_inverse, summed, precision=FAST) - jnp.dot(v_factor.T, u_own, precision=FAST)
+    ugram = jnp.dot(qt_piece, qt_piece.T, precision=FAST)
     ugram = gather_sum(gather_sum(gather_sum(ugram, "col"), "row_lo"), "row_hi")
     u_factor, u_inverse = cholesky_and_inverse(ugram / total_rows)
     u_next = jnp.dot(u_inverse, qt_piece, precision=HIGH)

time: 229 us -> 229 us (level)
  no operation moved by 1% of the time
where the time goes in v12:
time: 229 us; the launch traced here: 227 us
  blocking collectives  90.7 us (40%)
  waiting for transfers between devices  59 us (26%)
  starting transfers between devices  22.5 us (10%)
  matrix products  19.8 us (9%)
  Pallas kernels  13.3 us (6%)
  local copies, waits for them, and re-layouts  12.3 us (5%)
  other arithmetic  8.74 us (4%)
    all_to_all x1, blocking collectives, per_device(): received = lax.all_to_all(partial, ROW, 0, 0, tiled=True)  68.8 us
    all_to_all x1, waiting for transfers between devices, per_device(): column = lax.all_to_all(spread, ROW, 0, 0, tiled=True)  50.8 us
    all_to_all x2, blocking collectives, gather_sum(): lax.all_to_all(jnp.broadcast_to(x[None], (n,) + x.shape), axis, 0, 0, til...  21.9 us
    pallas_call x2, Pallas kernels, cholesky_and_inverse(): pl.pallas_call(_factor_kernel, out_shape=(jax.ShapeDtypeStruct(aug.shape,...  13.3 us
    all_to_all x1, starting transfers between devices, per_device(): column = lax.all_to_all(spread, ROW, 0, 0, tiled=True)  9.23 us
    all_to_all x2, starting transfers between devices, gather_sum(): lax.all_to_all(jnp.broadcast_to(x[None], (n,) + x.shape), axis, 0, 0, til...  8.5 us
    all_to_all x2, waiting for transfers between devices, gather_sum(): lax.all_to_all(jnp.broadcast_to(x[None], (n,) + x.shape), axis, 0, 0, til...  8.23 us
    dot_general x1, matrix products, per_device(): products = jnp.einsum('tsb,tab->tsa', chosen, local_tiles, precision=FAST)  7.02 us
  transfers between devices with their start and end apart: 4, of which 2 were waited for; matrix products, arithmetic and copies ran while one was open for 7% of the time, Pallas kernels for 3%

profile of v12, /device:TPU:2, one launch (start us, length us, event | category | flops | bytes accessed | tf_op | source)
XLA Modules:
  0.0 227.3 jit_solution(15578757921918364278)
XLA Ops:
  0.6 0.8 select_reduce_fusion
  1.5 0.7 compare_and_fusion.2
  2.1 0.7 fusion.24
  2.8 0.8 exponential_bitcast_fusion
  3.7 0.7 gather_fusion
  4.3 5.4 %fusion.2 = f32[64,64,128]{2,1,0:T(8,128)} fusion(f32[1,1,64,128,128]{4,3,2,1,0:T(8,128)} %param.9, f32[64,64,128]{2,1,0:T(8,128)S(1)} %gather_fusion, pred[64]{0:T(512)(128)(4,1)S(1)} %compare_and_fusion.2), kind=kOutput, calls=%fused_computation.6 | convolution fusion | flops 403177472 | bytes 8388672 | tf_op jit(solution)/shard_map/tsa,tab->tsb/dot_general | solution.py:75
  9.7 2.3 gather_fusion.2
  12.0 0.2 select_multiply_fusion.2
  12.3 68.8 %all_to_all.35 = f32[64,64,128]{2,1,0:T(8,128)S(1)} all-to-all(f32[64,64,128]{2,1,0:T(8,128)S(1)} %select_multiply_fusion.2), channel_id=1, replica_groups=mesh['row_hi'=8,'row_lo'=8,'col'=8] {'row_hi','row_lo'}, dimensions={0} | all-to-all | bytes 4194304 | tf_op jit(solution)/shard_map/all_to_all | solution.py:79
  81.0 0.1 reduce_sum.64
  81.2 0.6 copy-done.2
  81.8 0.2 convolution_subtract_fusion.1
  82.0 1.6 broadcast_in_dim.83
  83.6 9.2 %all-to-all-start.1 = ((f32[64,64,128]{2,1,0:T(8,128)}), f32[64,64,128]{2,1,0:T(8,128)S(1)}, u32[]{:S(2)}, u32[]{:S(2)}) async-start(f32[64,64,128]{2,1,0:T(8,128)} %broadcast_in_dim.83), calls=%async_computation.1 | async-start | bytes 4194304 | tf_op jit(solution)/shard_map/all_to_all | solution.py:82
  92.8 0.6 gather_fusion.1
  93.5 50.8 %all-to-all-done.1 = f32[64,64,128]{2,1,0:T(8,128)S(1)} async-done(((f32[64,64,128]{2,1,0:T(8,128)}), f32[64,64,128]{2,1,0:T(8,128)S(1)}, u32[]{:S(2)}, u32[]{:S(2)}) %all-to-all-start.1) | async-done | bytes 2097184 | tf_op jit(solution)/shard_map/all_to_all | solution.py:82
  144.4 1.0 convolution_bitcast_fusion
  145.4 0.8 reshape.170
  146.2 4.8 %all-to-all-start.2 = ((f32[8,1,4096]{2,1,0:T(1,128)}), f32[8,1,4096]{2,1,0:T(1,128)S(1)}, u32[]{:S(2)}, u32[]{:S(2)}) async-start(f32[8,1,4096]{2,1,0:T(1,128)} %reshape.170), calls=%async_computation.2 | async-start | bytes 262144 | tf_op jit(solution)/shard_map/all_to_all | solution.py:48
  151.0 2.0 gather_fusion.3
  153.1 7.0 %fusion = f32[64,64,128]{2,1,0:T(8,128)S(1)} fusion(f32[1,1,64,128,128]{4,3,2,1,0:T(8,128)} %param.9, f32[64,64,128]{2,1,0:T(8,128)} %gather_fusion.3, f32[64,128]{1,0:T(8,128)S(1)} %broadcast_select_fusion, pred[64]{0:T(512)(128)(4,1)S(1)} %compare_and_fusion), kind=kOutput, calls=%fused_computation.4 | convolution fusion | flops 403701760 | bytes 8421440 | tf_op jit(solution)/shard_map/tsb,tab->tsa/dot_general | solution.py:90
  160.1 1.6 fusion.4
  161.7 0.4 reshape.169
  162.1 1.0 copy.19
  163.1 4.8 %all-to-all-start.3 = ((f32[8,64,256]{2,1,0:T(8,128)}), f32[8,64,256]{2,1,0:T(8,128)S(1)}, u32[]{:S(2)}, u32[]{:S(2)}) async-start(f32[8,64,256]{2,1,0:T(8,128)} %copy.19), calls=%async_computation.3 | async-start | bytes 1048576 | tf_op jit(solution)/shard_map/all_to_all | solution.py:94
  167.9 0.5 broadcast.89
  168.4 1.0 reduce
  169.4 0.1 reshape.171
  169.5 0.7 pad_maximum_fusion.aug_ref
  170.2 6.7 %shard_map.102 = (f32[64,128]{1,0:T(8,128)}, f32[64,128]{1,0:T(8,128)}) custom-call(f32[64,128]{1,0:T(8,128)} %pad_maximum_fusion.aug_ref), custom_call_target="tpu_custom_call" | custom-call | tf_op jit(solution)/shard_map/pallas_call | solution.py:33
  176.9 1.0 convolution_multiply_fusion
  177.9 1.0 convolution_subtract_fusion
  178.9 0.2 fusion.30
  179.1 0.2 reshape.172
  179.3 9.3 %all_to_all.36 = f32[8,1,4096]{2,1,0:T(1,128)S(1)} all-to-all(f32[8,1,4096]{2,1,0:T(1,128)S(1)} %reshape.172), channel_id=1, replica_groups=mesh['row_hi'=8,'row_lo'=8,'col'=8] {'col'}, dimensions={0} | all-to-all | bytes 262144 | tf_op jit(solution)/shard_map/all_to_all | solution.py:48
  188.6 1.0 reduce.1
  189.6 0.1 reshape.173
  189.7 0.2 reshape.174
  189.9 12.6 %all_to_all.37 = f32[8,1,4096]{2,1,0:T(1,128)S(1)} all-to-all(f32[8,1,4096]{2,1,0:T(1,128)S(1)} %reshape.174), channel_id=1, replica_groups=mesh['row_hi'=8,'row_lo'=8,'col'=8] {'row_lo'}, dimensions={0} | all-to-all | bytes 262144 | tf_op jit(solution)/shard_map/all_to_all | solution.py:48
  202.5 1.0 reduce.2
  203.6 0.8 reshape.176
  204.5 3.7 %all-to-all-start.6 = ((f32[8,1,4096]{2,1,0:T(1,128)}), f32[8,1,4096]{2,1,0:T(1,128)S(1)}, u32[]{:S(2)}, u32[]{:S(2)}) async-start(f32[8,1,4096]{2,1,0:T(1,128)} %reshape.176), calls=%async_computation.6 | async-start | bytes 262144 | tf_op jit(solution)/shard_map/all_to_all | solution.py:48
  208.1 0.8 fusion.17
  209.0 8.2 %all-to-all-done.6 = f32[8,1,4096]{2,1,0:T(1,128)S(1)} async-done(((f32[8,1,4096]{2,1,0:T(1,128)}), f32[8,1,4096]{2,1,0:T(1,128)S(1)}, u32[]{:S(2)}, u32[]{:S(2)}) %all-to-all-start.6) | async-done | bytes 131104 | tf_op jit(solution)/shard_map/all_to_all | solution.py:48
  217.2 1.0 reduce.3
  218.3 0.7 pad_maximum_fusion.1.aug_ref
  219.0 6.7 %shard_map.103 = (f32[64,128]{1,0:T(8,128)}, f32[64,128]{1,0:T(8,128)}) custom-call(f32[64,128]{1,0:T(8,128)} %pad_maximum_fusion.1.aug_ref), custom_call_target="tpu_custom_call" | custom-call | tf_op jit(solution)/shard_map/pallas_call | solution.py:33
  225.7 1.6 fusion.13
  (38 shorter events, 0.7 us)
Async XLA Ops:
  0.6 3.0 %copy-start = (f32[64,2048]{1,0:T(8,128)S(1)}, f32[64,2048]{1,0:T(8,128)}, u32[]{:S(2)}) copy-start(f32[64,2048]{1,0:T(8,128)} %param.13) | copy-start | bytes 1572868
  81.0 0.8 copy-start.2
  81.0 0.8 copy-start.3
  83.6 9.2 %copy-start.5 = (s32[1,1,64]{2,1,0:T(1,128)S(1)}, s32[1,1,64]{2,1,0:T(1,128)}, u32[]{:S(2)}) copy-start(s32[1,1,64]{2,1,0:T(1,128)} %param.11) | copy-start | bytes 772
  83.6 60.8 %all-to-all-start.1 = ((f32[64,64,128]{2,1,0:T(8,128)}), f32[64,64,128]{2,1,0:T(8,128)S(1)}, u32[]{:S(2)}, u32[]{:S(2)}) async-start(f32[64,64,128]{2,1,0:T(8,128)} %broadcast_in_dim.83), calls=%async_computation.1 | async-start | bytes 4194304 | tf_op jit(solution)/shard_map/all_to_all | solution.py:82
  146.2 16.9 %all-to-all-start.2 = ((f32[8,1,4096]{2,1,0:T(1,128)}), f32[8,1,4096]{2,1,0:T(1,128)S(1)}, u32[]{:S(2)}, u32[]{:S(2)}) async-start(f32[8,1,4096]{2,1,0:T(1,128)} %reshape.170), calls=%async_computation.2 | async-start | bytes 262144 | tf_op jit(solution)/shard_map/all_to_all | solution.py:48
  153.1 7.0 %copy-start.4 = (s32[1,1,64]{2,1,0:T(1,128)S(1)}, s32[1,1,64]{2,1,0:T(1,128)}, u32[]{:S(2)}) copy-start(s32[1,1,64]{2,1,0:T(1,128)} %param.10) | copy-start | bytes 772
  163.1 13.8 %all-to-all-start.3 = ((f32[8,64,256]{2,1,0:T(8,128)}), f32[8,64,256]{2,1,0:T(8,128)S(1)}, u32[]{:S(2)}, u32[]{:S(2)}) async-start(f32[8,64,256]{2,1,0:T(8,128)} %copy.19), calls=%async_computation.3 | async-start | bytes 1048576 | tf_op jit(solution)/shard_map/all_to_all | solution.py:94
  179.3 28.8 %copy-start.1 = (f32[64,128]{1,0:T(8,128)S(1)}, f32[64,128]{1,0:T(8,128)}, u32[]{:S(2)}) copy-start(f32[64,128]{1,0:T(8,128)} %get-tuple-element.9) | copy-start | bytes 98308
  204.5 12.8 %all-to-all-start.6 = ((f32[8,1,4096]{2,1,0:T(1,128)}), f32[8,1,4096]{2,1,0:T(1,128)S(1)}, u32[]{:S(2)}, u32[]{:S(2)}) async-start(f32[8,1,4096]{2,1,0:T(1,128)} %reshape.176), calls=%async_computation.6 | async-start | bytes 262144 | tf_op jit(solution)/shard_map/all_to_all | solution.py:48

commit v13 on v11

--- a/solution.py
+++ b/solution.py
@@ -77,7 +77,7 @@
     partial = (partial * col_scale.reshape(n_row, v_piece // tl, 1, tl)).transpose(0, 2, 1, 3)
     partial = partial.reshape(n_row, width, v_piece)
     received = lax.all_to_all(partial, ROW, 0, 0, tiled=True)
-    pt_piece = received.sum(0) - jnp.dot(lowtri, v_basis, precision=HIGH)
+    pt_piece = received.sum(0) - jnp.dot(lowtri, v_basis, precision=FAST)
     spread = jnp.broadcast_to(pt_piece[None], (n_row, width, v_piece))
     column = lax.all_to_all(spread, ROW, 0, 0, tiled=True)
     gram = gather_sum(jnp.einsum("jsb,jtb->st", column, column, precision=FAST), "col")

time: 229 us -> 229 us (level)
  no operation moved by 1% of the time
where the time goes in v13:
time: 229 us; the launch traced here: 227 us
  blocking collectives  90.6 us (40%)
  waiting for transfers between devices  59 us (26%)
  starting transfers between devices  22.5 us (10%)
  matrix products  19.9 us (9%)
  Pallas kernels  13.3 us (6%)
  local copies, waits for them, and re-layouts  12.3 us (5%)
  other arithmetic  8.74 us (4%)
    all_to_all x1, blocking collectives, per_device(): received = lax.all_to_all(partial, ROW, 0, 0, tiled=True)  68.8 us
    all_to_all x1, waiting for transfers between devices, per_device(): column = lax.all_to_all(spread, ROW, 0, 0, tiled=True)  50.8 us
    all_to_all x2, blocking collectives, gather_sum(): lax.all_to_all(jnp.broadcast_to(x[None], (n,) + x.shape), axis, 0, 0, til...  21.9 us
    pallas_call x2, Pallas kernels, cholesky_and_inverse(): pl.pallas_call(_factor_kernel, out_shape=(jax.ShapeDtypeStruct(aug.shape,...  13.3 us
    all_to_all x1, starting transfers between devices, per_device(): column = lax.all_to_all(spread, ROW, 0, 0, tiled=True)  9.22 us
    all_to_all x2, starting transfers between devices, gather_sum(): lax.all_to_all(jnp.broadcast_to(x[None], (n,) + x.shape), axis, 0, 0, til...  8.51 us
    all_to_all x2, waiting for transfers between devices, gather_sum(): lax.all_to_all(jnp.broadcast_to(x[None], (n,) + x.shape), axis, 0, 0, til...  8.23 us
    dot_general x1, matrix products, per_device(): products = jnp.einsum('tsb,tab->tsa', chosen, local_tiles, precision=FAST)  7.02 us
  transfers between devices with their start and end apart: 4, of which 2 were waited for; matrix products, arithmetic and copies ran while one was open for 7% of the time, Pallas kernels for 3%

profile of v13, /device:TPU:2, one launch (start us, length us, event | category | flops | bytes accessed | tf_op | source)
XLA Modules:
  0.0 227.4 jit_solution(17588095221752861939)
XLA Ops:
  0.6 0.8 select_reduce_fusion
  1.5 0.7 compare_and_fusion.2
  2.1 0.7 fusion.24
  2.8 0.8 exponential_bitcast_fusion
  3.7 0.7 gather_fusion
  4.3 5.4 %fusion.2 = f32[64,64,128]{2,1,0:T(8,128)} fusion(f32[1,1,64,128,128]{4,3,2,1,0:T(8,128)} %param.9, f32[64,64,128]{2,1,0:T(8,128)S(1)} %gather_fusion, pred[64]{0:T(512)(128)(4,1)S(1)} %compare_and_fusion.2), kind=kOutput, calls=%fused_computation.6 | convolution fusion | flops 403177472 | bytes 8388672 | tf_op jit(solution)/shard_map/tsa,tab->tsb/dot_general | solution.py:75
  9.7 2.3 gather_fusion.2
  12.0 0.2 select_multiply_fusion.2
  12.3 68.8 %all_to_all.35 = f32[64,64,128]{2,1,0:T(8,128)S(1)} all-to-all(f32[64,64,128]{2,1,0:T(8,128)S(1)} %select_multiply_fusion.2), channel_id=1, replica_groups=mesh['row_hi'=8,'row_lo'=8,'col'=8] {'row_hi','row_lo'}, dimensions={0} | all-to-all | bytes 4194304 | tf_op jit(solution)/shard_map/all_to_all | solution.py:79
  81.0 0.1 reduce_sum.64
  81.2 0.6 copy-done.2
  81.8 0.1 convolution_subtract_fusion.1
  81.9 1.6 broadcast_in_dim.83
  83.6 9.2 %all-to-all-start.1 = ((f32[64,64,128]{2,1,0:T(8,128)}), f32[64,64,128]{2,1,0:T(8,128)S(1)}, u32[]{:S(2)}, u32[]{:S(2)}) async-start(f32[64,64,128]{2,1,0:T(8,128)} %broadcast_in_dim.83), calls=%async_computation.1 | async-start | bytes 4194304 | tf_op jit(solution)/shard_map/all_to_all | solution.py:82
  92.8 0.6 gather_fusion.1
  93.5 50.8 %all-to-all-done.1 = f32[64,64,128]{2,1,0:T(8,128)S(1)} async-done(((f32[64,64,128]{2,1,0:T(8,128)}), f32[64,64,128]{2,1,0:T(8,128)S(1)}, u32[]{:S(2)}, u32[]{:S(2)}) %all-to-all-start.1) | async-done | bytes 2097184 | tf_op jit(solution)/shard_map/all_to_all | solution.py:82
  144.3 1.0 convolution_bitcast_fusion
  145.3 0.8 reshape.170
  146.2 4.8 %all-to-all-start.2 = ((f32[8,1,4096]{2,1,0:T(1,128)}), f32[8,1,4096]{2,1,0:T(1,128)S(1)}, u32[]{:S(2)}, u32[]{:S(2)}) async-start(f32[8,1,4096]{2,1,0:T(1,128)} %reshape.170), calls=%async_computation.2 | async-start | bytes 262144 | tf_op jit(solution)/shard_map/all_to_all | solution.py:48
  151.0 2.0 gather_fusion.3
  153.1 7.0 %fusion = f32[64,64,128]{2,1,0:T(8,128)S(1)} fusion(f32[1,1,64,128,128]{4,3,2,1,0:T(8,128)} %param.9, f32[64,64,128]{2,1,0:T(8,128)} %gather_fusion.3, f32[64,128]{1,0:T(8,128)S(1)} %broadcast_select_fusion, pred[64]{0:T(512)(128)(4,1)S(1)} %compare_and_fusion), kind=kOutput, calls=%fused_computation.4 | convolution fusion | flops 403701760 | bytes 8421440 | tf_op jit(solution)/shard_map/tsb,tab->tsa/dot_general | solution.py:90
  160.1 1.6 fusion.4
  161.7 0.4 reshape.169
  162.1 1.0 copy.19
  163.1 4.8 %all-to-all-start.3 = ((f32[8,64,256]{2,1,0:T(8,128)}), f32[8,64,256]{2,1,0:T(8,128)S(1)}, u32[]{:S(2)}, u32[]{:S(2)}) async-start(f32[8,64,256]{2,1,0:T(8,128)} %copy.19), calls=%async_computation.3 | async-start | bytes 1048576 | tf_op jit(solution)/shard_map/all_to_all | solution.py:94
  167.9 0.5 broadcast.89
  168.4 1.0 reduce
  169.4 0.1 reshape.171
  169.5 0.7 pad_maximum_fusion.aug_ref
  170.2 6.7 %shard_map.102 = (f32[64,128]{1,0:T(8,128)}, f32[64,128]{1,0:T(8,128)}) custom-call(f32[64,128]{1,0:T(8,128)} %pad_maximum_fusion.aug_ref), custom_call_target="tpu_custom_call" | custom-call | tf_op jit(solution)/shard_map/pallas_call | solution.py:33
  176.9 1.0 convolution_multiply_fusion
  177.9 1.0 convolution_subtract_fusion
  179.0 0.2 fusion.30
  179.2 0.2 reshape.172
  179.4 9.3 %all_to_all.36 = f32[8,1,4096]{2,1,0:T(1,128)S(1)} all-to-all(f32[8,1,4096]{2,1,0:T(1,128)S(1)} %reshape.172), channel_id=1, replica_groups=mesh['row_hi'=8,'row_lo'=8,'col'=8] {'col'}, dimensions={0} | all-to-all | bytes 262144 | tf_op jit(solution)/shard_map/all_to_all | solution.py:48
  188.7 1.0 reduce.1
  189.8 0.2 reshape.174
  190.0 12.6 %all_to_all.37 = f32[8,1,4096]{2,1,0:T(1,128)S(1)} all-to-all(f32[8,1,4096]{2,1,0:T(1,128)S(1)} %reshape.174), channel_id=1, replica_groups=mesh['row_hi'=8,'row_lo'=8,'col'=8] {'row_lo'}, dimensions={0} | all-to-all | bytes 262144 | tf_op jit(solution)/shard_map/all_to_all | solution.py:48
  202.6 1.0 reduce.2
  203.5 0.1 reshape.175
  203.7 0.8 reshape.176
  204.5 3.7 %all-to-all-start.6 = ((f32[8,1,4096]{2,1,0:T(1,128)}), f32[8,1,4096]{2,1,0:T(1,128)S(1)}, u32[]{:S(2)}, u32[]{:S(2)}) async-start(f32[8,1,4096]{2,1,0:T(1,128)} %reshape.176), calls=%async_computation.6 | async-start | bytes 262144 | tf_op jit(solution)/shard_map/all_to_all | solution.py:48
  208.2 0.8 fusion.17
  209.0 8.2 %all-to-all-done.6 = f32[8,1,4096]{2,1,0:T(1,128)S(1)} async-done(((f32[8,1,4096]{2,1,0:T(1,128)}), f32[8,1,4096]{2,1,0:T(1,128)S(1)}, u32[]{:S(2)}, u32[]{:S(2)}) %all-to-all-start.6) | async-done | bytes 131104 | tf_op jit(solution)/shard_map/all_to_all | solution.py:48
  217.3 1.0 reduce.3
  218.4 0.7 pad_maximum_fusion.1.aug_ref
  219.1 6.7 %shard_map.103 = (f32[64,128]{1,0:T(8,128)}, f32[64,128]{1,0:T(8,128)}) custom-call(f32[64,128]{1,0:T(8,128)} %pad_maximum_fusion.1.aug_ref), custom_call_target="tpu_custom_call" | custom-call | tf_op jit(solution)/shard_map/pallas_call | solution.py:33
  225.7 1.6 fusion.13
  (38 shorter events, 0.7 us)
Async XLA Ops:
  0.6 3.0 %copy-start = (f32[64,2048]{1,0:T(8,128)S(1)}, f32[64,2048]{1,0:T(8,128)}, u32[]{:S(2)}) copy-start(f32[64,2048]{1,0:T(8,128)} %param.13) | copy-start | bytes 1572868
  81.0 0.8 copy-start.2
  81.0 0.8 copy-start.3
  83.6 9.2 %copy-start.5 = (s32[1,1,64]{2,1,0:T(1,128)S(1)}, s32[1,1,64]{2,1,0:T(1,128)}, u32[]{:S(2)}) copy-start(s32[1,1,64]{2,1,0:T(1,128)} %param.11) | copy-start | bytes 772
  83.6 60.8 %all-to-all-start.1 = ((f32[64,64,128]{2,1,0:T(8,128)}), f32[64,64,128]{2,1,0:T(8,128)S(1)}, u32[]{:S(2)}, u32[]{:S(2)}) async-start(f32[64,64,128]{2,1,0:T(8,128)} %broadcast_in_dim.83), calls=%async_computation.1 | async-start | bytes 4194304 | tf_op jit(solution)/shard_map/all_to_all | solution.py:82
  146.2 16.9 %all-to-all-start.2 = ((f32[8,1,4096]{2,1,0:T(1,128)}), f32[8,1,4096]{2,1,0:T(1,128)S(1)}, u32[]{:S(2)}, u32[]{:S(2)}) async-start(f32[8,1,4096]{2,1,0:T(1,128)} %reshape.170), calls=%async_computation.2 | async-start | bytes 262144 | tf_op jit(solution)/shard_map/all_to_all | solution.py:48
  153.0 7.0 %copy-start.4 = (s32[1,1,64]{2,1,0:T(1,128)S(1)}, s32[1,1,64]{2,1,0:T(1,128)}, u32[]{:S(2)}) copy-start(s32[1,1,64]{2,1,0:T(1,128)} %param.10) | copy-start | bytes 772
  163.1 13.8 %all-to-all-start.3 = ((f32[8,64,256]{2,1,0:T(8,128)}), f32[8,64,256]{2,1,0:T(8,128)S(1)}, u32[]{:S(2)}, u32[]{:S(2)}) async-start(f32[8,64,256]{2,1,0:T(8,128)} %copy.19), calls=%async_computation.3 | async-start | bytes 1048576 | tf_op jit(solution)/shard_map/all_to_all | solution.py:94
  179.4 28.8 %copy-start.1 = (f32[64,128]{1,0:T(8,128)S(1)}, f32[64,128]{1,0:T(8,128)}, u32[]{:S(2)}) copy-start(f32[64,128]{1,0:T(8,128)} %get-tuple-element.9) | copy-start | bytes 98308
  204.5 12.8 %all-to-all-start.6 = ((f32[8,1,4096]{2,1,0:T(1,128)}), f32[8,1,4096]{2,1,0:T(1,128)S(1)}, u32[]{:S(2)}, u32[]{:S(2)}) async-start(f32[8,1,4096]{2,1,0:T(1,128)} %reshape.176), calls=%async_computation.6 | async-start | bytes 262144 | tf_op jit(solution)/shard_map/all_to_all | solution.py:48
